TPU v7x, 256 devices: a whole 4x4x8 slice. The times are simulated.
256 devices in a mesh: row: 16 (over x, y), col: 16 (over z, core).
Axes of the slice: x: 4, y: 4, z: 8, core: 2. Of those that a mesh axis runs over, the one named last changes fastest.
Arguments:
- rhs: float32 [4, 16, 16, 128, 256], P(None, 'row', 'col'), may hold values from -6 to 6
- diag_inverse: float32 [4, 16, 16, 128, 128], P(None, 'row', 'col'), as said below
- update_blocks: float32 [3, 16, 16, 48, 128, 128], P(None, 'row', 'col'), may hold values from -0.15625 to 0.15625
- source_slot: int32 [3, 16, 16, 48], P(None, 'row', 'col'), may hold values from 0 to 15
- target_slot: int32 [3, 16, 16, 48], P(None, 'row', 'col'), may hold values from 0 to 15
- block_count: int32 [3, 16, 16], P(None, 'row', 'col'), may hold values from 1 to 48, as said below
Outputs:
- forward_solution: float32 [4, 16, 16, 128, 256], P(None, 'row', 'col')
- solution: float32 [4, 16, 16, 128, 256], P(None, 'row', 'col')
Inputs may be any that keep to these rules, and one draw needn't show every extreme that they name: Each diag_inverse block is lower triangular with diagonal entries between 0.5 and 1.6. `block_count`: at every level some device uses all 48 slots.
All inputs are finite; a program needn't handle non-finite values.
Results may differ from a plain program's by a relative error of at most 0.0003.
Values sent between devices are 32-bit elements; how exact they have to be, the bound alone decides.
No kernel may reach another device: no remote copies, remote signals or barrier semaphores. Data moves between devices by JAX's collectives and lax.ppermute only.
A program may use at most 128 MiB of HBM per device.

v0:
```python
import math

import jax
import jax.numpy as jnp
from jax import lax
from jax.sharding import PartitionSpec as P


def apply_inverse(inverse, values):
    return jnp.einsum("...st,...tn->...sn", inverse, values, precision=lax.Precision.HIGHEST)


def apply_transposed(inverse, values):
    return jnp.einsum("...ts,...tn->...sn", inverse, values, precision=lax.Precision.HIGHEST)


def block_terms(tile_stack, picked, placed, filled, operand, totals, transposed):
    slot_count = tile_stack.shape[0]
    group_size = math.gcd(slot_count, 8)
    rounds = (filled + group_size - 1) // group_size

    def advance(number, running):
        offset = number * group_size
        tile_group = lax.dynamic_slice_in_dim(tile_stack, offset, group_size, 0)
        chosen_rows = lax.dynamic_slice_in_dim(picked, offset, group_size, 0)
        target_rows = lax.dynamic_slice_in_dim(placed, offset, group_size, 0)
        active = (offset + jnp.arange(group_size, dtype=jnp.int32) < filled).astype(jnp.float32)
        selected = operand[chosen_rows]
        if transposed:
            products = jnp.einsum(
                "gts,gtn->gsn", tile_group, selected, precision=lax.Precision.HIGHEST
            )
        else:
            products = jnp.einsum(
                "gst,gtn->gsn", tile_group, selected, precision=lax.Precision.HIGHEST
            )
        return running.at[target_rows].add(products * active[:, None, None])

    return lax.fori_loop(0, rounds, advance, totals)


def per_device(rhs, diag_inverse, update_blocks, source_slot, target_slot, block_count):
    levels = rhs.shape[0]
    last_level = levels - 1
    rhs_local = rhs[:, 0, 0]
    inverse_local = diag_inverse[:, 0, 0]
    tiles_local = update_blocks[:, 0, 0]
    sources_local = source_slot[:, 0, 0]
    targets_local = target_slot[:, 0, 0]
    filled_local = block_count[:, 0, 0]
    row_count = lax.axis_size("row")
    col_count = lax.axis_size("col")
    block_shape = rhs_local.shape[1:]
    forward = [apply_inverse(inverse_local[0], rhs_local[0])]
    for level_index in range(1, levels):
        forward_gathered = lax.all_gather(forward[-1][None], "row", axis=0, tiled=True)
        forward_zero_terms = jnp.zeros((col_count,) + block_shape, jnp.float32)
        owner_reduced = lax.psum_scatter(
            block_terms(
                tiles_local[level_index - 1],
                sources_local[level_index - 1],
                targets_local[level_index - 1],
                filled_local[level_index - 1],
                forward_gathered,
                forward_zero_terms,
                False,
            ),
            "col",
            scatter_dimension=0,
            tiled=True,
        )
        forward.append(
            apply_inverse(inverse_local[level_index], rhs_local[level_index] - owner_reduced[0])
        )
    backward = [apply_transposed(inverse_local[last_level], forward[-1])]
    for level_index in range(last_level - 1, -1, -1):
        gathered = lax.all_gather(backward[0][None], "col", axis=0, tiled=True)
        solved = forward[level_index]
        zero_terms = jnp.zeros((row_count,) + block_shape, jnp.float32)
        totals = block_terms(
            tiles_local[level_index],
            targets_local[level_index],
            sources_local[level_index],
            filled_local[level_index],
            gathered,
            zero_terms,
            True,
        )
        reduced = lax.psum_scatter(totals, "row", scatter_dimension=0, tiled=True)
        backward.insert(0, apply_transposed(inverse_local[level_index], solved - reduced[0]))
    forward_out = jnp.stack(forward)[:, None, None]
    backward_out = jnp.stack(backward)[:, None, None]
    return (forward_out, backward_out)


def solution(mesh):
    in_specs = (
        P(None, "row", "col", None, None),
        P(None, "row", "col", None, None),
        P(None, "row", "col", None, None, None),
        P(None, "row", "col", None),
        P(None, "row", "col", None),
        P(None, "row", "col"),
    )
    out_specs = (P(None, "row", "col", None, None), P(None, "row", "col", None, None))
    return jax.shard_map(
        per_device, mesh=mesh, in_specs=in_specs, out_specs=out_specs, check_vma=False
    )
```

profile of v0, /device:TPU:8, one launch (start us, length us, event | category | flops | bytes accessed | tf_op | source)
XLA Modules:
  0.0 1020.0 jit_solution(9488122937329640545)
XLA Ops:
  7.2 1.9 fusion.20
  11.2 7.6 fusion.45
  18.8 2.3 copy.44
  21.1 42.4 %all-gather.13.cloned.1.call-done = f32[2048,256]{1,0:T(8,128)} async-done(((f32[128,256]{1,0:T(8,128)}), f32[2048,256]{1,0:T(8,128)}) %all-gather.13.cloned.1.call-update) | async-done | bytes 2097168 | tf_op jit(solution)/shard_map/all_gather | solution.py:56
  65.0 24.9 %while.60 = (s32[]{:T(128)}, f32[16,128,256]{2,1,0:T(8,128)}, s32[]{:T(128)}, s32[48]{0:T(128)S(1)}, f32[48,128,128]{1,2,0:T(8,128)}, /*index=5*/s32[48]{0:T(128...) while((s32[]{:T(128)}, f32[16,128,256]{2,1,0:T(8,128)}, ...), condition=%wide.region_2.3_spmd, body=%wide.region_0.2_spmd.sunk | while | flops 403178560 | bytes 7868883 | solution.py:39
  65.1 2.2 gather_fusion
  67.9 2.1 convolution_multiply_fusion.12
  70.1 3.3 scatter_fusion
  73.4 2.2 gather_fusion
  76.3 2.1 convolution_multiply_fusion.12
  78.4 3.2 scatter_fusion
  81.7 2.2 gather_fusion
  84.6 2.1 convolution_multiply_fusion.12
  86.7 3.2 scatter_fusion
  90.0 81.3 %reduce-scatter.13.cloned.1.call-done = f32[1,128,256]{2,1,0:T(8,128)} async-done(((f32[16,128,256]{2,1,0:T(8,128)}), f32[1,128,256]{2,1,0:T(8,128)}) %reduce-scatter.13.cloned.1.call-update) | async-done | bytes 131088 | tf_op jit(solution)/shard_map/reduce_scatter | solution.py:58
  171.3 1.8 fusion.18
  173.8 3.6 copy.45
  177.4 45.1 %all-gather.15.cloned.1.call-done = f32[2048,256]{1,0:T(8,128)} async-done(((f32[128,256]{1,0:T(8,128)}), f32[2048,256]{1,0:T(8,128)}) %all-gather.15.cloned.1.call-update) | async-done | bytes 2097168 | tf_op jit(solution)/shard_map/all_gather | solution.py:56
  222.5 1.5 broadcast.90.clone.1
  224.0 8.4 while.61
  224.1 2.2 gather_fusion.1
  226.9 2.1 convolution_multiply_fusion.13
  229.0 3.3 scatter_fusion.1
  232.4 100.5 %reduce-scatter.15.cloned.1.call-done = f32[1,128,256]{2,1,0:T(8,128)} async-done(((f32[16,128,256]{2,1,0:T(8,128)}), f32[1,128,256]{2,1,0:T(8,128)}) %reduce-scatter.15.cloned.1.call-update) | async-done | bytes 131088 | tf_op jit(solution)/shard_map/reduce_scatter | solution.py:58
  332.9 1.8 fusion.16
  335.4 3.6 copy.46
  339.0 44.2 %all-gather.17.cloned.1.call-done = f32[2048,256]{1,0:T(8,128)} async-done(((f32[128,256]{1,0:T(8,128)}), f32[2048,256]{1,0:T(8,128)}) %all-gather.17.cloned.1.call-update) | async-done | bytes 2097168 | tf_op jit(solution)/shard_map/all_gather | solution.py:56
  383.2 1.6 broadcast.90.clone
  384.8 8.4 while.62
  384.8 2.2 gather_fusion.2
  387.6 2.1 convolution_multiply_fusion.14
  389.8 3.4 scatter_fusion.2
  393.2 97.3 %reduce-scatter.17.cloned.1.call-done = f32[1,128,256]{2,1,0:T(8,128)} async-done(((f32[16,128,256]{2,1,0:T(8,128)}), f32[1,128,256]{2,1,0:T(8,128)}) %reduce-scatter.17.cloned.1.call-update) | async-done | bytes 131088 | tf_op jit(solution)/shard_map/reduce_scatter | solution.py:58
  492.8 39.3 %all-gather.19.cloned.1.call-done = f32[2048,256]{0,1:T(8,128)} async-done(((f32[128,256]{0,1:T(8,128)}), f32[2048,256]{0,1:T(8,128)}) %all-gather.19.cloned.1.call-update) | async-done | bytes 2097168 | tf_op jit(solution)/shard_map/all_gather | solution.py:77
  532.1 3.0 copy.38
  536.6 8.3 while.63
  536.7 2.2 gather_fusion.3
  539.4 2.1 convolution_multiply_fusion.15
  541.5 3.3 scatter_fusion.3
  544.9 117.6 %reduce-scatter.19.cloned.1.call-done = f32[1,128,256]{2,1,0:T(8,128)} async-done(((f32[16,128,256]{2,1,0:T(8,128)}), f32[1,128,256]{2,1,0:T(8,128)}) %reduce-scatter.19.cloned.1.call-update) | async-done | bytes 131088
  662.5 1.9 fusion.13
  664.5 40.4 %all-gather.21.cloned.1.call-done = f32[2048,256]{0,1:T(8,128)} async-done(((f32[128,256]{0,1:T(8,128)}), f32[2048,256]{0,1:T(8,128)}) %all-gather.21.cloned.1.call-update) | async-done | bytes 2097168 | tf_op jit(solution)/shard_map/all_gather | solution.py:77
  704.9 3.0 copy.39
  707.9 1.6 broadcast.90.clone.4
  709.5 8.2 while.64
  709.6 2.2 gather_fusion.4
  712.4 2.1 convolution_multiply_fusion.16
  714.5 3.2 scatter_fusion.4
  717.8 119.2 %reduce-scatter.21.cloned.1.call-done = f32[1,128,256]{2,1,0:T(8,128)} async-done(((f32[16,128,256]{2,1,0:T(8,128)}), f32[1,128,256]{2,1,0:T(8,128)}) %reduce-scatter.21.cloned.1.call-update) | async-done | bytes 131088
  837.0 1.9 fusion.12
  839.0 40.4 %all-gather.23.cloned.1.call-done = f32[2048,256]{0,1:T(8,128)} async-done(((f32[128,256]{0,1:T(8,128)}), f32[2048,256]{0,1:T(8,128)}) %all-gather.23.cloned.1.call-update) | async-done | bytes 2097168 | tf_op jit(solution)/shard_map/all_gather | solution.py:77
  879.4 2.9 copy.40
  882.3 1.6 broadcast.90
  883.9 24.7 %while.65 = (s32[]{:T(128)}, f32[16,128,256]{2,1,0:T(8,128)}, s32[]{:T(128)}, s32[48]{0:T(128)S(1)}, f32[48,128,128]{1,2,0:T(8,128)}, /*index=5*/s32[48]{0:T(128...) while((s32[]{:T(128)}, f32[16,128,256]{2,1,0:T(8,128)}, ...), condition=%wide.region_22.23_spmd, body=%wide.region_20.22_spmd.sunk | while | flops 403178560 | bytes 7868883 | solution.py:39
  884.0 2.2 gather_fusion.5
  886.8 2.1 convolution_multiply_fusion.17
  888.9 3.2 scatter_fusion.5
  892.2 2.2 gather_fusion.5
  895.1 2.1 convolution_multiply_fusion.17
  897.2 3.3 scatter_fusion.5
  900.5 2.2 gather_fusion.5
  903.4 2.1 convolution_multiply_fusion.17
  905.4 3.2 scatter_fusion.5
  910.4 100.4 %reduce-scatter.23.cloned.1.call-done = f32[1,128,256]{2,1,0:T(8,128)} async-done(((f32[16,128,256]{2,1,0:T(8,128)}), f32[1,128,256]{2,1,0:T(8,128)}) %reduce-scatter.23.cloned.1.call-update) | async-done | bytes 131088
  (85 shorter events, 18.4 us)
Async XLA Ops:
  7.2 56.3 %all-gather.13.cloned.1.call-start = ((), (), s32[]{:S(2)}) async-start(), calls=%async_computation.9 | async-start | bytes 2228224 | tf_op jit(solution)/shard_map/all_gather | solution.py:56
  9.1 162.2 %reduce-scatter.13.cloned.1.call-start = ((), (), s32[]{:S(2)}) async-start(), calls=%async_computation.6 | async-start | bytes 2228224 | tf_op jit(solution)/shard_map/reduce_scatter | solution.py:58
  18.8 2.3 copy-start.8
  18.8 2.3 copy-start.9
  89.9 81.4 %copy-start.6 = (f32[4,1,1,128,128]{4,3,2,1,0:T(8,128)S(1)}, f32[4,1,1,128,128]{4,3,2,1,0:T(8,128)}, u32[]{:S(2)}) copy-start(f32[4,1,1,128,128]{4,3,2,1,0:T(8,128)} %param.19) | copy-start | bytes 786436
  89.9 81.4 %copy-start.7 = (f32[4,1,1,128,256]{4,3,2,1,0:T(8,128)S(1)}, f32[4,1,1,128,256]{4,3,2,1,0:T(8,128)}, u32[]{:S(2)}) copy-start(f32[4,1,1,128,256]{4,3,2,1,0:T(8,128)} %param.18) | copy-start | bytes 1572868
  89.9 132.5 %all-gather.15.cloned.1.call-start = ((), (), s32[]{:S(2)}) async-start(), calls=%async_computation.10 | async-start | bytes 2228224 | tf_op jit(solution)/shard_map/all_gather | solution.py:56
  173.2 159.8 %reduce-scatter.15.cloned.1.call-start = ((), (), s32[]{:S(2)}) async-start(), calls=%async_computation.7 | async-start | bytes 2228224 | tf_op jit(solution)/shard_map/reduce_scatter | solution.py:58
  232.4 150.8 %all-gather.17.cloned.1.call-start = ((), (), s32[]{:S(2)}) async-start(), calls=%async_computation.11 | async-start | bytes 2228224 | tf_op jit(solution)/shard_map/all_gather | solution.py:56
  334.8 155.7 %reduce-scatter.17.cloned.1.call-start = ((), (), s32[]{:S(2)}) async-start(), calls=%async_computation.8 | async-start | bytes 2228224 | tf_op jit(solution)/shard_map/reduce_scatter | solution.py:58
  393.1 138.9 %all-gather.19.cloned.1.call-start = ((), (), s32[]{:S(2)}) async-start(), calls=%async_computation.12 | async-start | bytes 2228224 | tf_op jit(solution)/shard_map/all_gather | solution.py:77
  492.7 169.7 %reduce-scatter.19.cloned.1.call-start = ((), (), s32[]{:S(2)}) async-start(), calls=%async_computation.15 | async-start | bytes 2228224
  544.8 117.6 %copy-start.1 = (f32[256,128]{0,1:T(8,128)S(1)}, f32[256,128]{0,1:T(8,128)}, u32[]{:S(2)}) copy-start(f32[256,128]{0,1:T(8,128)} %fusion.16) | copy-start | bytes 393220
  544.9 160.1 %all-gather.21.cloned.1.call-start = ((), (), s32[]{:S(2)}) async-start(), calls=%async_computation.13 | async-start | bytes 2228224 | tf_op jit(solution)/shard_map/all_gather | solution.py:77
  664.4 172.5 %reduce-scatter.21.cloned.1.call-start = ((), (), s32[]{:S(2)}) async-start(), calls=%async_computation.16 | async-start | bytes 2228224
  717.7 119.3 %copy-start = (f32[256,128]{0,1:T(8,128)S(1)}, f32[256,128]{0,1:T(8,128)}, u32[]{:S(2)}) copy-start(f32[256,128]{0,1:T(8,128)} %fusion.18) | copy-start | bytes 393220
  717.7 161.7 %all-gather.23.cloned.1.call-start = ((), (), s32[]{:S(2)}) async-start(), calls=%async_computation.14 | async-start | bytes 2228224 | tf_op jit(solution)/shard_map/all_gather | solution.py:77
  838.9 171.8 %reduce-scatter.23.cloned.1.call-start = ((), (), s32[]{:S(2)}) async-start(), calls=%async_computation.17 | async-start | bytes 2228224
  908.6 0.9 copy-start.2
  908.6 103.4 %copy-start.3 = (f32[256,128]{1,0:T(8,128)S(1)}, f32[256,128]{1,0:T(8,128)}, u32[]{:S(2)}) copy-start(f32[256,128]{1,0:T(8,128)} %fusion.13) | copy-start | bytes 393220
  908.7 103.4 %copy-start.4 = (f32[256,128]{1,0:T(8,128)S(1)}, f32[256,128]{1,0:T(8,128)}, u32[]{:S(2)}) copy-start(f32[256,128]{1,0:T(8,128)} %fusion.12) | copy-start | bytes 393220
  908.7 103.4 %copy-start.5 = (f32[256,128]{1,0:T(8,128)S(1)}, f32[256,128]{1,0:T(8,128)}, u32[]{:S(2)}) copy-start(f32[256,128]{1,0:T(8,128)} %fusion.26) | copy-start | bytes 393220
Sparse Core Ops, SparseCore 0:
  11.0 52.4 all-gather.12
  90.1 81.1 reduce-scatter.12
  174.3 48.0 all-gather.14
  232.5 100.3 reduce-scatter.14
  335.2 47.9 all-gather.16
  393.3 97.1 reduce-scatter.16
  492.9 39.1 all-gather.18
  545.0 117.4 reduce-scatter.18
  664.5 40.3 all-gather.20
  717.8 119.0 reduce-scatter.20
  839.0 40.3 all-gather.22
  908.8 101.8 reduce-scatter.22
where the time goes:
time: 1020 us
  waiting for transfers between devices  868 us (85%)
  local copies, waits for them, and re-layouts  60.6 us (6%)
  other arithmetic  40.5 us (4%)
  matrix products  33.9 us (3%)
  between operations  16.1 us (2%)
    unnamed x15, waiting for transfers between devices  337 us
    reduce_scatter x3, waiting for transfers between devices, per_device(): lax.psum_scatter(block_terms(tiles_local[level_index - 1], sources_local[...  279 us
    all_gather x3, waiting for transfers between devices, per_device(): lax.all_gather(forward[-1][None], 'row', axis=0, tiled=True)  132 us
    all_gather x3, waiting for transfers between devices, per_device(): gathered = lax.all_gather(backward[0][None], 'col', axis=0, tiled=True)  120 us
    scatter-add x10, other arithmetic, advance(): return running.at[target_rows].add(products * active[:, None, None])  32.6 us
    gather x10, local copies, waits for them, and re-layouts, advance(): selected = operand[chosen_rows]  22 us
  transfers between devices with their start and end apart: 12, of which 12 were waited for; matrix products, arithmetic and copies ran while one was open for 2% of the time, Pallas kernels for 0%

commit v1 on v0

v1 whole, which is shorter than its diff:
```python
import functools
import math

import jax
import jax.numpy as jnp
from jax import lax
from jax.experimental import pallas as pl
from jax.experimental.pallas import tpu as pltpu
from jax.sharding import PartitionSpec as P

GROUP = 8


def apply_inverse(inverse, values):
    return jnp.einsum("...st,...tn->...sn", inverse, values, precision=lax.Precision.HIGHEST)


def apply_transposed(inverse, values):
    return jnp.einsum("...ts,...tn->...sn", inverse, values, precision=lax.Precision.HIGHEST)


def _terms_kernel(transposed, group, picked_ref, placed_ref, filled_ref, tiles_ref, operand_ref, out_ref):
    step = pl.program_id(0)

    @pl.when(step == 0)
    def _():
        out_ref[...] = jnp.zeros_like(out_ref)

    filled = filled_ref[0]
    for g in range(group):
        b = step * group + g

        @pl.when(b < filled)
        def _():
            source = picked_ref[b]
            target = placed_ref[b]
            tile = tiles_ref[g]
            values = operand_ref[source]
            if transposed:
                product = lax.dot_general(tile, values, (((0,), (0,)), ((), ())),
                                          precision=lax.Precision.HIGHEST, preferred_element_type=jnp.float32)
            else:
                product = jnp.dot(tile, values, precision=lax.Precision.HIGHEST, preferred_element_type=jnp.float32)
            out_ref[target] += product


def block_terms_kernel(tile_stack, picked, placed, filled, operand, count, transposed):
    slot_count, s, _ = tile_stack.shape
    n_src, _, width = operand.shape
    group = math.gcd(slot_count, GROUP)
    steps = slot_count // group

    def tile_map(j, picked_ref, placed_ref, filled_ref):
        last = jnp.maximum(filled_ref[0] - 1, 0) // group
        return (jnp.minimum(j, last), 0, 0)

    grid_spec = pltpu.PrefetchScalarGridSpec(
        num_scalar_prefetch=3,
        grid=(steps,),
        in_specs=[
            pl.BlockSpec((group, s, s), tile_map),
            pl.BlockSpec((n_src, s, width), lambda j, *_: (0, 0, 0)),
        ],
        out_specs=pl.BlockSpec((count, s, width), lambda j, *_: (0, 0, 0)),
    )
    flops = 2 * slot_count * s * s * width
    return pl.pallas_call(
        functools.partial(_terms_kernel, transposed, group),
        grid_spec=grid_spec,
        out_shape=jax.ShapeDtypeStruct((count, s, width), jnp.float32),
        compiler_params=pltpu.CompilerParams(dimension_semantics=("arbitrary",)),
        cost_estimate=pl.CostEstimate(flops=flops, bytes_accessed=4 * (slot_count * s * s + 2 * n_src * s * width), transcendentals=0),
    )(jnp.clip(picked, 0, n_src - 1), jnp.clip(placed, 0, count - 1), jnp.reshape(filled, (1,)), tile_stack, operand)


def block_terms(tile_stack, picked, placed, filled, operand, totals, transposed):
    return block_terms_kernel(tile_stack, picked, placed, filled, operand, totals.shape[0], transposed)


def gather_blocks(block, axis, count):
    stacked = jnp.broadcast_to(block[None], (count,) + block.shape)
    return lax.all_to_all(stacked, axis, 0, 0, tiled=True)


def scatter_sum(parts, axis):
    return lax.all_to_all(parts, axis, 0, 0, tiled=True).sum(axis=0)


def per_device(rhs, diag_inverse, update_blocks, source_slot, target_slot, block_count):
    levels = rhs.shape[0]
    last_level = levels - 1
    rhs_local = rhs[:, 0, 0]
    inverse_local = diag_inverse[:, 0, 0]
    tiles_local = update_blocks[:, 0, 0]
    sources_local = source_slot[:, 0, 0]
    targets_local = target_slot[:, 0, 0]
    filled_local = block_count[:, 0, 0]
    row_count = lax.axis_size("row")
    col_count = lax.axis_size("col")
    block_shape = rhs_local.shape[1:]
    forward = [apply_inverse(inverse_local[0], rhs_local[0])]
    for level_index in range(1, levels):
        forward_gathered = gather_blocks(forward[-1], "row", row_count)
        forward_zero_terms = jnp.zeros((col_count,) + block_shape, jnp.float32)
        owner_reduced = scatter_sum(
            block_terms(
                tiles_local[level_index - 1],
                sources_local[level_index - 1],
                targets_local[level_index - 1],
                filled_local[level_index - 1],
                forward_gathered,
                forward_zero_terms,
                False,
            ),
            "col",
        )
        forward.append(
            apply_inverse(inverse_local[level_index], rhs_local[level_index] - owner_reduced)
        )
    backward = [apply_transposed(inverse_local[last_level], forward[-1])]
    for level_index in range(last_level - 1, -1, -1):
        gathered = gather_blocks(backward[0], "col", col_count)
        solved = forward[level_index]
        zero_terms = jnp.zeros((row_count,) + block_shape, jnp.float32)
        totals = block_terms(
            tiles_local[level_index],
            targets_local[level_index],
            sources_local[level_index],
            filled_local[level_index],
            gathered,
            zero_terms,
            True,
        )
        reduced = scatter_sum(totals, "row")
        backward.insert(0, apply_transposed(inverse_local[level_index], solved - reduced))
    forward_out = jnp.stack(forward)[:, None, None]
    backward_out = jnp.stack(backward)[:, None, None]
    return (forward_out, backward_out)


def solution(mesh):
    in_specs = (
        P(None, "row", "col", None, None),
        P(None, "row", "col", None, None),
        P(None, "row", "col", None, None, None),
        P(None, "row", "col", None),
        P(None, "row", "col", None),
        P(None, "row", "col"),
    )
    out_specs = (P(None, "row", "col", None, None), P(None, "row", "col", None, None))
    return jax.shard_map(
        per_device, mesh=mesh, in_specs=in_specs, out_specs=out_specs, check_vma=False
    )
```

time: 1020 us -> 631 us (0.62)
  waiting for transfers between devices: 868 us -> 44.8 us
  blocking collectives: 0 us -> 493 us
  Pallas kernels: 0 us -> 49.9 us
  local copies, waits for them, and re-layouts: 60.6 us -> 14.5 us
  other arithmetic: 40.5 us -> 2.25 us
  matrix products: 33.9 us -> 4.47 us
  starting transfers between devices: 0.5 us -> 15.8 us
  between operations: 16.1 us -> 0.8 us
    all_to_all x0 -> x10, blocking collectives: none -> 493 us  [the longest x5 256 us: scatter_sum(): return lax.all_to_all(parts, axis, 0, 0, tiled=True).sum(axis=0)]
    unnamed x15 -> x0, waiting for transfers between devices: 337 us -> none
    reduce_scatter x3 -> x0, waiting for transfers between devices: 279 us -> none  [per_device(): lax.psum_scatter(block_terms(tiles_local[level_index - 1], sources_local[...]
    all_gather x6 -> x0, waiting for transfers between devices: 252 us -> none  [the longest x3 132 us: per_device(): lax.all_gather(forward[-1][None], 'row', axis=0, tiled=True)]
    pallas_call x0 -> x6, Pallas kernels: none -> 49.9 us  [block_terms_kernel(): pl.pallas_call(functools.partial(_terms_kernel, transposed, group), grid_...]
    all_to_all x0 -> x2, waiting for transfers between devices: none -> 44.8 us  [the longest x1 24.7 us: scatter_sum(): return lax.all_to_all(parts, axis, 0, 0, tiled=True).sum(axis=0)]
    scatter-add x10 -> x0, other arithmetic: 32.6 us -> none  [advance(): return running.at[target_rows].add(products * active[:, None, None])]
    gather x10 -> x0, local copies, waits for them, and re-layouts: 22 us -> none  [advance(): selected = operand[chosen_rows]]
  transfers between devices with their start and end apart: 12 -> 2, of which waited for: 12 -> 2; matrix products, arithmetic and copies ran while one was open for 2% -> 2% of each run, Pallas kernels for 0% -> 0%
where the time goes in v1:
time: 631 us; the launch traced here: 625 us
  blocking collectives  493 us (78%)
  Pallas kernels  49.9 us (8%)
  waiting for transfers between devices  44.8 us (7%)
  starting transfers between devices  15.8 us (3%)
  local copies, waits for them, and re-layouts  14.5 us (2%)
    all_to_all x5, blocking collectives, scatter_sum(): return lax.all_to_all(parts, axis, 0, 0, tiled=True).sum(axis=0)  256 us
    all_to_all x5, blocking collectives, gather_blocks(): return lax.all_to_all(stacked, axis, 0, 0, tiled=True)  236 us
    pallas_call x6, Pallas kernels, block_terms_kernel(): pl.pallas_call(functools.partial(_terms_kernel, transposed, group), grid_...  49.9 us
    all_to_all x1, waiting for transfers between devices, scatter_sum(): return lax.all_to_all(parts, axis, 0, 0, tiled=True).sum(axis=0)  24.7 us
    all_to_all x1, waiting for transfers between devices, gather_blocks(): return lax.all_to_all(stacked, axis, 0, 0, tiled=True)  20.1 us
  transfers between devices with their start and end apart: 2, of which 2 were waited for; matrix products, arithmetic and copies ran while one was open for 2% of the time, Pallas kernels for 0%

profile of v1, /device:TPU:8, one launch (start us, length us, event | category | flops | bytes accessed | tf_op | source)
XLA Modules:
  0.0 625.1 jit_solution(10703115750600487905)
XLA Ops:
  0.6 1.2 fusion.6
  1.8 1.5 broadcast_in_dim.22
  3.4 0.0 copy-start.3
  3.4 0.0 copy-start.4
  3.4 0.0 copy-start.5
  3.4 7.5 %all-to-all-start = ((f32[16,128,256]{2,1,0:T(8,128)}), f32[16,128,256]{2,1,0:T(8,128)S(1)}, u32[]{:S(2)}, u32[]{:S(2)}) async-start(f32[16,128,256]{2,1,0:T(8,128)} %broadcast_in_dim.22), calls=%async_computation | async-start | bytes 4194304 | tf_op jit(solution)/shard_map/all_to_all | solution.py:82
  10.9 0.0 copy-done.3
  10.9 0.6 fusion.36
  11.5 0.0 copy-done.4
  11.5 0.0 copy-done.5
  11.5 0.6 clamp_bitcast_fusion.4
  12.1 7.7 %slice_bitcast_fusion.2 = (f32[48,128,128]{2,1,0:T(8,128)}, f32[48,128,128]{2,1,0:T(8,128)}, f32[48,128,128]{2,1,0:T(8,128)}) fusion(f32[3,1,1,48,128,128]{5,4,3,2,1,0:T(8,128)} %param.8), kind=kLoop, calls=%fused_computation.2 | loop fusion | bytes 18874368 | tf_op jit(solution)/shard_map/squeeze | solution.py:107
  19.9 20.1 %all-to-all-done.operand_ref = f32[16,128,256]{2,1,0:T(8,128)S(1)} async-done(((f32[16,128,256]{2,1,0:T(8,128)}), f32[16,128,256]{2,1,0:T(8,128)S(1)}, u32[]{:S(2)}, u32[]{:S(2)}) %all-to-all-start) | async-done | bytes 2097184 | tf_op jit(solution)/shard_map/all_to_all | solution.py:82
  39.9 0.0 copy-start
  39.9 1.3 copy-done
  41.3 11.1 %shard_map.77 = f32[16,128,256]{2,1,0:T(8,128)} custom-call(s32[48]{0:T(128)} %get-tuple-element.18.picked_ref.placed_ref, s32[48]{0:T(128)} %get-tuple-element.7.placed_ref.picked_ref, s32[1]{0:T(128)} %bitcast.5.filled_ref, f32[48,128,128]{2,1,0:T(8,128)} %get-tuple-element.4.tiles_ref, f32[16,128,256]{2,1,0:T(8,128)} %copy-done), custom_call_target="tpu_custom_call" | custom-call | flops 402653184 | bytes 7340032 | tf_op jit(solution)/shard_map/pallas_call | solution.py:67
  52.4 58.6 %all_to_all.60 = f32[16,128,256]{2,1,0:T(8,128)S(1)} all-to-all(f32[16,128,256]{2,1,0:T(8,128)} %shard_map.77), channel_id=1, replica_groups=mesh['row'=16,'col'=16] {'col'}, dimensions={0} | all-to-all | bytes 4194304 | tf_op jit(solution)/shard_map/all_to_all | solution.py:86
  111.0 0.0 copy-start.1
  111.0 0.0 copy-start.2
  111.0 0.1 reduce_sum.60
  111.1 0.8 copy-done.1
  111.9 0.2 copy-done.2
  112.1 0.3 fusion.4
  112.4 0.2 broadcast_in_dim.23
  112.6 33.0 %all_to_all.61.operand_ref = f32[16,128,256]{2,1,0:T(8,128)} all-to-all(f32[16,128,256]{2,1,0:T(8,128)S(1)} %broadcast_in_dim.23), channel_id=1, replica_groups=mesh['row'=16,'col'=16] {'row'}, dimensions={0} | all-to-all | bytes 4194304 | tf_op jit(solution)/shard_map/all_to_all | solution.py:82
  145.6 7.5 %shard_map.78 = f32[16,128,256]{2,1,0:T(8,128)} custom-call(s32[48]{0:T(128)} %get-tuple-element.16.picked_ref.placed_ref, s32[48]{0:T(128)} %get-tuple-element.9.placed_ref.picked_ref, s32[1]{0:T(128)} %bitcast.14.filled_ref, f32[48,128,128]{2,1,0:T(8,128)} %get-tuple-element.6.tiles_ref, f32[16,128,256]{2,1,0:T(8,128)} %all_to_all.61.operand_ref), custom_call_target="tpu_custom_call" | custom-call | flops 402653184 | bytes 7340032 | tf_op jit(solution)/shard_map/pallas_call | solution.py:67
  153.2 62.1 %all_to_all.62 = f32[16,128,256]{2,1,0:T(8,128)S(1)} all-to-all(f32[16,128,256]{2,1,0:T(8,128)} %shard_map.78), channel_id=1, replica_groups=mesh['row'=16,'col'=16] {'col'}, dimensions={0} | all-to-all | bytes 4194304 | tf_op jit(solution)/shard_map/all_to_all | solution.py:86
  215.3 0.1 reduce_sum.62
  215.4 0.3 fusion.2
  215.7 0.2 broadcast_in_dim.24
  215.9 31.7 %all_to_all.63.operand_ref = f32[16,128,256]{2,1,0:T(8,128)} all-to-all(f32[16,128,256]{2,1,0:T(8,128)S(1)} %broadcast_in_dim.24), channel_id=1, replica_groups=mesh['row'=16,'col'=16] {'row'}, dimensions={0} | all-to-all | bytes 4194304 | tf_op jit(solution)/shard_map/all_to_all | solution.py:82
  247.6 5.4 shard_map.79
  253.0 62.5 %all_to_all.64 = f32[16,128,256]{2,1,0:T(8,128)S(1)} all-to-all(f32[16,128,256]{2,1,0:T(8,128)} %shard_map.79), channel_id=1, replica_groups=mesh['row'=16,'col'=16] {'col'}, dimensions={0} | all-to-all | bytes 4194304 | tf_op jit(solution)/shard_map/all_to_all | solution.py:86
  315.5 0.1 reduce_sum.64
  315.6 1.3 fusion
  316.9 0.3 fusion.17
  317.2 0.1 copy.11
  317.3 0.2 broadcast_in_dim.52
  317.5 53.9 %all_to_all.65.operand_ref = f32[16,128,256]{2,1,0:T(8,128)} all-to-all(f32[16,128,256]{2,1,0:T(8,128)S(1)} %broadcast_in_dim.52), channel_id=1, replica_groups=mesh['row'=16,'col'=16] {'col'}, dimensions={0} | all-to-all | bytes 4194304 | tf_op jit(solution)/shard_map/all_to_all | solution.py:82
  371.4 5.4 shard_map.80
  376.8 36.2 %all_to_all.66 = f32[16,128,256]{2,1,0:T(8,128)S(1)} all-to-all(f32[16,128,256]{2,1,0:T(8,128)} %shard_map.80), channel_id=1, replica_groups=mesh['row'=16,'col'=16] {'row'}, dimensions={0} | all-to-all | bytes 4194304 | tf_op jit(solution)/shard_map/all_to_all | solution.py:86
  413.0 0.1 reduce_sum.66
  413.2 0.4 fusion.11
  413.6 0.1 copy.12
  413.7 0.2 broadcast_in_dim.53
  413.9 60.7 %all_to_all.67.operand_ref = f32[16,128,256]{2,1,0:T(8,128)} all-to-all(f32[16,128,256]{2,1,0:T(8,128)S(1)} %broadcast_in_dim.53), channel_id=1, replica_groups=mesh['row'=16,'col'=16] {'col'}, dimensions={0} | all-to-all | bytes 4194304 | tf_op jit(solution)/shard_map/all_to_all | solution.py:82
  474.5 8.1 %shard_map.81 = f32[16,128,256]{2,1,0:T(8,128)} custom-call(s32[48]{0:T(128)} %get-tuple-element.9.placed_ref.picked_ref, s32[48]{0:T(128)} %get-tuple-element.16.picked_ref.placed_ref, s32[1]{0:T(128)} %bitcast.14.filled_ref, f32[48,128,128]{2,1,0:T(8,128)} %get-tuple-element.6.tiles_ref, f32[16,128,256]{2,1,0:T(8,128)} %all_to_all.67.operand_ref), custom_call_target="tpu_custom_call" | custom-call | flops 402653184 | bytes 7340032 | tf_op jit(solution)/shard_map/pallas_call | solution.py:67
  482.6 36.8 %all_to_all.68 = f32[16,128,256]{2,1,0:T(8,128)S(1)} all-to-all(f32[16,128,256]{2,1,0:T(8,128)} %shard_map.81), channel_id=1, replica_groups=mesh['row'=16,'col'=16] {'row'}, dimensions={0} | all-to-all | bytes 4194304 | tf_op jit(solution)/shard_map/all_to_all | solution.py:86
  519.4 0.1 reduce_sum.67
  519.5 0.4 fusion.9
  519.9 0.1 copy.13
  520.0 0.2 broadcast_in_dim.54
  520.2 57.0 %all_to_all.69.operand_ref = f32[16,128,256]{2,1,0:T(8,128)} all-to-all(f32[16,128,256]{2,1,0:T(8,128)S(1)} %broadcast_in_dim.54), channel_id=1, replica_groups=mesh['row'=16,'col'=16] {'col'}, dimensions={0} | all-to-all | bytes 4194304 | tf_op jit(solution)/shard_map/all_to_all | solution.py:82
  577.2 12.4 %shard_map.82 = f32[16,128,256]{2,1,0:T(8,128)} custom-call(s32[48]{0:T(128)} %get-tuple-element.7.placed_ref.picked_ref, s32[48]{0:T(128)} %get-tuple-element.18.picked_ref.placed_ref, s32[1]{0:T(128)} %bitcast.5.filled_ref, f32[48,128,128]{2,1,0:T(8,128)} %get-tuple-element.4.tiles_ref, f32[16,128,256]{2,1,0:T(8,128)} %all_to_all.69.operand_ref), custom_call_target="tpu_custom_call" | custom-call | flops 402653184 | bytes 7340032 | tf_op jit(solution)/shard_map/pallas_call | solution.py:67
  589.6 8.3 %all-to-all-start.11 = ((f32[16,128,256]{2,1,0:T(8,128)}), f32[16,128,256]{2,1,0:T(8,128)S(1)}, u32[]{:S(2)}, u32[]{:S(2)}) async-start(f32[16,128,256]{2,1,0:T(8,128)} %shard_map.82), calls=%async_computation.11 | async-start | bytes 4194304 | tf_op jit(solution)/shard_map/all_to_all | solution.py:86
  597.9 0.1 copy.10
  598.0 0.8 maximum_bitcast_fusion
  598.8 24.7 %all-to-all-done.11 = f32[16,128,256]{2,1,0:T(8,128)S(1)} async-done(((f32[16,128,256]{2,1,0:T(8,128)}), f32[16,128,256]{2,1,0:T(8,128)S(1)}, u32[]{:S(2)}, u32[]{:S(2)}) %all-to-all-start.11) | async-done | bytes 2097184 | tf_op jit(solution)/shard_map/all_to_all | solution.py:86
  623.6 0.1 reduce_sum.68
  623.7 0.4 convolution_bitcast_fusion
  624.1 1.0 copy.15
  (1 shorter events, 0.0 us)
Async XLA Ops:
  3.4 7.5 %copy-start.3 = (s32[3,1,1]{0,2,1:T(1,128)S(1)}, s32[3,1,1]{0,2,1:T(1,128)}, u32[]{:S(2)}) copy-start(s32[3,1,1]{0,2,1:T(1,128)} %param.11) | copy-start | bytes 40
  3.4 8.2 %copy-start.4 = (s32[3,1,1,48]{3,2,1,0:T(1,128)S(1)}, s32[3,1,1,48]{3,2,1,0:T(1,128)}, u32[]{:S(2)}) copy-start(s32[3,1,1,48]{3,2,1,0:T(1,128)} %param.10) | copy-start | bytes 1732
  3.4 8.2 %copy-start.5 = (s32[3,1,1,48]{3,2,1,0:T(1,128)S(1)}, s32[3,1,1,48]{3,2,1,0:T(1,128)}, u32[]{:S(2)}) copy-start(s32[3,1,1,48]{3,2,1,0:T(1,128)} %param.9) | copy-start | bytes 1732
  3.4 36.6 %all-to-all-start = ((f32[16,128,256]{2,1,0:T(8,128)}), f32[16,128,256]{2,1,0:T(8,128)S(1)}, u32[]{:S(2)}, u32[]{:S(2)}) async-start(f32[16,128,256]{2,1,0:T(8,128)} %broadcast_in_dim.22), calls=%async_computation | async-start | bytes 4194304 | tf_op jit(solution)/shard_map/all_to_all | solution.py:82
  39.9 1.3 copy-start
  111.0 1.0 copy-start.1
  111.0 1.1 copy-start.2
  589.6 34.0 %all-to-all-start.11 = ((f32[16,128,256]{2,1,0:T(8,128)}), f32[16,128,256]{2,1,0:T(8,128)S(1)}, u32[]{:S(2)}, u32[]{:S(2)}) async-start(f32[16,128,256]{2,1,0:T(8,128)} %shard_map.82), calls=%async_computation.11 | async-start | bytes 4194304 | tf_op jit(solution)/shard_map/all_to_all | solution.py:86

commit v2 on v1

--- a/solution.py
+++ b/solution.py
@@ -6,6 +6,7 @@
 from jax import lax
 from jax.experimental import pallas as pl
 from jax.experimental.pallas import tpu as pltpu
+from jax.sharding import Mesh
 from jax.sharding import PartitionSpec as P
 
 GROUP = 8
@@ -86,6 +87,28 @@
     return lax.all_to_all(parts, axis, 0, 0, tiled=True).sum(axis=0)
 
 
+def column_slot(position):
+    cores = lax.axis_size("core")
+    return (position % cores) * lax.axis_size("chip") + position // cores
+
+
+def gather_columns(block):
+    chips = lax.axis_size("chip")
+    cores = lax.axis_size("core")
+    by_chip = gather_blocks(block, "chip", chips)
+    stacked = jnp.broadcast_to(by_chip[None], (cores,) + by_chip.shape)
+    both = lax.all_to_all(stacked, "core", 0, 0, tiled=True)
+    return both.reshape((cores * chips,) + block.shape)
+
+
+def scatter_columns(parts):
+    chips = lax.axis_size("chip")
+    cores = lax.axis_size("core")
+    by_core = parts.reshape((cores, chips) + parts.shape[1:])
+    chip_sums = lax.all_to_all(by_core, "core", 0, 0, tiled=True).sum(axis=0)
+    return scatter_sum(chip_sums, "chip")
+
+
 def per_device(rhs, diag_inverse, update_blocks, source_slot, target_slot, block_count):
     levels = rhs.shape[0]
     last_level = levels - 1
@@ -96,35 +119,34 @@
     targets_local = target_slot[:, 0, 0]
     filled_local = block_count[:, 0, 0]
     row_count = lax.axis_size("row")
-    col_count = lax.axis_size("col")
+    col_count = lax.axis_size("chip") * lax.axis_size("core")
     block_shape = rhs_local.shape[1:]
     forward = [apply_inverse(inverse_local[0], rhs_local[0])]
     for level_index in range(1, levels):
         forward_gathered = gather_blocks(forward[-1], "row", row_count)
         forward_zero_terms = jnp.zeros((col_count,) + block_shape, jnp.float32)
-        owner_reduced = scatter_sum(
+        owner_reduced = scatter_columns(
             block_terms(
                 tiles_local[level_index - 1],
                 sources_local[level_index - 1],
-                targets_local[level_index - 1],
+                column_slot(targets_local[level_index - 1]),
                 filled_local[level_index - 1],
                 forward_gathered,
                 forward_zero_terms,
                 False,
             ),
-            "col",
         )
         forward.append(
             apply_inverse(inverse_local[level_index], rhs_local[level_index] - owner_reduced)
         )
     backward = [apply_transposed(inverse_local[last_level], forward[-1])]
     for level_index in range(last_level - 1, -1, -1):
-        gathered = gather_blocks(backward[0], "col", col_count)
+        gathered = gather_columns(backward[0])
         solved = forward[level_index]
         zero_terms = jnp.zeros((row_count,) + block_shape, jnp.float32)
         totals = block_terms(
             tiles_local[level_index],
-            targets_local[level_index],
+            column_slot(targets_local[level_index]),
             sources_local[level_index],
             filled_local[level_index],
             gathered,
@@ -139,15 +161,18 @@
 
 
 def solution(mesh):
+    rows, cols = mesh.devices.shape
+    split = Mesh(mesh.devices.reshape(rows, cols // 2, 2), ("row", "chip", "core"))
+    col = ("chip", "core")
     in_specs = (
-        P(None, "row", "col", None, None),
-        P(None, "row", "col", None, None),
-        P(None, "row", "col", None, None, None),
-        P(None, "row", "col", None),
-        P(None, "row", "col", None),
-        P(None, "row", "col"),
+        P(None, "row", col, None, None),
+        P(None, "row", col, None, None),
+        P(None, "row", col, None, None, None),
+        P(None, "row", col, None),
+        P(None, "row", col, None),
+        P(None, "row", col),
     )
-    out_specs = (P(None, "row", "col", None, None), P(None, "row", "col", None, None))
+    out_specs = (P(None, "row", col, None, None), P(None, "row", col, None, None))
     return jax.shard_map(
-        per_device, mesh=mesh, in_specs=in_specs, out_specs=out_specs, check_vma=False
+        per_device, mesh=split, in_specs=in_specs, out_specs=out_specs, check_vma=False
     )

time: 631 us -> 542 us (0.86)
  blocking collectives: 493 us -> 397 us
    all_to_all x5, blocking collectives: 236 us -> 165 us  [gather_blocks(): return lax.all_to_all(stacked, axis, 0, 0, tiled=True)]
    all_to_all x5, blocking collectives: 256 us -> 193 us  [scatter_sum(): return lax.all_to_all(parts, axis, 0, 0, tiled=True).sum(axis=0)]
    all_to_all x0 -> x6, blocking collectives: none -> 38.8 us  [the longest x3 19.8 us: scatter_columns(): chip_sums = lax.all_to_all(by_core, 'core', 0, 0, tiled=True).sum(axis=0)]
where the time goes in v2:
time: 542 us; the launch traced here: 532 us
  blocking collectives  397 us (73%)
  Pallas kernels  52.7 us (10%)
  waiting for transfers between devices  44.2 us (8%)
  local copies, waits for them, and re-layouts  14.7 us (3%)
  starting transfers between devices  12.8 us (2%)
  matrix products  6.28 us (1%)
    all_to_all x5, blocking collectives, scatter_sum(): return lax.all_to_all(parts, axis, 0, 0, tiled=True).sum(axis=0)  193 us
    all_to_all x5, blocking collectives, gather_blocks(): return lax.all_to_all(stacked, axis, 0, 0, tiled=True)  165 us
    pallas_call x6, Pallas kernels, block_terms_kernel(): pl.pallas_call(functools.partial(_terms_kernel, transposed, group), grid_...  52.7 us
    all_to_all x1, waiting for transfers between devices, scatter_sum(): return lax.all_to_all(parts, axis, 0, 0, tiled=True).sum(axis=0)  24.6 us
    all_to_all x3, blocking collectives, scatter_columns(): chip_sums = lax.all_to_all(by_core, 'core', 0, 0, tiled=True).sum(axis=0)  19.8 us
    all_to_all x1, waiting for transfers between devices, gather_blocks(): return lax.all_to_all(stacked, axis, 0, 0, tiled=True)  19.6 us
    all_to_all x3, blocking collectives, gather_columns(): both = lax.all_to_all(stacked, 'core', 0, 0, tiled=True)  18.9 us
  transfers between devices with their start and end apart: 2, of which 2 were waited for; matrix products, arithmetic and copies ran while one was open for 2% of the time, Pallas kernels for 0%

profile of v2, /device:TPU:8, one launch (start us, length us, event | category | flops | bytes accessed | tf_op | source)
XLA Modules:
  0.0 531.6 jit_solution(1272435386161301979)
XLA Ops:
  0.6 1.2 fusion.6
  1.8 1.5 broadcast_in_dim.28
  3.4 7.5 %all-to-all-start = ((f32[16,128,256]{2,1,0:T(8,128)}), f32[16,128,256]{2,1,0:T(8,128)S(1)}, u32[]{:S(2)}, u32[]{:S(2)}) async-start(f32[16,128,256]{2,1,0:T(8,128)} %broadcast_in_dim.28), calls=%async_computation | async-start | bytes 4194304 | tf_op jit(solution)/shard_map/all_to_all | solution.py:83
  10.9 0.6 fusion.45
  11.5 0.5 clamp_bitcast_fusion.2
  12.1 0.6 fusion.42
  12.7 7.7 %slice_bitcast_fusion.2 = (f32[48,128,128]{2,1,0:T(8,128)}, f32[48,128,128]{2,1,0:T(8,128)}, f32[48,128,128]{2,1,0:T(8,128)}) fusion(f32[3,1,1,48,128,128]{5,4,3,2,1,0:T(8,128)} %param.8), kind=kLoop, calls=%fused_computation.2 | loop fusion | bytes 18874368 | tf_op jit(solution)/shard_map/squeeze | solution.py:130
  20.4 19.6 %all-to-all-done.operand_ref = f32[16,128,256]{2,1,0:T(8,128)S(1)} async-done(((f32[16,128,256]{2,1,0:T(8,128)}), f32[16,128,256]{2,1,0:T(8,128)S(1)}, u32[]{:S(2)}, u32[]{:S(2)}) %all-to-all-start) | async-done | bytes 2097184 | tf_op jit(solution)/shard_map/all_to_all | solution.py:83
  39.9 1.3 copy-done
  41.3 12.1 %shard_map.77 = f32[16,128,256]{2,1,0:T(8,128)} custom-call(s32[48]{0:T(128)} %get-tuple-element.12.picked_ref.placed_ref, s32[48]{0:T(128)} %get-tuple-element.9.placed_ref.picked_ref, s32[1]{0:T(128)} %bitcast.5.filled_ref, f32[48,128,128]{2,1,0:T(8,128)} %get-tuple-element.6.tiles_ref, f32[16,128,256]{2,1,0:T(8,128)} %copy-done), custom_call_target="tpu_custom_call" | custom-call | flops 402653184 | bytes 7340032 | tf_op jit(solution)/shard_map/pallas_call | solution.py:68
  53.4 6.6 %all_to_all.90 = f32[2,8,128,256]{3,2,1,0:T(8,128)S(1)} all-to-all(f32[2,8,128,256]{3,2,1,0:T(8,128)} %bitcast.154), channel_id=1, replica_groups=mesh['row'=16,'chip'=8,'core'=2] {'core'}, dimensions={0} | all-to-all | bytes 4194304 | tf_op jit(solution)/shard_map/all_to_all | solution.py:108
  60.0 0.2 reduce_sum.87
  60.3 36.9 %all_to_all.91 = f32[8,128,256]{2,1,0:T(8,128)S(1)} all-to-all(f32[8,128,256]{2,1,0:T(8,128)S(1)} %reduce_sum.87), channel_id=1, replica_groups=mesh['row'=16,'chip'=8,'core'=2] {'chip'}, dimensions={0} | all-to-all | bytes 2097152 | tf_op jit(solution)/shard_map/all_to_all | solution.py:87
  97.2 0.1 reduce_sum.88
  97.3 1.2 fusion.4
  98.4 0.2 broadcast_in_dim.29
  98.6 34.0 %all_to_all.92.operand_ref = f32[16,128,256]{2,1,0:T(8,128)} all-to-all(f32[16,128,256]{2,1,0:T(8,128)S(1)} %broadcast_in_dim.29), channel_id=1, replica_groups=mesh['row'=16,'chip'=8,'core'=2] {'row'}, dimensions={0} | all-to-all | bytes 4194304 | tf_op jit(solution)/shard_map/all_to_all | solution.py:83
  132.6 6.0 %shard_map.78 = f32[16,128,256]{2,1,0:T(8,128)} custom-call(s32[48]{0:T(128)} %get-tuple-element.14.picked_ref.placed_ref, s32[48]{0:T(128)} %get-tuple-element.11.placed_ref.picked_ref, s32[1]{0:T(128)} %bitcast.15.filled_ref, f32[48,128,128]{2,1,0:T(8,128)} %get-tuple-element.8.tiles_ref, f32[16,128,256]{2,1,0:T(8,128)} %all_to_all.92.operand_ref), custom_call_target="tpu_custom_call" | custom-call | flops 402653184 | bytes 7340032 | tf_op jit(solution)/shard_map/pallas_call | solution.py:68
  138.6 6.6 %all_to_all.93 = f32[2,8,128,256]{3,2,1,0:T(8,128)S(1)} all-to-all(f32[2,8,128,256]{3,2,1,0:T(8,128)} %bitcast.155), channel_id=1, replica_groups=mesh['row'=16,'chip'=8,'core'=2] {'core'}, dimensions={0} | all-to-all | bytes 4194304 | tf_op jit(solution)/shard_map/all_to_all | solution.py:108
  145.3 0.2 reduce_sum.90
  145.5 38.1 %all_to_all.94 = f32[8,128,256]{2,1,0:T(8,128)S(1)} all-to-all(f32[8,128,256]{2,1,0:T(8,128)S(1)} %reduce_sum.90), channel_id=1, replica_groups=mesh['row'=16,'chip'=8,'core'=2] {'chip'}, dimensions={0} | all-to-all | bytes 2097152 | tf_op jit(solution)/shard_map/all_to_all | solution.py:87
  183.6 0.1 reduce_sum.91
  183.7 1.2 fusion.2
  184.9 0.2 broadcast_in_dim.30
  185.1 35.0 %all_to_all.95.operand_ref = f32[16,128,256]{2,1,0:T(8,128)} all-to-all(f32[16,128,256]{2,1,0:T(8,128)S(1)} %broadcast_in_dim.30), channel_id=1, replica_groups=mesh['row'=16,'chip'=8,'core'=2] {'row'}, dimensions={0} | all-to-all | bytes 4194304 | tf_op jit(solution)/shard_map/all_to_all | solution.py:83
  220.1 7.1 %shard_map.79 = f32[16,128,256]{2,1,0:T(8,128)} custom-call(s32[48]{0:T(128)} %get-tuple-element.13.picked_ref.placed_ref, s32[48]{0:T(128)} %get-tuple-element.10.placed_ref.picked_ref, s32[1]{0:T(128)} %bitcast.25.filled_ref, f32[48,128,128]{2,1,0:T(8,128)} %get-tuple-element.7.tiles_ref, f32[16,128,256]{2,1,0:T(8,128)} %all_to_all.95.operand_ref), custom_call_target="tpu_custom_call" | custom-call | flops 402653184 | bytes 7340032 | tf_op jit(solution)/shard_map/pallas_call | solution.py:68
  227.2 6.6 %all_to_all.96 = f32[2,8,128,256]{3,2,1,0:T(8,128)S(1)} all-to-all(f32[2,8,128,256]{3,2,1,0:T(8,128)} %bitcast.156), channel_id=1, replica_groups=mesh['row'=16,'chip'=8,'core'=2] {'core'}, dimensions={0} | all-to-all | bytes 4194304 | tf_op jit(solution)/shard_map/all_to_all | solution.py:108
  233.8 0.2 reduce_sum.93
  234.1 31.9 %all_to_all.97 = f32[8,128,256]{2,1,0:T(8,128)S(1)} all-to-all(f32[8,128,256]{2,1,0:T(8,128)S(1)} %reduce_sum.93), channel_id=1, replica_groups=mesh['row'=16,'chip'=8,'core'=2] {'chip'}, dimensions={0} | all-to-all | bytes 2097152 | tf_op jit(solution)/shard_map/all_to_all | solution.py:87
  265.9 0.1 reduce_sum.94
  266.0 1.3 fusion
  267.3 0.3 fusion.17
  267.6 0.1 copy.19
  267.7 0.1 broadcast_in_dim.32
  267.8 31.6 %all_to_all.98 = f32[8,128,256]{2,1,0:T(8,128)S(1)} all-to-all(f32[8,128,256]{2,1,0:T(8,128)S(1)} %broadcast_in_dim.32), channel_id=1, replica_groups=mesh['row'=16,'chip'=8,'core'=2] {'chip'}, dimensions={0} | all-to-all | bytes 2097152 | tf_op jit(solution)/shard_map/all_to_all | solution.py:83
  299.4 0.2 broadcast_in_dim.33
  299.6 6.3 %all_to_all.99 = f32[2,8,128,256]{3,2,1,0:T(8,128)} all-to-all(f32[2,8,128,256]{3,2,1,0:T(8,128)S(1)} %broadcast_in_dim.33), channel_id=1, replica_groups=mesh['row'=16,'chip'=8,'core'=2] {'core'}, dimensions={0} | all-to-all | bytes 4194304 | tf_op jit(solution)/shard_map/all_to_all | solution.py:100
  305.9 7.6 %shard_map.80 = f32[16,128,256]{2,1,0:T(8,128)} custom-call(s32[48]{0:T(128)} %get-tuple-element.10.placed_ref.picked_ref, s32[48]{0:T(128)} %get-tuple-element.13.picked_ref.placed_ref, s32[1]{0:T(128)} %bitcast.25.filled_ref, f32[48,128,128]{2,1,0:T(8,128)} %get-tuple-element.7.tiles_ref, f32[16,128,256]{2,1,0:T(8,128)} %bitcast.151), custom_call_target="tpu_custom_call" | custom-call | flops 402653184 | bytes 7340032 | tf_op jit(solution)/shard_map/pallas_call | solution.py:68
  313.5 48.4 %all_to_all.100 = f32[16,128,256]{2,1,0:T(8,128)S(1)} all-to-all(f32[16,128,256]{2,1,0:T(8,128)} %shard_map.80), channel_id=1, replica_groups=mesh['row'=16,'chip'=8,'core'=2] {'row'}, dimensions={0} | all-to-all | bytes 4194304 | tf_op jit(solution)/shard_map/all_to_all | solution.py:87
  361.9 0.1 reduce_sum.96
  362.1 0.8 copy-done.2
  362.9 0.4 fusion.11
  363.3 0.1 copy.20
  363.4 0.1 broadcast_in_dim.34
  363.5 30.2 %all_to_all.101 = f32[8,128,256]{2,1,0:T(8,128)S(1)} all-to-all(f32[8,128,256]{2,1,0:T(8,128)S(1)} %broadcast_in_dim.34), channel_id=1, replica_groups=mesh['row'=16,'chip'=8,'core'=2] {'chip'}, dimensions={0} | all-to-all | bytes 2097152 | tf_op jit(solution)/shard_map/all_to_all | solution.py:83
  393.7 0.2 broadcast_in_dim.35
  393.9 6.3 %all_to_all.102 = f32[2,8,128,256]{3,2,1,0:T(8,128)} all-to-all(f32[2,8,128,256]{3,2,1,0:T(8,128)S(1)} %broadcast_in_dim.35), channel_id=1, replica_groups=mesh['row'=16,'chip'=8,'core'=2] {'core'}, dimensions={0} | all-to-all | bytes 4194304 | tf_op jit(solution)/shard_map/all_to_all | solution.py:100
  400.2 6.2 %shard_map.81 = f32[16,128,256]{2,1,0:T(8,128)} custom-call(s32[48]{0:T(128)} %get-tuple-element.11.placed_ref.picked_ref, s32[48]{0:T(128)} %get-tuple-element.14.picked_ref.placed_ref, s32[1]{0:T(128)} %bitcast.15.filled_ref, f32[48,128,128]{2,1,0:T(8,128)} %get-tuple-element.8.tiles_ref, f32[16,128,256]{2,1,0:T(8,128)} %bitcast.152), custom_call_target="tpu_custom_call" | custom-call | flops 402653184 | bytes 7340032 | tf_op jit(solution)/shard_map/pallas_call | solution.py:68
  406.4 37.7 %all_to_all.103 = f32[16,128,256]{2,1,0:T(8,128)S(1)} all-to-all(f32[16,128,256]{2,1,0:T(8,128)} %shard_map.81), channel_id=1, replica_groups=mesh['row'=16,'chip'=8,'core'=2] {'row'}, dimensions={0} | all-to-all | bytes 4194304 | tf_op jit(solution)/shard_map/all_to_all | solution.py:87
  444.1 0.1 reduce_sum.97
  444.2 0.4 fusion.9
  444.6 0.1 copy.21
  444.7 0.1 broadcast_in_dim.36
  444.8 34.2 %all_to_all.104 = f32[8,128,256]{2,1,0:T(8,128)S(1)} all-to-all(f32[8,128,256]{2,1,0:T(8,128)S(1)} %broadcast_in_dim.36), channel_id=1, replica_groups=mesh['row'=16,'chip'=8,'core'=2] {'chip'}, dimensions={0} | all-to-all | bytes 2097152 | tf_op jit(solution)/shard_map/all_to_all | solution.py:83
  479.0 0.2 broadcast_in_dim.37
  479.2 6.3 %all_to_all.105 = f32[2,8,128,256]{3,2,1,0:T(8,128)} all-to-all(f32[2,8,128,256]{3,2,1,0:T(8,128)S(1)} %broadcast_in_dim.37), channel_id=1, replica_groups=mesh['row'=16,'chip'=8,'core'=2] {'core'}, dimensions={0} | all-to-all | bytes 4194304 | tf_op jit(solution)/shard_map/all_to_all | solution.py:100
  485.5 13.6 %shard_map.82 = f32[16,128,256]{2,1,0:T(8,128)} custom-call(s32[48]{0:T(128)} %get-tuple-element.9.placed_ref.picked_ref, s32[48]{0:T(128)} %get-tuple-element.12.picked_ref.placed_ref, s32[1]{0:T(128)} %bitcast.5.filled_ref, f32[48,128,128]{2,1,0:T(8,128)} %get-tuple-element.6.tiles_ref, f32[16,128,256]{2,1,0:T(8,128)} %bitcast.153), custom_call_target="tpu_custom_call" | custom-call | flops 402653184 | bytes 7340032 | tf_op jit(solution)/shard_map/pallas_call | solution.py:68
  499.2 5.3 all-to-all-start.17
  504.5 0.1 copy.18
  504.6 0.8 maximum_bitcast_fusion
  505.4 24.6 %all-to-all-done.17 = f32[16,128,256]{2,1,0:T(8,128)S(1)} async-done(((f32[16,128,256]{2,1,0:T(8,128)}), f32[16,128,256]{2,1,0:T(8,128)S(1)}, u32[]{:S(2)}, u32[]{:S(2)}) %all-to-all-start.17) | async-done | bytes 2097184 | tf_op jit(solution)/shard_map/all_to_all | solution.py:87
  530.0 0.1 reduce_sum.98
  530.1 0.4 convolution_bitcast_fusion
  530.6 1.0 copy.23
  (11 shorter events, 0.1 us)
Async XLA Ops:
  3.4 7.5 %copy-start.3 = (s32[3,1,1]{0,2,1:T(1,128)S(1)}, s32[3,1,1]{0,2,1:T(1,128)}, u32[]{:S(2)}) copy-start(s32[3,1,1]{0,2,1:T(1,128)} %param.11) | copy-start | bytes 40
  3.4 8.2 %copy-start.4 = (s32[3,1,1,48]{3,2,1,0:T(1,128)S(1)}, s32[3,1,1,48]{3,2,1,0:T(1,128)}, u32[]{:S(2)}) copy-start(s32[3,1,1,48]{3,2,1,0:T(1,128)} %param.9) | copy-start | bytes 1732
  3.4 8.7 %copy-start.5 = (s32[3,1,1,48]{3,2,1,0:T(1,128)S(1)}, s32[3,1,1,48]{3,2,1,0:T(1,128)}, u32[]{:S(2)}) copy-start(s32[3,1,1,48]{3,2,1,0:T(1,128)} %param.10) | copy-start | bytes 1732
  3.4 36.6 %all-to-all-start = ((f32[16,128,256]{2,1,0:T(8,128)}), f32[16,128,256]{2,1,0:T(8,128)S(1)}, u32[]{:S(2)}, u32[]{:S(2)}) async-start(f32[16,128,256]{2,1,0:T(8,128)} %broadcast_in_dim.28), calls=%async_computation | async-start | bytes 4194304 | tf_op jit(solution)/shard_map/all_to_all | solution.py:83
  39.9 1.3 copy-start
  234.1 31.9 %copy-start.1 = (f32[4,1,1,128,128]{4,3,2,1,0:T(8,128)S(1)}, f32[4,1,1,128,128]{4,3,2,1,0:T(8,128)}, u32[]{:S(2)}) copy-start(f32[4,1,1,128,128]{4,3,2,1,0:T(8,128)} %param.7) | copy-start | bytes 786436
  361.9 1.0 copy-start.2
  499.2 30.8 %all-to-all-start.17 = ((f32[16,128,256]{2,1,0:T(8,128)}), f32[16,128,256]{2,1,0:T(8,128)S(1)}, u32[]{:S(2)}, u32[]{:S(2)}) async-start(f32[16,128,256]{2,1,0:T(8,128)} %shard_map.82), calls=%async_computation.17 | async-start | bytes 4194304 | tf_op jit(solution)/shard_map/all_to_all | solution.py:87

commit v3 on v2

--- a/solution.py
+++ b/solution.py
@@ -20,12 +20,21 @@
     return jnp.einsum("...ts,...tn->...sn", inverse, values, precision=lax.Precision.HIGHEST)
 
 
-def _terms_kernel(transposed, group, picked_ref, placed_ref, filled_ref, tiles_ref, operand_ref, out_ref):
+def _split(values):
+    high = values.astype(jnp.bfloat16)
+    low = (values - high.astype(jnp.float32)).astype(jnp.bfloat16)
+    return high, low
+
+
+def _terms_kernel(transposed, group, picked_ref, placed_ref, filled_ref, tiles_ref, operand_ref, out_ref, split_ref):
     step = pl.program_id(0)
 
     @pl.when(step == 0)
     def _():
         out_ref[...] = jnp.zeros_like(out_ref)
+        for source in range(operand_ref.shape[0]):
+            high, low = _split(operand_ref[source])
+            split_ref[source] = jnp.concatenate([high, low, high], axis=0)
 
     filled = filled_ref[0]
     for g in range(group):
@@ -33,16 +42,16 @@
 
         @pl.when(b < filled)
         def _():
-            source = picked_ref[b]
-            target = placed_ref[b]
-            tile = tiles_ref[g]
-            values = operand_ref[source]
+            high, low = _split(tiles_ref[g])
+            values = split_ref[picked_ref[b]]
             if transposed:
-                product = lax.dot_general(tile, values, (((0,), (0,)), ((), ())),
-                                          precision=lax.Precision.HIGHEST, preferred_element_type=jnp.float32)
+                stacked = jnp.concatenate([high, high, low], axis=0)
+                product = lax.dot_general(stacked, values, (((0,), (0,)), ((), ())),
+                                          preferred_element_type=jnp.float32)
             else:
-                product = jnp.dot(tile, values, precision=lax.Precision.HIGHEST, preferred_element_type=jnp.float32)
-            out_ref[target] += product
+                stacked = jnp.concatenate([high, high, low], axis=1)
+                product = jnp.dot(stacked, values, preferred_element_type=jnp.float32)
+            out_ref[placed_ref[b]] += product
 
 
 def block_terms_kernel(tile_stack, picked, placed, filled, operand, count, transposed):
@@ -63,6 +72,7 @@
             pl.BlockSpec((n_src, s, width), lambda j, *_: (0, 0, 0)),
         ],
         out_specs=pl.BlockSpec((count, s, width), lambda j, *_: (0, 0, 0)),
+        scratch_shapes=[pltpu.VMEM((n_src, 3 * s, width), jnp.bfloat16)],
     )
     flops = 2 * slot_count * s * s * width
     return pl.pallas_call(

time: 542 us -> 517 us (0.954); the launches traced: 532 us -> 513 us
  blocking collectives: 397 us -> 384 us
  Pallas kernels: 52.7 us -> 44 us
    all_to_all x5, blocking collectives: 193 us -> 179 us  [scatter_sum(): return lax.all_to_all(parts, axis, 0, 0, tiled=True).sum(axis=0)]
    pallas_call x6, Pallas kernels: 52.7 us -> 44 us  [block_terms_kernel(): pl.pallas_call(functools.partial(_terms_kernel, transposed, group), grid_...]
where the time goes in v3:
time: 517 us; the launch traced here: 513 us
  blocking collectives  384 us (74%)
  waiting for transfers between devices  46.1 us (9%)
  Pallas kernels  44 us (9%)
  local copies, waits for them, and re-layouts  14.7 us (3%)
  starting transfers between devices  13.7 us (3%)
  matrix products  6.28 us (1%)
    all_to_all x5, blocking collectives, scatter_sum(): return lax.all_to_all(parts, axis, 0, 0, tiled=True).sum(axis=0)  179 us
    all_to_all x5, blocking collectives, gather_blocks(): return lax.all_to_all(stacked, axis, 0, 0, tiled=True)  164 us
    pallas_call x6, Pallas kernels, block_terms_kernel(): pl.pallas_call(functools.partial(_terms_kernel, transposed, group), grid_...  44 us
    all_to_all x1, waiting for transfers between devices, scatter_sum(): return lax.all_to_all(parts, axis, 0, 0, tiled=True).sum(axis=0)  26.6 us
    all_to_all x3, blocking collectives, scatter_columns(): chip_sums = lax.all_to_all(by_core, 'core', 0, 0, tiled=True).sum(axis=0)  22.1 us
    all_to_all x1, waiting for transfers between devices, gather_blocks(): return lax.all_to_all(stacked, axis, 0, 0, tiled=True)  19.6 us
    all_to_all x3, blocking collectives, gather_columns(): both = lax.all_to_all(stacked, 'core', 0, 0, tiled=True)  18.9 us
  transfers between devices with their start and end apart: 2, of which 2 were waited for; matrix products, arithmetic and copies ran while one was open for 2% of the time, Pallas kernels for 0%

profile of v3, /device:TPU:8, one launch (start us, length us, event | category | flops | bytes accessed | tf_op | source)
XLA Modules:
  0.0 513.0 jit_solution(12496670990686822218)
XLA Ops:
  0.6 1.2 fusion.6
  1.8 1.5 broadcast_in_dim.28
  3.4 7.5 %all-to-all-start = ((f32[16,128,256]{2,1,0:T(8,128)}), f32[16,128,256]{2,1,0:T(8,128)S(1)}, u32[]{:S(2)}, u32[]{:S(2)}) async-start(f32[16,128,256]{2,1,0:T(8,128)} %broadcast_in_dim.28), calls=%async_computation | async-start | bytes 4194304 | tf_op jit(solution)/shard_map/all_to_all | solution.py:93
  10.9 0.6 fusion.45
  11.5 0.5 clamp_bitcast_fusion.2
  12.1 0.6 fusion.42
  12.7 7.7 %slice_bitcast_fusion.2 = (f32[48,128,128]{2,1,0:T(8,128)}, f32[48,128,128]{2,1,0:T(8,128)}, f32[48,128,128]{2,1,0:T(8,128)}) fusion(f32[3,1,1,48,128,128]{5,4,3,2,1,0:T(8,128)} %param.8), kind=kLoop, calls=%fused_computation.2 | loop fusion | bytes 18874368 | tf_op jit(solution)/shard_map/squeeze | solution.py:140
  20.4 19.6 %all-to-all-done.operand_ref = f32[16,128,256]{2,1,0:T(8,128)S(1)} async-done(((f32[16,128,256]{2,1,0:T(8,128)}), f32[16,128,256]{2,1,0:T(8,128)S(1)}, u32[]{:S(2)}, u32[]{:S(2)}) %all-to-all-start) | async-done | bytes 2097184 | tf_op jit(solution)/shard_map/all_to_all | solution.py:93
  39.9 1.3 copy-done
  41.3 9.6 %shard_map.77 = f32[16,128,256]{2,1,0:T(8,128)} custom-call(s32[48]{0:T(128)} %get-tuple-element.12.picked_ref.placed_ref, s32[48]{0:T(128)} %get-tuple-element.9.placed_ref.picked_ref, s32[1]{0:T(128)} %bitcast.5.filled_ref, f32[48,128,128]{2,1,0:T(8,128)} %get-tuple-element.6.tiles_ref, f32[16,128,256]{2,1,0:T(8,128)} %copy-done), custom_call_target="tpu_custom_call" | custom-call | flops 402653184 | bytes 7340032 | tf_op jit(solution)/shard_map/pallas_call | solution.py:78
  50.8 6.6 %all_to_all.90 = f32[2,8,128,256]{3,2,1,0:T(8,128)S(1)} all-to-all(f32[2,8,128,256]{3,2,1,0:T(8,128)} %bitcast.154), channel_id=1, replica_groups=mesh['row'=16,'chip'=8,'core'=2] {'core'}, dimensions={0} | all-to-all | bytes 4194304 | tf_op jit(solution)/shard_map/all_to_all | solution.py:118
  57.4 0.2 reduce_sum.87
  57.7 38.0 %all_to_all.91 = f32[8,128,256]{2,1,0:T(8,128)S(1)} all-to-all(f32[8,128,256]{2,1,0:T(8,128)S(1)} %reduce_sum.87), channel_id=1, replica_groups=mesh['row'=16,'chip'=8,'core'=2] {'chip'}, dimensions={0} | all-to-all | bytes 2097152 | tf_op jit(solution)/shard_map/all_to_all | solution.py:97
  95.7 0.1 reduce_sum.88
  95.8 1.2 fusion.4
  97.0 0.2 broadcast_in_dim.29
  97.2 31.7 %all_to_all.92.operand_ref = f32[16,128,256]{2,1,0:T(8,128)} all-to-all(f32[16,128,256]{2,1,0:T(8,128)S(1)} %broadcast_in_dim.29), channel_id=1, replica_groups=mesh['row'=16,'chip'=8,'core'=2] {'row'}, dimensions={0} | all-to-all | bytes 4194304 | tf_op jit(solution)/shard_map/all_to_all | solution.py:93
  128.9 6.6 %shard_map.78 = f32[16,128,256]{2,1,0:T(8,128)} custom-call(s32[48]{0:T(128)} %get-tuple-element.14.picked_ref.placed_ref, s32[48]{0:T(128)} %get-tuple-element.11.placed_ref.picked_ref, s32[1]{0:T(128)} %bitcast.15.filled_ref, f32[48,128,128]{2,1,0:T(8,128)} %get-tuple-element.8.tiles_ref, f32[16,128,256]{2,1,0:T(8,128)} %all_to_all.92.operand_ref), custom_call_target="tpu_custom_call" | custom-call | flops 402653184 | bytes 7340032 | tf_op jit(solution)/shard_map/pallas_call | solution.py:78
  135.5 8.9 %all_to_all.93 = f32[2,8,128,256]{3,2,1,0:T(8,128)S(1)} all-to-all(f32[2,8,128,256]{3,2,1,0:T(8,128)} %bitcast.155), channel_id=1, replica_groups=mesh['row'=16,'chip'=8,'core'=2] {'core'}, dimensions={0} | all-to-all | bytes 4194304 | tf_op jit(solution)/shard_map/all_to_all | solution.py:118
  144.3 0.2 reduce_sum.90
  144.6 31.7 %all_to_all.94 = f32[8,128,256]{2,1,0:T(8,128)S(1)} all-to-all(f32[8,128,256]{2,1,0:T(8,128)S(1)} %reduce_sum.90), channel_id=1, replica_groups=mesh['row'=16,'chip'=8,'core'=2] {'chip'}, dimensions={0} | all-to-all | bytes 2097152 | tf_op jit(solution)/shard_map/all_to_all | solution.py:97
  176.3 0.1 reduce_sum.91
  176.4 1.2 fusion.2
  177.5 0.2 broadcast_in_dim.30
  177.8 32.9 %all_to_all.95.operand_ref = f32[16,128,256]{2,1,0:T(8,128)} all-to-all(f32[16,128,256]{2,1,0:T(8,128)S(1)} %broadcast_in_dim.30), channel_id=1, replica_groups=mesh['row'=16,'chip'=8,'core'=2] {'row'}, dimensions={0} | all-to-all | bytes 4194304 | tf_op jit(solution)/shard_map/all_to_all | solution.py:93
  210.7 5.6 %shard_map.79 = f32[16,128,256]{2,1,0:T(8,128)} custom-call(s32[48]{0:T(128)} %get-tuple-element.13.picked_ref.placed_ref, s32[48]{0:T(128)} %get-tuple-element.10.placed_ref.picked_ref, s32[1]{0:T(128)} %bitcast.25.filled_ref, f32[48,128,128]{2,1,0:T(8,128)} %get-tuple-element.7.tiles_ref, f32[16,128,256]{2,1,0:T(8,128)} %all_to_all.95.operand_ref), custom_call_target="tpu_custom_call" | custom-call | flops 402653184 | bytes 7340032 | tf_op jit(solution)/shard_map/pallas_call | solution.py:78
  216.2 6.6 %all_to_all.96 = f32[2,8,128,256]{3,2,1,0:T(8,128)S(1)} all-to-all(f32[2,8,128,256]{3,2,1,0:T(8,128)} %bitcast.156), channel_id=1, replica_groups=mesh['row'=16,'chip'=8,'core'=2] {'core'}, dimensions={0} | all-to-all | bytes 4194304 | tf_op jit(solution)/shard_map/all_to_all | solution.py:118
  222.8 0.2 reduce_sum.93
  223.1 36.2 %all_to_all.97 = f32[8,128,256]{2,1,0:T(8,128)S(1)} all-to-all(f32[8,128,256]{2,1,0:T(8,128)S(1)} %reduce_sum.93), channel_id=1, replica_groups=mesh['row'=16,'chip'=8,'core'=2] {'chip'}, dimensions={0} | all-to-all | bytes 2097152 | tf_op jit(solution)/shard_map/all_to_all | solution.py:97
  259.2 0.1 reduce_sum.94
  259.3 1.3 fusion
  260.6 0.3 fusion.17
  260.9 0.1 copy.19
  261.0 0.1 broadcast_in_dim.32
  261.1 30.4 %all_to_all.98 = f32[8,128,256]{2,1,0:T(8,128)S(1)} all-to-all(f32[8,128,256]{2,1,0:T(8,128)S(1)} %broadcast_in_dim.32), channel_id=1, replica_groups=mesh['row'=16,'chip'=8,'core'=2] {'chip'}, dimensions={0} | all-to-all | bytes 2097152 | tf_op jit(solution)/shard_map/all_to_all | solution.py:93
  291.5 0.2 broadcast_in_dim.33
  291.7 6.3 %all_to_all.99 = f32[2,8,128,256]{3,2,1,0:T(8,128)} all-to-all(f32[2,8,128,256]{3,2,1,0:T(8,128)S(1)} %broadcast_in_dim.33), channel_id=1, replica_groups=mesh['row'=16,'chip'=8,'core'=2] {'core'}, dimensions={0} | all-to-all | bytes 4194304 | tf_op jit(solution)/shard_map/all_to_all | solution.py:110
  298.0 5.6 %shard_map.80 = f32[16,128,256]{2,1,0:T(8,128)} custom-call(s32[48]{0:T(128)} %get-tuple-element.10.placed_ref.picked_ref, s32[48]{0:T(128)} %get-tuple-element.13.picked_ref.placed_ref, s32[1]{0:T(128)} %bitcast.25.filled_ref, f32[48,128,128]{2,1,0:T(8,128)} %get-tuple-element.7.tiles_ref, f32[16,128,256]{2,1,0:T(8,128)} %bitcast.151), custom_call_target="tpu_custom_call" | custom-call | flops 402653184 | bytes 7340032 | tf_op jit(solution)/shard_map/pallas_call | solution.py:78
  303.6 37.6 %all_to_all.100 = f32[16,128,256]{2,1,0:T(8,128)S(1)} all-to-all(f32[16,128,256]{2,1,0:T(8,128)} %shard_map.80), channel_id=1, replica_groups=mesh['row'=16,'chip'=8,'core'=2] {'row'}, dimensions={0} | all-to-all | bytes 4194304 | tf_op jit(solution)/shard_map/all_to_all | solution.py:97
  341.2 0.1 reduce_sum.96
  341.4 0.8 copy-done.2
  342.2 0.4 fusion.11
  342.6 0.1 copy.20
  342.7 0.1 broadcast_in_dim.34
  342.8 34.5 %all_to_all.101 = f32[8,128,256]{2,1,0:T(8,128)S(1)} all-to-all(f32[8,128,256]{2,1,0:T(8,128)S(1)} %broadcast_in_dim.34), channel_id=1, replica_groups=mesh['row'=16,'chip'=8,'core'=2] {'chip'}, dimensions={0} | all-to-all | bytes 2097152 | tf_op jit(solution)/shard_map/all_to_all | solution.py:93
  377.3 0.2 broadcast_in_dim.35
  377.5 6.3 %all_to_all.102 = f32[2,8,128,256]{3,2,1,0:T(8,128)} all-to-all(f32[2,8,128,256]{3,2,1,0:T(8,128)S(1)} %broadcast_in_dim.35), channel_id=1, replica_groups=mesh['row'=16,'chip'=8,'core'=2] {'core'}, dimensions={0} | all-to-all | bytes 4194304 | tf_op jit(solution)/shard_map/all_to_all | solution.py:110
  383.8 6.7 %shard_map.81 = f32[16,128,256]{2,1,0:T(8,128)} custom-call(s32[48]{0:T(128)} %get-tuple-element.11.placed_ref.picked_ref, s32[48]{0:T(128)} %get-tuple-element.14.picked_ref.placed_ref, s32[1]{0:T(128)} %bitcast.15.filled_ref, f32[48,128,128]{2,1,0:T(8,128)} %get-tuple-element.8.tiles_ref, f32[16,128,256]{2,1,0:T(8,128)} %bitcast.152), custom_call_target="tpu_custom_call" | custom-call | flops 402653184 | bytes 7340032 | tf_op jit(solution)/shard_map/pallas_call | solution.py:78
  390.5 35.4 %all_to_all.103 = f32[16,128,256]{2,1,0:T(8,128)S(1)} all-to-all(f32[16,128,256]{2,1,0:T(8,128)} %shard_map.81), channel_id=1, replica_groups=mesh['row'=16,'chip'=8,'core'=2] {'row'}, dimensions={0} | all-to-all | bytes 4194304 | tf_op jit(solution)/shard_map/all_to_all | solution.py:97
  425.9 0.1 reduce_sum.97
  426.1 0.4 fusion.9
  426.4 0.1 copy.21
  426.6 0.1 broadcast_in_dim.36
  426.6 34.6 %all_to_all.104 = f32[8,128,256]{2,1,0:T(8,128)S(1)} all-to-all(f32[8,128,256]{2,1,0:T(8,128)S(1)} %broadcast_in_dim.36), channel_id=1, replica_groups=mesh['row'=16,'chip'=8,'core'=2] {'chip'}, dimensions={0} | all-to-all | bytes 2097152 | tf_op jit(solution)/shard_map/all_to_all | solution.py:93
  461.2 0.2 broadcast_in_dim.37
  461.4 6.3 %all_to_all.105 = f32[2,8,128,256]{3,2,1,0:T(8,128)} all-to-all(f32[2,8,128,256]{3,2,1,0:T(8,128)S(1)} %broadcast_in_dim.37), channel_id=1, replica_groups=mesh['row'=16,'chip'=8,'core'=2] {'core'}, dimensions={0} | all-to-all | bytes 4194304 | tf_op jit(solution)/shard_map/all_to_all | solution.py:110
  467.7 10.1 %shard_map.82 = f32[16,128,256]{2,1,0:T(8,128)} custom-call(s32[48]{0:T(128)} %get-tuple-element.9.placed_ref.picked_ref, s32[48]{0:T(128)} %get-tuple-element.12.picked_ref.placed_ref, s32[1]{0:T(128)} %bitcast.5.filled_ref, f32[48,128,128]{2,1,0:T(8,128)} %get-tuple-element.6.tiles_ref, f32[16,128,256]{2,1,0:T(8,128)} %bitcast.153), custom_call_target="tpu_custom_call" | custom-call | flops 402653184 | bytes 7340032 | tf_op jit(solution)/shard_map/pallas_call | solution.py:78
  477.8 6.2 %all-to-all-start.17 = ((f32[16,128,256]{2,1,0:T(8,128)}), f32[16,128,256]{2,1,0:T(8,128)S(1)}, u32[]{:S(2)}, u32[]{:S(2)}) async-start(f32[16,128,256]{2,1,0:T(8,128)} %shard_map.82), calls=%async_computation.17 | async-start | bytes 4194304 | tf_op jit(solution)/shard_map/all_to_all | solution.py:97
  483.9 0.1 copy.18
  484.1 0.8 maximum_bitcast_fusion
  484.9 26.6 %all-to-all-done.17 = f32[16,128,256]{2,1,0:T(8,128)S(1)} async-done(((f32[16,128,256]{2,1,0:T(8,128)}), f32[16,128,256]{2,1,0:T(8,128)S(1)}, u32[]{:S(2)}, u32[]{:S(2)}) %all-to-all-start.17) | async-done | bytes 2097184 | tf_op jit(solution)/shard_map/all_to_all | solution.py:97
  511.5 0.1 reduce_sum.98
  511.6 0.4 convolution_bitcast_fusion
  512.0 1.0 copy.23
  (11 shorter events, 0.1 us)
Async XLA Ops:
  3.4 7.5 %copy-start.3 = (s32[3,1,1]{0,2,1:T(1,128)S(1)}, s32[3,1,1]{0,2,1:T(1,128)}, u32[]{:S(2)}) copy-start(s32[3,1,1]{0,2,1:T(1,128)} %param.11) | copy-start | bytes 40
  3.4 8.2 %copy-start.4 = (s32[3,1,1,48]{3,2,1,0:T(1,128)S(1)}, s32[3,1,1,48]{3,2,1,0:T(1,128)}, u32[]{:S(2)}) copy-start(s32[3,1,1,48]{3,2,1,0:T(1,128)} %param.9) | copy-start | bytes 1732
  3.4 8.7 %copy-start.5 = (s32[3,1,1,48]{3,2,1,0:T(1,128)S(1)}, s32[3,1,1,48]{3,2,1,0:T(1,128)}, u32[]{:S(2)}) copy-start(s32[3,1,1,48]{3,2,1,0:T(1,128)} %param.10) | copy-start | bytes 1732
  3.4 36.6 %all-to-all-start = ((f32[16,128,256]{2,1,0:T(8,128)}), f32[16,128,256]{2,1,0:T(8,128)S(1)}, u32[]{:S(2)}, u32[]{:S(2)}) async-start(f32[16,128,256]{2,1,0:T(8,128)} %broadcast_in_dim.28), calls=%async_computation | async-start | bytes 4194304 | tf_op jit(solution)/shard_map/all_to_all | solution.py:93
  39.9 1.3 copy-start
  223.1 36.2 %copy-start.1 = (f32[4,1,1,128,128]{4,3,2,1,0:T(8,128)S(1)}, f32[4,1,1,128,128]{4,3,2,1,0:T(8,128)}, u32[]{:S(2)}) copy-start(f32[4,1,1,128,128]{4,3,2,1,0:T(8,128)} %param.7) | copy-start | bytes 786436
  341.2 1.0 copy-start.2
  477.8 33.7 %all-to-all-start.17 = ((f32[16,128,256]{2,1,0:T(8,128)}), f32[16,128,256]{2,1,0:T(8,128)S(1)}, u32[]{:S(2)}, u32[]{:S(2)}) async-start(f32[16,128,256]{2,1,0:T(8,128)} %shard_map.82), calls=%async_computation.17 | async-start | bytes 4194304 | tf_op jit(solution)/shard_map/all_to_all | solution.py:97

commit v4 on v3

--- a/solution.py
+++ b/solution.py
@@ -10,6 +10,7 @@
 from jax.sharding import PartitionSpec as P
 
 GROUP = 8
+CHUNKS = 2
 
 
 def apply_inverse(inverse, values):
@@ -37,7 +38,8 @@
             split_ref[source] = jnp.concatenate([high, low, high], axis=0)
 
     filled = filled_ref[0]
-    for g in range(group):
+
+    def one_block(g, carry):
         b = step * group + g
 
         @pl.when(b < filled)
@@ -52,6 +54,10 @@
                 stacked = jnp.concatenate([high, high, low], axis=1)
                 product = jnp.dot(stacked, values, preferred_element_type=jnp.float32)
             out_ref[placed_ref[b]] += product
+
+        return carry
+
+    lax.fori_loop(0, group, one_block, 0)
 
 
 def block_terms_kernel(tile_stack, picked, placed, filled, operand, count, transposed):
@@ -119,15 +125,9 @@
     return scatter_sum(chip_sums, "chip")
 
 
-def per_device(rhs, diag_inverse, update_blocks, source_slot, target_slot, block_count):
-    levels = rhs.shape[0]
+def solve_columns(rhs_local, inverse_local, tiles_local, sources_local, targets_local, filled_local):
+    levels = rhs_local.shape[0]
     last_level = levels - 1
-    rhs_local = rhs[:, 0, 0]
-    inverse_local = diag_inverse[:, 0, 0]
-    tiles_local = update_blocks[:, 0, 0]
-    sources_local = source_slot[:, 0, 0]
-    targets_local = target_slot[:, 0, 0]
-    filled_local = block_count[:, 0, 0]
     row_count = lax.axis_size("row")
     col_count = lax.axis_size("chip") * lax.axis_size("core")
     block_shape = rhs_local.shape[1:]
@@ -165,8 +165,19 @@
         )
         reduced = scatter_sum(totals, "row")
         backward.insert(0, apply_transposed(inverse_local[level_index], solved - reduced))
-    forward_out = jnp.stack(forward)[:, None, None]
-    backward_out = jnp.stack(backward)[:, None, None]
+    return jnp.stack(forward), jnp.stack(backward)
+
+
+def per_device(rhs, diag_inverse, update_blocks, source_slot, target_slot, block_count):
+    rhs_local = rhs[:, 0, 0]
+    shared = (diag_inverse[:, 0, 0], update_blocks[:, 0, 0], source_slot[:, 0, 0], target_slot[:, 0, 0],
+              block_count[:, 0, 0])
+    width = rhs_local.shape[-1]
+    chunks = CHUNKS if width % (CHUNKS * 128) == 0 else 1
+    step = width // chunks
+    results = [solve_columns(rhs_local[..., k * step:(k + 1) * step], *shared) for k in range(chunks)]
+    forward_out = jnp.concatenate([r[0] for r in results], axis=-1)[:, None, None]
+    backward_out = jnp.concatenate([r[1] for r in results], axis=-1)[:, None, None]
     return (forward_out, backward_out)
 
 

time: 517 us -> 630 us (1.22)
  blocking collectives: 384 us -> 32.3 us
  waiting for transfers between devices: 46.1 us -> 322 us
  starting transfers between devices: 13.7 us -> 156 us
  Pallas kernels: 44 us -> 80.9 us
  local copies, waits for them, and re-layouts: 14.7 us -> 24.3 us
    all_to_all x13 -> x0, blocking collectives: 365 us -> none  [the longest x5 179 us: scatter_sum(): return lax.all_to_all(parts, axis, 0, 0, tiled=True).sum(axis=0)]
    all_to_all x1 -> x12, waiting for transfers between devices: 26.6 us -> 174 us  [scatter_sum(): return lax.all_to_all(parts, axis, 0, 0, tiled=True).sum(axis=0)]
    all_to_all x1 -> x12, waiting for transfers between devices: 19.6 us -> 144 us  [gather_blocks(): return lax.all_to_all(stacked, axis, 0, 0, tiled=True)]
    all_to_all x1 -> x12, starting transfers between devices: 6.16 us -> 70.5 us  [scatter_sum(): return lax.all_to_all(parts, axis, 0, 0, tiled=True).sum(axis=0)]
    all_to_all x1 -> x12, starting transfers between devices: 7.52 us -> 64.1 us  [gather_blocks(): return lax.all_to_all(stacked, axis, 0, 0, tiled=True)]
    pallas_call x6 -> x12, Pallas kernels: 44 us -> 80.9 us  [block_terms_kernel(): pl.pallas_call(functools.partial(_terms_kernel, transposed, group), grid_...]
    all_to_all x0 -> x6, starting transfers between devices: none -> 21.5 us  [scatter_columns(): chip_sums = lax.all_to_all(by_core, 'core', 0, 0, tiled=True).sum(axis=0)]
    all_to_all x3 -> x6, blocking collectives: 18.9 us -> 32.3 us  [gather_columns(): both = lax.all_to_all(stacked, 'core', 0, 0, tiled=True)]
  transfers between devices with their start and end apart: 2 -> 30, of which waited for: 2 -> 26; matrix products, arithmetic and copies ran while one was open for 2% -> 3% of each run, Pallas kernels for 0% -> 13%
where the time goes in v4:
time: 630 us; the launch traced here: 629 us
  waiting for transfers between devices  322 us (51%)
  starting transfers between devices  156 us (25%)
  Pallas kernels  80.9 us (13%)
  blocking collectives  32.3 us (5%)
  local copies, waits for them, and re-layouts  24.3 us (4%)
  other arithmetic  8.03 us (1%)
    all_to_all x12, waiting for transfers between devices, scatter_sum(): return lax.all_to_all(parts, axis, 0, 0, tiled=True).sum(axis=0)  174 us
    all_to_all x12, waiting for transfers between devices, gather_blocks(): return lax.all_to_all(stacked, axis, 0, 0, tiled=True)  144 us
    pallas_call x12, Pallas kernels, block_terms_kernel(): pl.pallas_call(functools.partial(_terms_kernel, transposed, group), grid_...  80.9 us
    all_to_all x12, starting transfers between devices, scatter_sum(): return lax.all_to_all(parts, axis, 0, 0, tiled=True).sum(axis=0)  70.5 us
    all_to_all x12, starting transfers between devices, gather_blocks(): return lax.all_to_all(stacked, axis, 0, 0, tiled=True)  64.1 us
    all_to_all x6, blocking collectives, gather_columns(): both = lax.all_to_all(stacked, 'core', 0, 0, tiled=True)  32.3 us
    all_to_all x6, starting transfers between devices, scatter_columns(): chip_sums = lax.all_to_all(by_core, 'core', 0, 0, tiled=True).sum(axis=0)  21.5 us
  transfers between devices with their start and end apart: 30, of which 26 were waited for; matrix products, arithmetic and copies ran while one was open for 3% of the time, Pallas kernels for 13%

profile of v4, /device:TPU:8, one launch (start us, length us, event | category | flops | bytes accessed | tf_op | source)
XLA Modules:
  0.0 629.3 jit_solution(10466416593063305579)
XLA Ops:
  3.1 7.4 %all-to-all-start = ((f32[16,128,128]{2,1,0:T(8,128)}), f32[16,128,128]{2,1,0:T(8,128)S(1)}, u32[]{:S(2)}, u32[]{:S(2)}) async-start(f32[16,128,128]{2,1,0:T(8,128)} %broadcast_in_dim.52), calls=%async_computation | async-start | bytes 2097152 | tf_op jit(solution)/shard_map/all_to_all | solution.py:99
  11.6 15.3 %all-to-all-done.operand_ref = f32[16,128,128]{2,1,0:T(8,128)S(1)} async-done(((f32[16,128,128]{2,1,0:T(8,128)}), f32[16,128,128]{2,1,0:T(8,128)S(1)}, u32[]{:S(2)}, u32[]{:S(2)}) %all-to-all-start) | async-done | bytes 1048608 | tf_op jit(solution)/shard_map/all_to_all | solution.py:99
  28.1 4.9 all-to-all-start.9
  34.1 7.7 %slice_bitcast_fusion.2 = (f32[48,128,128]{2,1,0:T(8,128)}, f32[48,128,128]{2,1,0:T(8,128)}, f32[48,128,128]{2,1,0:T(8,128)}) fusion(f32[3,1,1,48,128,128]{5,4,3,2,1,0:T(8,128)} %param.8), kind=kLoop, calls=%fused_computation.2 | loop fusion | bytes 18874368 | tf_op jit(solution)/shard_map/squeeze | solution.py:140
  41.8 7.2 %shard_map.77 = f32[16,128,128]{2,1,0:T(8,128)} custom-call(s32[48]{0:T(128)} %get-tuple-element.14.picked_ref.placed_ref, s32[48]{0:T(128)} %get-tuple-element.11.placed_ref.picked_ref, s32[1]{0:T(128)} %bitcast.6.filled_ref, f32[48,128,128]{2,1,0:T(8,128)} %get-tuple-element.8.tiles_ref, f32[16,128,128]{2,1,0:T(8,128)} %copy-done.1), custom_call_target="tpu_custom_call" | custom-call | flops 201326592 | bytes 5242880 | tf_op jit(solution)/shard_map/pallas_call | solution.py:84
  49.1 3.6 all-to-all-start.1
  52.7 7.2 %shard_map.80 = f32[16,128,128]{2,1,0:T(8,128)} custom-call(s32[48]{0:T(128)} %get-tuple-element.14.picked_ref.placed_ref, s32[48]{0:T(128)} %get-tuple-element.11.placed_ref.picked_ref, s32[1]{0:T(128)} %bitcast.6.filled_ref, f32[48,128,128]{2,1,0:T(8,128)} %get-tuple-element.8.tiles_ref, f32[16,128,128]{2,1,0:T(8,128)} %copy-done.2), custom_call_target="tpu_custom_call" | custom-call | flops 201326592 | bytes 5242880 | tf_op jit(solution)/shard_map/pallas_call | solution.py:84
  59.9 3.6 all-to-all-start.10
  65.6 15.2 %all-to-all-start.2 = ((f32[8,128,128]{2,1,0:T(8,128)}), f32[8,128,128]{2,1,0:T(8,128)S(1)}, u32[]{:S(2)}, u32[]{:S(2)}) async-start(f32[8,128,128]{2,1,0:T(8,128)} %reduce_sum.174), calls=%async_computation.2 | async-start | bytes 1048576 | tf_op jit(solution)/shard_map/all_to_all | solution.py:103
  81.7 16.9 %all-to-all-done.2 = f32[8,128,128]{2,1,0:T(8,128)S(1)} async-done(((f32[8,128,128]{2,1,0:T(8,128)}), f32[8,128,128]{2,1,0:T(8,128)S(1)}, u32[]{:S(2)}, u32[]{:S(2)}) %all-to-all-start.2) | async-done | bytes 524320 | tf_op jit(solution)/shard_map/all_to_all | solution.py:103
  102.5 17.4 %all-to-all-done.11 = f32[8,128,128]{2,1,0:T(8,128)S(1)} async-done(((f32[8,128,128]{2,1,0:T(8,128)}), f32[8,128,128]{2,1,0:T(8,128)S(1)}, u32[]{:S(2)}, u32[]{:S(2)}) %all-to-all-start.11) | async-done | bytes 524320 | tf_op jit(solution)/shard_map/all_to_all | solution.py:103
  121.1 11.0 %all-to-all-start.3 = ((f32[16,128,128]{2,1,0:T(8,128)}), f32[16,128,128]{2,1,0:T(8,128)S(1)}, u32[]{:S(2)}, u32[]{:S(2)}) async-start(f32[16,128,128]{2,1,0:T(8,128)} %broadcast_in_dim.53), calls=%async_computation.3 | async-start | bytes 2097152 | tf_op jit(solution)/shard_map/all_to_all | solution.py:99
  132.5 16.2 %all-to-all-done.3.operand_ref = f32[16,128,128]{2,1,0:T(8,128)S(1)} async-done(((f32[16,128,128]{2,1,0:T(8,128)}), f32[16,128,128]{2,1,0:T(8,128)S(1)}, u32[]{:S(2)}, u32[]{:S(2)}) %all-to-all-start.3) | async-done | bytes 1048608 | tf_op jit(solution)/shard_map/all_to_all | solution.py:99
  149.9 4.9 all-to-all-start.12
  154.8 5.0 shard_map.78
  159.7 9.4 %all-to-all-done.12.operand_ref = f32[16,128,128]{2,1,0:T(8,128)S(1)} async-done(((f32[16,128,128]{2,1,0:T(8,128)}), f32[16,128,128]{2,1,0:T(8,128)S(1)}, u32[]{:S(2)}, u32[]{:S(2)}) %all-to-all-start.12) | async-done | bytes 1048608 | tf_op jit(solution)/shard_map/all_to_all | solution.py:99
  169.1 3.6 all-to-all-start.4
  172.7 5.0 shard_map.81
  177.7 3.6 all-to-all-start.13
  183.7 6.0 all-to-all-start.5
  190.6 16.9 %all-to-all-done.5 = f32[8,128,128]{2,1,0:T(8,128)S(1)} async-done(((f32[8,128,128]{2,1,0:T(8,128)}), f32[8,128,128]{2,1,0:T(8,128)S(1)}, u32[]{:S(2)}, u32[]{:S(2)}) %all-to-all-start.5) | async-done | bytes 524320 | tf_op jit(solution)/shard_map/all_to_all | solution.py:103
  207.5 3.5 all-to-all-start.14
  211.5 17.4 %all-to-all-done.14 = f32[8,128,128]{2,1,0:T(8,128)S(1)} async-done(((f32[8,128,128]{2,1,0:T(8,128)}), f32[8,128,128]{2,1,0:T(8,128)S(1)}, u32[]{:S(2)}, u32[]{:S(2)}) %all-to-all-start.14) | async-done | bytes 524320 | tf_op jit(solution)/shard_map/all_to_all | solution.py:103
  230.0 9.9 %all-to-all-start.6 = ((f32[16,128,128]{2,1,0:T(8,128)}), f32[16,128,128]{2,1,0:T(8,128)S(1)}, u32[]{:S(2)}, u32[]{:S(2)}) async-start(f32[16,128,128]{2,1,0:T(8,128)} %broadcast_in_dim.54), calls=%async_computation.6 | async-start | bytes 2097152 | tf_op jit(solution)/shard_map/all_to_all | solution.py:99
  240.3 16.2 %all-to-all-done.6.operand_ref = f32[16,128,128]{2,1,0:T(8,128)S(1)} async-done(((f32[16,128,128]{2,1,0:T(8,128)}), f32[16,128,128]{2,1,0:T(8,128)S(1)}, u32[]{:S(2)}, u32[]{:S(2)}) %all-to-all-start.6) | async-done | bytes 1048608 | tf_op jit(solution)/shard_map/all_to_all | solution.py:99
  257.7 4.9 all-to-all-start.15
  262.6 7.4 %shard_map.79 = f32[16,128,128]{2,1,0:T(8,128)} custom-call(s32[48]{0:T(128)} %get-tuple-element.15.picked_ref.placed_ref, s32[48]{0:T(128)} %get-tuple-element.12.placed_ref.picked_ref, s32[1]{0:T(128)} %bitcast.26.filled_ref, f32[48,128,128]{2,1,0:T(8,128)} %get-tuple-element.9.tiles_ref, f32[16,128,128]{2,1,0:T(8,128)} %copy-done.3), custom_call_target="tpu_custom_call" | custom-call | flops 201326592 | bytes 5242880 | tf_op jit(solution)/shard_map/pallas_call | solution.py:84
  270.0 6.9 %all-to-all-done.15.operand_ref = f32[16,128,128]{2,1,0:T(8,128)S(1)} async-done(((f32[16,128,128]{2,1,0:T(8,128)}), f32[16,128,128]{2,1,0:T(8,128)S(1)}, u32[]{:S(2)}, u32[]{:S(2)}) %all-to-all-start.15) | async-done | bytes 1048608 | tf_op jit(solution)/shard_map/all_to_all | solution.py:99
  276.9 3.6 all-to-all-start.7
  280.5 7.4 %shard_map.82 = f32[16,128,128]{2,1,0:T(8,128)} custom-call(s32[48]{0:T(128)} %get-tuple-element.15.picked_ref.placed_ref, s32[48]{0:T(128)} %get-tuple-element.12.placed_ref.picked_ref, s32[1]{0:T(128)} %bitcast.26.filled_ref, f32[48,128,128]{2,1,0:T(8,128)} %get-tuple-element.9.tiles_ref, f32[16,128,128]{2,1,0:T(8,128)} %copy-done.5), custom_call_target="tpu_custom_call" | custom-call | flops 201326592 | bytes 5242880 | tf_op jit(solution)/shard_map/pallas_call | solution.py:84
  288.0 3.6 all-to-all-start.16
  298.0 17.1 %all-to-all-done.8 = f32[8,128,128]{2,1,0:T(8,128)S(1)} async-done(((f32[8,128,128]{2,1,0:T(8,128)}), f32[8,128,128]{2,1,0:T(8,128)S(1)}, u32[]{:S(2)}, u32[]{:S(2)}) %all-to-all-start.8) | async-done | bytes 524320 | tf_op jit(solution)/shard_map/all_to_all | solution.py:103
  319.3 17.2 %all-to-all-done.17 = f32[8,128,128]{2,1,0:T(8,128)S(1)} async-done(((f32[8,128,128]{2,1,0:T(8,128)}), f32[8,128,128]{2,1,0:T(8,128)S(1)}, u32[]{:S(2)}, u32[]{:S(2)}) %all-to-all-start.17) | async-done | bytes 524320 | tf_op jit(solution)/shard_map/all_to_all | solution.py:103
  341.5 17.2 %all-to-all-done.18 = f32[8,128,128]{2,1,0:T(8,128)S(1)} async-done(((f32[8,128,128]{2,1,0:T(8,128)}), f32[8,128,128]{2,1,0:T(8,128)S(1)}, u32[]{:S(2)}, u32[]{:S(2)}) %all-to-all-start.18) | async-done | bytes 524320 | tf_op jit(solution)/shard_map/all_to_all | solution.py:99
  358.8 5.4 all_to_all.180
  368.5 8.0 %shard_map.83 = f32[16,128,128]{2,1,0:T(8,128)} custom-call(s32[48]{0:T(128)} %get-tuple-element.12.placed_ref.picked_ref, s32[48]{0:T(128)} %get-tuple-element.15.picked_ref.placed_ref, s32[1]{0:T(128)} %bitcast.26.filled_ref, f32[48,128,128]{2,1,0:T(8,128)} %get-tuple-element.9.tiles_ref, f32[16,128,128]{2,1,0:T(8,128)} %bitcast.240), custom_call_target="tpu_custom_call" | custom-call | flops 201326592 | bytes 5242880 | tf_op jit(solution)/shard_map/pallas_call | solution.py:84
  376.6 10.0 %all-to-all-done.27 = f32[8,128,128]{2,1,0:T(8,128)S(1)} async-done(((f32[8,128,128]{2,1,0:T(8,128)}), f32[8,128,128]{2,1,0:T(8,128)S(1)}, u32[]{:S(2)}, u32[]{:S(2)}) %all-to-all-start.27) | async-done | bytes 524320 | tf_op jit(solution)/shard_map/all_to_all | solution.py:99
  386.6 5.4 all_to_all.181
  392.0 8.1 %all-to-all-start.20 = ((f32[16,128,128]{2,1,0:T(8,128)}), f32[16,128,128]{2,1,0:T(8,128)S(1)}, u32[]{:S(2)}, u32[]{:S(2)}) async-start(f32[16,128,128]{2,1,0:T(8,128)} %shard_map.83), calls=%async_computation.20 | async-start | bytes 2097152 | tf_op jit(solution)/shard_map/all_to_all | solution.py:103
  400.1 8.0 %shard_map.86 = f32[16,128,128]{2,1,0:T(8,128)} custom-call(s32[48]{0:T(128)} %get-tuple-element.12.placed_ref.picked_ref, s32[48]{0:T(128)} %get-tuple-element.15.picked_ref.placed_ref, s32[1]{0:T(128)} %bitcast.26.filled_ref, f32[48,128,128]{2,1,0:T(8,128)} %get-tuple-element.9.tiles_ref, f32[16,128,128]{2,1,0:T(8,128)} %bitcast.237), custom_call_target="tpu_custom_call" | custom-call | flops 201326592 | bytes 5242880 | tf_op jit(solution)/shard_map/pallas_call | solution.py:84
  408.1 8.7 %all-to-all-done.20 = f32[16,128,128]{2,1,0:T(8,128)S(1)} async-done(((f32[16,128,128]{2,1,0:T(8,128)}), f32[16,128,128]{2,1,0:T(8,128)S(1)}, u32[]{:S(2)}, u32[]{:S(2)}) %all-to-all-start.20) | async-done | bytes 1048608 | tf_op jit(solution)/shard_map/all_to_all | solution.py:103
  416.9 4.9 all-to-all-start.29
  422.3 14.1 %all-to-all-done.29 = f32[16,128,128]{2,1,0:T(8,128)S(1)} async-done(((f32[16,128,128]{2,1,0:T(8,128)}), f32[16,128,128]{2,1,0:T(8,128)S(1)}, u32[]{:S(2)}, u32[]{:S(2)}) %all-to-all-start.29) | async-done | bytes 1048608 | tf_op jit(solution)/shard_map/all_to_all | solution.py:103
  441.2 14.7 %all-to-all-done.21 = f32[8,128,128]{2,1,0:T(8,128)S(1)} async-done(((f32[8,128,128]{2,1,0:T(8,128)}), f32[8,128,128]{2,1,0:T(8,128)S(1)}, u32[]{:S(2)}, u32[]{:S(2)}) %all-to-all-start.21) | async-done | bytes 524320 | tf_op jit(solution)/shard_map/all_to_all | solution.py:99
  456.0 5.4 all_to_all.182
  462.2 3.7 all-to-all-start.30
  465.8 5.0 shard_map.84
  470.9 13.0 %all-to-all-done.30 = f32[8,128,128]{2,1,0:T(8,128)S(1)} async-done(((f32[8,128,128]{2,1,0:T(8,128)}), f32[8,128,128]{2,1,0:T(8,128)S(1)}, u32[]{:S(2)}, u32[]{:S(2)}) %all-to-all-start.30) | async-done | bytes 524320 | tf_op jit(solution)/shard_map/all_to_all | solution.py:99
  483.9 5.4 all_to_all.183
  489.4 6.2 all-to-all-start.23
  495.6 5.1 shard_map.87
  500.7 11.6 %all-to-all-done.23 = f32[16,128,128]{2,1,0:T(8,128)S(1)} async-done(((f32[16,128,128]{2,1,0:T(8,128)}), f32[16,128,128]{2,1,0:T(8,128)S(1)}, u32[]{:S(2)}, u32[]{:S(2)}) %all-to-all-start.23) | async-done | bytes 1048608 | tf_op jit(solution)/shard_map/all_to_all | solution.py:103
  512.3 4.9 all-to-all-start.32
  517.7 14.1 %all-to-all-done.32 = f32[16,128,128]{2,1,0:T(8,128)S(1)} async-done(((f32[16,128,128]{2,1,0:T(8,128)}), f32[16,128,128]{2,1,0:T(8,128)S(1)}, u32[]{:S(2)}, u32[]{:S(2)}) %all-to-all-start.32) | async-done | bytes 1048608 | tf_op jit(solution)/shard_map/all_to_all | solution.py:103
  536.6 14.7 %all-to-all-done.24 = f32[8,128,128]{2,1,0:T(8,128)S(1)} async-done(((f32[8,128,128]{2,1,0:T(8,128)}), f32[8,128,128]{2,1,0:T(8,128)S(1)}, u32[]{:S(2)}, u32[]{:S(2)}) %all-to-all-start.24) | async-done | bytes 524320 | tf_op jit(solution)/shard_map/all_to_all | solution.py:99
  551.4 5.4 all_to_all.184
  561.1 7.7 %shard_map.85 = f32[16,128,128]{2,1,0:T(8,128)} custom-call(s32[48]{0:T(128)} %get-tuple-element.11.placed_ref.picked_ref, s32[48]{0:T(128)} %get-tuple-element.14.picked_ref.placed_ref, s32[1]{0:T(128)} %bitcast.6.filled_ref, f32[48,128,128]{2,1,0:T(8,128)} %get-tuple-element.8.tiles_ref, f32[16,128,128]{2,1,0:T(8,128)} %bitcast.242), custom_call_target="tpu_custom_call" | custom-call | flops 201326592 | bytes 5242880 | tf_op jit(solution)/shard_map/pallas_call | solution.py:84
  568.8 10.2 %all-to-all-done.33 = f32[8,128,128]{2,1,0:T(8,128)S(1)} async-done(((f32[8,128,128]{2,1,0:T(8,128)}), f32[8,128,128]{2,1,0:T(8,128)S(1)}, u32[]{:S(2)}, u32[]{:S(2)}) %all-to-all-start.33) | async-done | bytes 524320 | tf_op jit(solution)/shard_map/all_to_all | solution.py:99
  579.2 5.4 all_to_all.185
  584.6 6.2 all-to-all-start.26
  590.7 7.8 %shard_map.88 = f32[16,128,128]{2,1,0:T(8,128)} custom-call(s32[48]{0:T(128)} %get-tuple-element.11.placed_ref.picked_ref, s32[48]{0:T(128)} %get-tuple-element.14.picked_ref.placed_ref, s32[1]{0:T(128)} %bitcast.6.filled_ref, f32[48,128,128]{2,1,0:T(8,128)} %get-tuple-element.8.tiles_ref, f32[16,128,128]{2,1,0:T(8,128)} %bitcast.239), custom_call_target="tpu_custom_call" | custom-call | flops 201326592 | bytes 5242880 | tf_op jit(solution)/shard_map/pallas_call | solution.py:84
  598.5 9.0 %all-to-all-done.26 = f32[16,128,128]{2,1,0:T(8,128)S(1)} async-done(((f32[16,128,128]{2,1,0:T(8,128)}), f32[16,128,128]{2,1,0:T(8,128)S(1)}, u32[]{:S(2)}, u32[]{:S(2)}) %all-to-all-start.26) | async-done | bytes 1048608 | tf_op jit(solution)/shard_map/all_to_all | solution.py:103
  607.5 4.9 all-to-all-start.35
  613.8 13.2 %all-to-all-done.35 = f32[16,128,128]{2,1,0:T(8,128)S(1)} async-done(((f32[16,128,128]{2,1,0:T(8,128)}), f32[16,128,128]{2,1,0:T(8,128)S(1)}, u32[]{:S(2)}, u32[]{:S(2)}) %all-to-all-start.35) | async-done | bytes 1048608 | tf_op jit(solution)/shard_map/all_to_all | solution.py:103
  (122 shorter events, 61.4 us)
Async XLA Ops:
  0.6 9.9 %copy-start.11 = (f32[4,1,1,128,256]{4,3,2,1,0:T(8,128)S(1)}, f32[4,1,1,128,256]{4,3,2,1,0:T(8,128)}, u32[]{:S(2)}) copy-start(f32[4,1,1,128,256]{4,3,2,1,0:T(8,128)} %param.6) | copy-start | bytes 1572868
  0.6 9.9 %copy-start = (f32[4,1,1,128,128]{4,3,2,1,0:T(8,128)S(1)}, f32[4,1,1,128,128]{4,3,2,1,0:T(8,128)}, u32[]{:S(2)}) copy-start(f32[4,1,1,128,128]{4,3,2,1,0:T(8,128)} %param.7) | copy-start | bytes 786436
  0.6 10.3 %copy-start.12 = (s32[3,1,1]{0,2,1:T(1,128)S(1)}, s32[3,1,1]{0,2,1:T(1,128)}, u32[]{:S(2)}) copy-start(s32[3,1,1]{0,2,1:T(1,128)} %param.11) | copy-start | bytes 40
  2.0 31.0 %copy-start.13 = (s32[3,1,1,48]{3,2,1,0:T(1,128)S(1)}, s32[3,1,1,48]{3,2,1,0:T(1,128)}, u32[]{:S(2)}) copy-start(s32[3,1,1,48]{3,2,1,0:T(1,128)} %param.10) | copy-start | bytes 1732
  2.0 31.5 %copy-start.14 = (s32[3,1,1,48]{3,2,1,0:T(1,128)S(1)}, s32[3,1,1,48]{3,2,1,0:T(1,128)}, u32[]{:S(2)}) copy-start(s32[3,1,1,48]{3,2,1,0:T(1,128)} %param.9) | copy-start | bytes 1732
  3.1 23.8 %all-to-all-start = ((f32[16,128,128]{2,1,0:T(8,128)}), f32[16,128,128]{2,1,0:T(8,128)S(1)}, u32[]{:S(2)}, u32[]{:S(2)}) async-start(f32[16,128,128]{2,1,0:T(8,128)} %broadcast_in_dim.52), calls=%async_computation | async-start | bytes 2097152 | tf_op jit(solution)/shard_map/all_to_all | solution.py:99
  26.9 14.9 %copy-start.1 = (f32[16,128,128]{2,1,0:T(8,128)}, f32[16,128,128]{2,1,0:T(8,128)S(1)}, u32[]{:S(2)}) copy-start(f32[16,128,128]{2,1,0:T(8,128)S(1)} %all-to-all-done.operand_ref) | copy-start | bytes 3145732
  28.1 21.0 %all-to-all-start.9 = ((f32[16,128,128]{2,1,0:T(8,128)}), f32[16,128,128]{2,1,0:T(8,128)S(1)}, u32[]{:S(2)}, u32[]{:S(2)}) async-start(f32[16,128,128]{2,1,0:T(8,128)} %broadcast_in_dim.55), calls=%async_computation.9 | async-start | bytes 2097152 | tf_op jit(solution)/shard_map/all_to_all | solution.py:99
  49.1 3.6 copy-start.2
  49.1 10.8 %all-to-all-start.1 = ((f32[2,8,128,128]{3,2,1,0:T(8,128)}), f32[2,8,128,128]{3,2,1,0:T(8,128)S(1)}, u32[]{:S(2)}, u32[]{:S(2)}) async-start(f32[2,8,128,128]{3,2,1,0:T(8,128)} %bitcast.231), calls=%async_computation.1 | async-start | bytes 2097152 | tf_op jit(solution)/shard_map/all_to_all | solution.py:124
  59.9 5.7 all-to-all-start.10
  65.6 33.0 %all-to-all-start.2 = ((f32[8,128,128]{2,1,0:T(8,128)}), f32[8,128,128]{2,1,0:T(8,128)S(1)}, u32[]{:S(2)}, u32[]{:S(2)}) async-start(f32[8,128,128]{2,1,0:T(8,128)} %reduce_sum.174), calls=%async_computation.2 | async-start | bytes 1048576 | tf_op jit(solution)/shard_map/all_to_all | solution.py:103
  98.6 21.4 %all-to-all-start.11 = ((f32[8,128,128]{2,1,0:T(8,128)}), f32[8,128,128]{2,1,0:T(8,128)S(1)}, u32[]{:S(2)}, u32[]{:S(2)}) async-start(f32[8,128,128]{2,1,0:T(8,128)} %reduce_sum.183), calls=%async_computation.11 | async-start | bytes 1048576 | tf_op jit(solution)/shard_map/all_to_all | solution.py:103
  121.1 27.6 %all-to-all-start.3 = ((f32[16,128,128]{2,1,0:T(8,128)}), f32[16,128,128]{2,1,0:T(8,128)S(1)}, u32[]{:S(2)}, u32[]{:S(2)}) async-start(f32[16,128,128]{2,1,0:T(8,128)} %broadcast_in_dim.53), calls=%async_computation.3 | async-start | bytes 2097152 | tf_op jit(solution)/shard_map/all_to_all | solution.py:99
  148.7 6.1 copy-start.4
  149.9 19.3 %all-to-all-start.12 = ((f32[16,128,128]{2,1,0:T(8,128)}), f32[16,128,128]{2,1,0:T(8,128)S(1)}, u32[]{:S(2)}, u32[]{:S(2)}) async-start(f32[16,128,128]{2,1,0:T(8,128)} %broadcast_in_dim.56), calls=%async_computation.12 | async-start | bytes 2097152 | tf_op jit(solution)/shard_map/all_to_all | solution.py:99
  169.1 3.6 copy-start.6
  169.1 8.6 %all-to-all-start.4 = ((f32[2,8,128,128]{3,2,1,0:T(8,128)}), f32[2,8,128,128]{3,2,1,0:T(8,128)S(1)}, u32[]{:S(2)}, u32[]{:S(2)}) async-start(f32[2,8,128,128]{3,2,1,0:T(8,128)} %bitcast.233), calls=%async_computation.4 | async-start | bytes 2097152 | tf_op jit(solution)/shard_map/all_to_all | solution.py:124
  177.7 6.0 all-to-all-start.13
  183.7 23.8 %all-to-all-start.5 = ((f32[8,128,128]{2,1,0:T(8,128)}), f32[8,128,128]{2,1,0:T(8,128)S(1)}, u32[]{:S(2)}, u32[]{:S(2)}) async-start(f32[8,128,128]{2,1,0:T(8,128)} %reduce_sum.177), calls=%async_computation.5 | async-start | bytes 1048576 | tf_op jit(solution)/shard_map/all_to_all | solution.py:103
  207.5 21.4 %all-to-all-start.14 = ((f32[8,128,128]{2,1,0:T(8,128)}), f32[8,128,128]{2,1,0:T(8,128)S(1)}, u32[]{:S(2)}, u32[]{:S(2)}) async-start(f32[8,128,128]{2,1,0:T(8,128)} %reduce_sum.186), calls=%async_computation.14 | async-start | bytes 1048576 | tf_op jit(solution)/shard_map/all_to_all | solution.py:103
  230.0 26.5 %all-to-all-start.6 = ((f32[16,128,128]{2,1,0:T(8,128)}), f32[16,128,128]{2,1,0:T(8,128)S(1)}, u32[]{:S(2)}, u32[]{:S(2)}) async-start(f32[16,128,128]{2,1,0:T(8,128)} %broadcast_in_dim.54), calls=%async_computation.6 | async-start | bytes 2097152 | tf_op jit(solution)/shard_map/all_to_all | solution.py:99
  256.5 6.1 copy-start.3
  257.7 19.3 %all-to-all-start.15 = ((f32[16,128,128]{2,1,0:T(8,128)}), f32[16,128,128]{2,1,0:T(8,128)S(1)}, u32[]{:S(2)}, u32[]{:S(2)}) async-start(f32[16,128,128]{2,1,0:T(8,128)} %broadcast_in_dim.57), calls=%async_computation.15 | async-start | bytes 2097152 | tf_op jit(solution)/shard_map/all_to_all | solution.py:99
  276.9 3.6 copy-start.5
  276.9 11.0 %all-to-all-start.7 = ((f32[2,8,128,128]{3,2,1,0:T(8,128)}), f32[2,8,128,128]{3,2,1,0:T(8,128)S(1)}, u32[]{:S(2)}, u32[]{:S(2)}) async-start(f32[2,8,128,128]{3,2,1,0:T(8,128)} %bitcast.235), calls=%async_computation.7 | async-start | bytes 2097152 | tf_op jit(solution)/shard_map/all_to_all | solution.py:124
  288.0 5.7 all-to-all-start.16
  293.6 21.5 %all-to-all-start.8 = ((f32[8,128,128]{2,1,0:T(8,128)}), f32[8,128,128]{2,1,0:T(8,128)S(1)}, u32[]{:S(2)}, u32[]{:S(2)}) async-start(f32[8,128,128]{2,1,0:T(8,128)} %reduce_sum.180), calls=%async_computation.8 | async-start | bytes 1048576 | tf_op jit(solution)/shard_map/all_to_all | solution.py:103
  315.1 21.4 %all-to-all-start.17 = ((f32[8,128,128]{2,1,0:T(8,128)}), f32[8,128,128]{2,1,0:T(8,128)S(1)}, u32[]{:S(2)}, u32[]{:S(2)}) async-start(f32[8,128,128]{2,1,0:T(8,128)} %reduce_sum.189), calls=%async_computation.17 | async-start | bytes 1048576 | tf_op jit(solution)/shard_map/all_to_all | solution.py:103
  337.4 21.4 %all-to-all-start.18 = ((f32[8,128,128]{2,1,0:T(8,128)}), f32[8,128,128]{2,1,0:T(8,128)S(1)}, u32[]{:S(2)}, u32[]{:S(2)}) async-start(f32[8,128,128]{2,1,0:T(8,128)} %broadcast_in_dim.59), calls=%async_computation.18 | async-start | bytes 1048576 | tf_op jit(solution)/shard_map/all_to_all | solution.py:99
  365.0 21.5 %all-to-all-start.27 = ((f32[8,128,128]{2,1,0:T(8,128)}), f32[8,128,128]{2,1,0:T(8,128)S(1)}, u32[]{:S(2)}, u32[]{:S(2)}) async-start(f32[8,128,128]{2,1,0:T(8,128)} %broadcast_in_dim.68), calls=%async_computation.27 | async-start | bytes 1048576 | tf_op jit(solution)/shard_map/all_to_all | solution.py:99
  392.0 24.9 %all-to-all-start.20 = ((f32[16,128,128]{2,1,0:T(8,128)}), f32[16,128,128]{2,1,0:T(8,128)S(1)}, u32[]{:S(2)}, u32[]{:S(2)}) async-start(f32[16,128,128]{2,1,0:T(8,128)} %shard_map.83), calls=%async_computation.20 | async-start | bytes 2097152 | tf_op jit(solution)/shard_map/all_to_all | solution.py:103
  416.9 19.5 %all-to-all-start.29 = ((f32[16,128,128]{2,1,0:T(8,128)}), f32[16,128,128]{2,1,0:T(8,128)S(1)}, u32[]{:S(2)}, u32[]{:S(2)}) async-start(f32[16,128,128]{2,1,0:T(8,128)} %shard_map.86), calls=%async_computation.29 | async-start | bytes 2097152 | tf_op jit(solution)/shard_map/all_to_all | solution.py:103
  422.1 15.0 %copy-start.7 = (f32[128,128]{1,0:T(8,128)}, f32[128,128]{1,0:T(8,128)S(1)}, u32[]{:S(2)}) copy-start(f32[128,128]{1,0:T(8,128)S(1)} %fusion.32) | copy-start | bytes 196612
  437.2 18.7 %all-to-all-start.21 = ((f32[8,128,128]{2,1,0:T(8,128)}), f32[8,128,128]{2,1,0:T(8,128)S(1)}, u32[]{:S(2)}, u32[]{:S(2)}) async-start(f32[8,128,128]{2,1,0:T(8,128)} %broadcast_in_dim.61), calls=%async_computation.21 | async-start | bytes 1048576 | tf_op jit(solution)/shard_map/all_to_all | solution.py:99
  441.1 21.1 %copy-start.8 = (f32[128,128]{1,0:T(8,128)}, f32[128,128]{1,0:T(8,128)S(1)}, u32[]{:S(2)}) copy-start(f32[128,128]{1,0:T(8,128)S(1)} %fusion.30) | copy-start | bytes 196612
  462.2 21.7 %all-to-all-start.30 = ((f32[8,128,128]{2,1,0:T(8,128)}), f32[8,128,128]{2,1,0:T(8,128)S(1)}, u32[]{:S(2)}, u32[]{:S(2)}) async-start(f32[8,128,128]{2,1,0:T(8,128)} %broadcast_in_dim.70), calls=%async_computation.30 | async-start | bytes 1048576 | tf_op jit(solution)/shard_map/all_to_all | solution.py:99
  489.4 22.9 %all-to-all-start.23 = ((f32[16,128,128]{2,1,0:T(8,128)}), f32[16,128,128]{2,1,0:T(8,128)S(1)}, u32[]{:S(2)}, u32[]{:S(2)}) async-start(f32[16,128,128]{2,1,0:T(8,128)} %shard_map.84), calls=%async_computation.23 | async-start | bytes 2097152 | tf_op jit(solution)/shard_map/all_to_all | solution.py:103
  512.3 19.5 %all-to-all-start.32 = ((f32[16,128,128]{2,1,0:T(8,128)}), f32[16,128,128]{2,1,0:T(8,128)S(1)}, u32[]{:S(2)}, u32[]{:S(2)}) async-start(f32[16,128,128]{2,1,0:T(8,128)} %shard_map.87), calls=%async_computation.32 | async-start | bytes 2097152 | tf_op jit(solution)/shard_map/all_to_all | solution.py:103
  517.6 15.0 %copy-start.9 = (f32[128,128]{1,0:T(8,128)}, f32[128,128]{1,0:T(8,128)S(1)}, u32[]{:S(2)}) copy-start(f32[128,128]{1,0:T(8,128)S(1)} %fusion.39) | copy-start | bytes 196612
  532.6 18.7 %all-to-all-start.24 = ((f32[8,128,128]{2,1,0:T(8,128)}), f32[8,128,128]{2,1,0:T(8,128)S(1)}, u32[]{:S(2)}, u32[]{:S(2)}) async-start(f32[8,128,128]{2,1,0:T(8,128)} %broadcast_in_dim.63), calls=%async_computation.24 | async-start | bytes 1048576 | tf_op jit(solution)/shard_map/all_to_all | solution.py:99
  536.5 21.1 %copy-start.10 = (f32[128,128]{1,0:T(8,128)}, f32[128,128]{1,0:T(8,128)S(1)}, u32[]{:S(2)}) copy-start(f32[128,128]{1,0:T(8,128)S(1)} %fusion.37) | copy-start | bytes 196612
  557.6 21.5 %all-to-all-start.33 = ((f32[8,128,128]{2,1,0:T(8,128)}), f32[8,128,128]{2,1,0:T(8,128)S(1)}, u32[]{:S(2)}, u32[]{:S(2)}) async-start(f32[8,128,128]{2,1,0:T(8,128)} %broadcast_in_dim.72), calls=%async_computation.33 | async-start | bytes 1048576 | tf_op jit(solution)/shard_map/all_to_all | solution.py:99
  584.6 22.9 %all-to-all-start.26 = ((f32[16,128,128]{2,1,0:T(8,128)}), f32[16,128,128]{2,1,0:T(8,128)S(1)}, u32[]{:S(2)}, u32[]{:S(2)}) async-start(f32[16,128,128]{2,1,0:T(8,128)} %shard_map.85), calls=%async_computation.26 | async-start | bytes 2097152 | tf_op jit(solution)/shard_map/all_to_all | solution.py:103
  607.5 19.5 %all-to-all-start.35 = ((f32[16,128,128]{2,1,0:T(8,128)}), f32[16,128,128]{2,1,0:T(8,128)S(1)}, u32[]{:S(2)}, u32[]{:S(2)}) async-start(f32[16,128,128]{2,1,0:T(8,128)} %shard_map.88), calls=%async_computation.35 | async-start | bytes 2097152 | tf_op jit(solution)/shard_map/all_to_all | solution.py:103

commit v5 on v3

--- a/solution.py
+++ b/solution.py
@@ -99,23 +99,22 @@
 
 def column_slot(position):
     cores = lax.axis_size("core")
-    return (position % cores) * lax.axis_size("chip") + position // cores
+    core_rel = (position % cores - lax.axis_index("core")) % cores
+    return core_rel * lax.axis_size("chip") + position // cores
 
 
 def gather_columns(block):
     chips = lax.axis_size("chip")
     cores = lax.axis_size("core")
     by_chip = gather_blocks(block, "chip", chips)
-    stacked = jnp.broadcast_to(by_chip[None], (cores,) + by_chip.shape)
-    both = lax.all_to_all(stacked, "core", 0, 0, tiled=True)
-    return both.reshape((cores * chips,) + block.shape)
+    other = lax.ppermute(by_chip, "core", [(j, (j + 1) % cores) for j in range(cores)])
+    return jnp.concatenate([by_chip, other], axis=0)
 
 
 def scatter_columns(parts):
     chips = lax.axis_size("chip")
     cores = lax.axis_size("core")
-    by_core = parts.reshape((cores, chips) + parts.shape[1:])
-    chip_sums = lax.all_to_all(by_core, "core", 0, 0, tiled=True).sum(axis=0)
+    chip_sums = parts[:chips] + lax.ppermute(parts[chips:], "core", [(j, (j + 1) % cores) for j in range(cores)])
     return scatter_sum(chip_sums, "chip")
 
 

time: 517 us -> 498 us (0.963)
  blocking collectives: 384 us -> 345 us
  waiting for transfers between devices: 46.1 us -> 62.8 us
  starting transfers between devices: 13.7 us -> 20.8 us
    all_to_all x6 -> x0, blocking collectives: 41 us -> none  [the longest x3 22.1 us: scatter_columns(): chip_sums = lax.all_to_all(by_core, 'core', 0, 0, tiled=True).sum(axis=0)]
    ppermute x0 -> x6, waiting for transfers between devices: none -> 15.8 us  [the longest x3 7.94 us: scatter_columns(): lax.ppermute(parts[chips:], 'core', [(j, (j + 1) % cores) for j in range(...]
    all_to_all x5, blocking collectives: 179 us -> 186 us  [scatter_sum(): return lax.all_to_all(parts, axis, 0, 0, tiled=True).sum(axis=0)]
    all_to_all x1, starting transfers between devices: 6.16 us -> 12.9 us  [scatter_sum(): return lax.all_to_all(parts, axis, 0, 0, tiled=True).sum(axis=0)]
    all_to_all x5, blocking collectives: 164 us -> 159 us  [gather_blocks(): return lax.all_to_all(stacked, axis, 0, 0, tiled=True)]
  transfers between devices with their start and end apart: 2 -> 8, of which waited for: 2 -> 8; matrix products, arithmetic and copies ran while one was open for 2% -> 2% of each run, Pallas kernels for 0% -> 0%
where the time goes in v5:
time: 498 us
  blocking collectives  345 us (69%)
  waiting for transfers between devices  62.8 us (13%)
  Pallas kernels  39.7 us (8%)
  starting transfers between devices  20.8 us (4%)
  local copies, waits for them, and re-layouts  17.6 us (4%)
  other arithmetic  7.69 us (2%)
    all_to_all x5, blocking collectives, scatter_sum(): return lax.all_to_all(parts, axis, 0, 0, tiled=True).sum(axis=0)  186 us
    all_to_all x5, blocking collectives, gather_blocks(): return lax.all_to_all(stacked, axis, 0, 0, tiled=True)  159 us
    pallas_call x6, Pallas kernels, block_terms_kernel(): pl.pallas_call(functools.partial(_terms_kernel, transposed, group), grid_...  39.7 us
    all_to_all x1, waiting for transfers between devices, scatter_sum(): return lax.all_to_all(parts, axis, 0, 0, tiled=True).sum(axis=0)  27.4 us
    all_to_all x1, waiting for transfers between devices, gather_blocks(): return lax.all_to_all(stacked, axis, 0, 0, tiled=True)  19.6 us
    all_to_all x1, starting transfers between devices, scatter_sum(): return lax.all_to_all(parts, axis, 0, 0, tiled=True).sum(axis=0)  12.9 us
  transfers between devices with their start and end apart: 8, of which 8 were waited for; matrix products, arithmetic and copies ran while one was open for 2% of the time, Pallas kernels for 0%

profile of v5, /device:TPU:8, one launch (start us, length us, event | category | flops | bytes accessed | tf_op | source)
XLA Modules:
  0.0 497.7 jit_solution(9954470336148143700)
XLA Ops:
  0.6 1.2 fusion.6
  1.8 1.5 broadcast_in_dim.22
  3.4 7.5 %all-to-all-start = ((f32[16,128,256]{2,1,0:T(8,128)}), f32[16,128,256]{2,1,0:T(8,128)S(1)}, u32[]{:S(2)}, u32[]{:S(2)}) async-start(f32[16,128,256]{2,1,0:T(8,128)} %broadcast_in_dim.22), calls=%async_computation | async-start | bytes 4194304 | tf_op jit(solution)/shard_map/all_to_all | solution.py:93
  10.9 0.6 fusion.51
  11.5 0.5 clamp_bitcast_fusion.2
  12.0 0.6 fusion.48
  12.6 7.7 %slice_bitcast_fusion.2 = (f32[48,128,128]{2,1,0:T(8,128)}, f32[48,128,128]{2,1,0:T(8,128)}, f32[48,128,128]{2,1,0:T(8,128)}) fusion(f32[3,1,1,48,128,128]{5,4,3,2,1,0:T(8,128)} %param.8), kind=kLoop, calls=%fused_computation.2 | loop fusion | bytes 18874368 | tf_op jit(solution)/shard_map/squeeze | solution.py:139
  20.3 19.6 %all-to-all-done.operand_ref = f32[16,128,256]{2,1,0:T(8,128)S(1)} async-done(((f32[16,128,256]{2,1,0:T(8,128)}), f32[16,128,256]{2,1,0:T(8,128)S(1)}, u32[]{:S(2)}, u32[]{:S(2)}) %all-to-all-start) | async-done | bytes 2097184 | tf_op jit(solution)/shard_map/all_to_all | solution.py:93
  39.9 1.3 copy-done.3
  41.2 5.9 %shard_map.77 = f32[16,128,256]{2,1,0:T(8,128)} custom-call(s32[48]{0:T(128)} %get-tuple-element.10.picked_ref.placed_ref, s32[48]{0:T(128)} %get-tuple-element.7.placed_ref.picked_ref, s32[1]{0:T(128)} %bitcast.5.filled_ref, f32[48,128,128]{2,1,0:T(8,128)} %get-tuple-element.4.tiles_ref, f32[16,128,256]{2,1,0:T(8,128)} %copy-done.3), custom_call_target="tpu_custom_call" | custom-call | flops 402653184 | bytes 7340032 | tf_op jit(solution)/shard_map/pallas_call | solution.py:78
  47.1 1.5 slice.150
  48.6 0.1 collective-permute-start
  48.7 2.6 collective-permute-done
  51.3 0.1 slice_add_fusion.2
  51.5 43.6 %all_to_all.60 = f32[8,128,256]{2,1,0:T(8,128)S(1)} all-to-all(f32[8,128,256]{2,1,0:T(8,128)S(1)} %slice_add_fusion.2), channel_id=1, replica_groups=mesh['row'=16,'chip'=8,'core'=2] {'chip'}, dimensions={0} | all-to-all | bytes 2097152 | tf_op jit(solution)/shard_map/all_to_all | solution.py:97
  95.2 0.3 fusion.4
  95.4 0.2 broadcast_in_dim.23
  95.7 29.1 %all_to_all.61.operand_ref = f32[16,128,256]{2,1,0:T(8,128)} all-to-all(f32[16,128,256]{2,1,0:T(8,128)S(1)} %broadcast_in_dim.23), channel_id=1, replica_groups=mesh['row'=16,'chip'=8,'core'=2] {'row'}, dimensions={0} | all-to-all | bytes 4194304 | tf_op jit(solution)/shard_map/all_to_all | solution.py:93
  124.8 8.1 %shard_map.78 = f32[16,128,256]{2,1,0:T(8,128)} custom-call(s32[48]{0:T(128)} %get-tuple-element.12.picked_ref.placed_ref, s32[48]{0:T(128)} %get-tuple-element.9.placed_ref.picked_ref, s32[1]{0:T(128)} %bitcast.14.filled_ref, f32[48,128,128]{2,1,0:T(8,128)} %get-tuple-element.6.tiles_ref, f32[16,128,256]{2,1,0:T(8,128)} %all_to_all.61.operand_ref), custom_call_target="tpu_custom_call" | custom-call | flops 402653184 | bytes 7340032 | tf_op jit(solution)/shard_map/pallas_call | solution.py:78
  132.9 1.5 slice.152
  134.4 0.1 collective-permute-start.1
  134.5 2.6 collective-permute-done.1
  137.2 0.1 slice_add_fusion.1
  137.3 34.1 %all_to_all.62 = f32[8,128,256]{2,1,0:T(8,128)S(1)} all-to-all(f32[8,128,256]{2,1,0:T(8,128)S(1)} %slice_add_fusion.1), channel_id=1, replica_groups=mesh['row'=16,'chip'=8,'core'=2] {'chip'}, dimensions={0} | all-to-all | bytes 2097152 | tf_op jit(solution)/shard_map/all_to_all | solution.py:97
  171.5 0.3 fusion.2
  171.8 0.2 broadcast_in_dim.24
  172.0 31.8 %all_to_all.63.operand_ref = f32[16,128,256]{2,1,0:T(8,128)} all-to-all(f32[16,128,256]{2,1,0:T(8,128)S(1)} %broadcast_in_dim.24), channel_id=1, replica_groups=mesh['row'=16,'chip'=8,'core'=2] {'row'}, dimensions={0} | all-to-all | bytes 4194304 | tf_op jit(solution)/shard_map/all_to_all | solution.py:93
  203.8 5.7 %shard_map.79 = f32[16,128,256]{2,1,0:T(8,128)} custom-call(s32[48]{0:T(128)} %get-tuple-element.11.picked_ref.placed_ref, s32[48]{0:T(128)} %get-tuple-element.8.placed_ref.picked_ref, s32[1]{0:T(128)} %bitcast.23.filled_ref, f32[48,128,128]{2,1,0:T(8,128)} %get-tuple-element.5.tiles_ref, f32[16,128,256]{2,1,0:T(8,128)} %all_to_all.63.operand_ref), custom_call_target="tpu_custom_call" | custom-call | flops 402653184 | bytes 7340032 | tf_op jit(solution)/shard_map/pallas_call | solution.py:78
  209.5 1.5 slice.154
  211.0 0.1 collective-permute-start.2
  211.1 2.6 collective-permute-done.2
  213.7 0.1 slice_add_fusion
  213.8 37.9 %all_to_all.64 = f32[8,128,256]{2,1,0:T(8,128)S(1)} all-to-all(f32[8,128,256]{2,1,0:T(8,128)S(1)} %slice_add_fusion), channel_id=1, replica_groups=mesh['row'=16,'chip'=8,'core'=2] {'chip'}, dimensions={0} | all-to-all | bytes 2097152 | tf_op jit(solution)/shard_map/all_to_all | solution.py:97
  251.8 0.4 fusion
  252.2 0.3 fusion.17
  252.5 0.1 copy.11
  252.7 30.4 %all_to_all.65 = f32[8,128,256]{2,1,0:T(8,128)S(1)} all-to-all(f32[8,128,256]{2,1,0:T(8,128)S(1)} %broadcast_in_dim.52), channel_id=1, replica_groups=mesh['row'=16,'chip'=8,'core'=2] {'chip'}, dimensions={0} | all-to-all | bytes 2097152 | tf_op jit(solution)/shard_map/all_to_all | solution.py:93
  283.1 2.7 collective-permute-done.3
  285.7 1.5 pad_maximum_fusion.operand_ref
  287.2 5.7 %shard_map.80 = f32[16,128,256]{2,1,0:T(8,128)} custom-call(s32[48]{0:T(128)} %get-tuple-element.8.placed_ref.picked_ref, s32[48]{0:T(128)} %get-tuple-element.11.picked_ref.placed_ref, s32[1]{0:T(128)} %bitcast.23.filled_ref, f32[48,128,128]{2,1,0:T(8,128)} %get-tuple-element.5.tiles_ref, f32[16,128,256]{2,1,0:T(8,128)} %pad_maximum_fusion.operand_ref), custom_call_target="tpu_custom_call" | custom-call | flops 402653184 | bytes 7340032 | tf_op jit(solution)/shard_map/pallas_call | solution.py:78
  293.0 37.6 %all_to_all.66 = f32[16,128,256]{2,1,0:T(8,128)S(1)} all-to-all(f32[16,128,256]{2,1,0:T(8,128)} %shard_map.80), channel_id=1, replica_groups=mesh['row'=16,'chip'=8,'core'=2] {'row'}, dimensions={0} | all-to-all | bytes 4194304 | tf_op jit(solution)/shard_map/all_to_all | solution.py:97
  330.6 0.1 reduce_sum.66
  330.7 0.4 fusion.11
  331.1 0.1 copy.12
  331.3 33.0 %all_to_all.67 = f32[8,128,256]{2,1,0:T(8,128)S(1)} all-to-all(f32[8,128,256]{2,1,0:T(8,128)S(1)} %broadcast_in_dim.53), channel_id=1, replica_groups=mesh['row'=16,'chip'=8,'core'=2] {'chip'}, dimensions={0} | all-to-all | bytes 2097152 | tf_op jit(solution)/shard_map/all_to_all | solution.py:93
  364.3 0.1 collective-permute-start.4
  364.4 2.5 collective-permute-done.4
  367.0 1.6 pad_maximum_fusion.1.operand_ref
  368.6 8.4 %shard_map.81 = f32[16,128,256]{2,1,0:T(8,128)} custom-call(s32[48]{0:T(128)} %get-tuple-element.9.placed_ref.picked_ref, s32[48]{0:T(128)} %get-tuple-element.12.picked_ref.placed_ref, s32[1]{0:T(128)} %bitcast.14.filled_ref, f32[48,128,128]{2,1,0:T(8,128)} %get-tuple-element.6.tiles_ref, f32[16,128,256]{2,1,0:T(8,128)} %pad_maximum_fusion.1.operand_ref), custom_call_target="tpu_custom_call" | custom-call | flops 402653184 | bytes 7340032 | tf_op jit(solution)/shard_map/pallas_call | solution.py:78
  377.0 32.9 %all_to_all.68 = f32[16,128,256]{2,1,0:T(8,128)S(1)} all-to-all(f32[16,128,256]{2,1,0:T(8,128)} %shard_map.81), channel_id=1, replica_groups=mesh['row'=16,'chip'=8,'core'=2] {'row'}, dimensions={0} | all-to-all | bytes 4194304 | tf_op jit(solution)/shard_map/all_to_all | solution.py:97
  409.9 0.1 reduce_sum.67
  410.0 0.4 fusion.9
  410.4 0.1 copy.13
  410.6 34.2 %all_to_all.69 = f32[8,128,256]{2,1,0:T(8,128)S(1)} all-to-all(f32[8,128,256]{2,1,0:T(8,128)S(1)} %broadcast_in_dim.54), channel_id=1, replica_groups=mesh['row'=16,'chip'=8,'core'=2] {'chip'}, dimensions={0} | all-to-all | bytes 2097152 | tf_op jit(solution)/shard_map/all_to_all | solution.py:93
  444.8 2.7 collective-permute-done.5
  447.4 1.6 pad_maximum_fusion.2.operand_ref
  449.0 5.9 %shard_map.82 = f32[16,128,256]{2,1,0:T(8,128)} custom-call(s32[48]{0:T(128)} %get-tuple-element.7.placed_ref.picked_ref, s32[48]{0:T(128)} %get-tuple-element.10.picked_ref.placed_ref, s32[1]{0:T(128)} %bitcast.5.filled_ref, f32[48,128,128]{2,1,0:T(8,128)} %get-tuple-element.4.tiles_ref, f32[16,128,256]{2,1,0:T(8,128)} %pad_maximum_fusion.2.operand_ref), custom_call_target="tpu_custom_call" | custom-call | flops 402653184 | bytes 7340032 | tf_op jit(solution)/shard_map/pallas_call | solution.py:78
  454.9 12.9 %all-to-all-start.11 = ((f32[16,128,256]{2,1,0:T(8,128)}), f32[16,128,256]{2,1,0:T(8,128)S(1)}, u32[]{:S(2)}, u32[]{:S(2)}) async-start(f32[16,128,256]{2,1,0:T(8,128)} %shard_map.82), calls=%async_computation.11 | async-start | bytes 4194304 | tf_op jit(solution)/shard_map/all_to_all | solution.py:97
  467.8 0.1 copy.10
  467.9 0.8 maximum_bitcast_fusion
  468.7 27.4 %all-to-all-done.11 = f32[16,128,256]{2,1,0:T(8,128)S(1)} async-done(((f32[16,128,256]{2,1,0:T(8,128)}), f32[16,128,256]{2,1,0:T(8,128)S(1)}, u32[]{:S(2)}, u32[]{:S(2)}) %all-to-all-start.11) | async-done | bytes 2097184 | tf_op jit(solution)/shard_map/all_to_all | solution.py:97
  496.1 0.1 reduce_sum.68
  496.3 0.4 convolution_bitcast_fusion
  496.7 1.0 copy.15
  (26 shorter events, 0.5 us)
Async XLA Ops:
  3.3 7.5 %copy-start.6 = (s32[3,1,1]{0,2,1:T(1,128)S(1)}, s32[3,1,1]{0,2,1:T(1,128)}, u32[]{:S(2)}) copy-start(s32[3,1,1]{0,2,1:T(1,128)} %param.11) | copy-start | bytes 40
  3.4 8.1 %copy-start.8 = (s32[3,1,1,48]{3,2,1,0:T(1,128)S(1)}, s32[3,1,1,48]{3,2,1,0:T(1,128)}, u32[]{:S(2)}) copy-start(s32[3,1,1,48]{3,2,1,0:T(1,128)} %param.9) | copy-start | bytes 1732
  3.4 8.7 %copy-start.7 = (s32[3,1,1,48]{3,2,1,0:T(1,128)S(1)}, s32[3,1,1,48]{3,2,1,0:T(1,128)}, u32[]{:S(2)}) copy-start(s32[3,1,1,48]{3,2,1,0:T(1,128)} %param.10) | copy-start | bytes 1732
  3.4 36.6 %all-to-all-start = ((f32[16,128,256]{2,1,0:T(8,128)}), f32[16,128,256]{2,1,0:T(8,128)S(1)}, u32[]{:S(2)}, u32[]{:S(2)}) async-start(f32[16,128,256]{2,1,0:T(8,128)} %broadcast_in_dim.22), calls=%async_computation | async-start | bytes 4194304 | tf_op jit(solution)/shard_map/all_to_all | solution.py:93
  39.9 1.3 copy-start.3
  47.1 4.2 copy-start
  48.6 2.7 collective-permute-start
  51.5 43.7 %copy-start.4 = (f32[4,1,1,128,128]{4,3,2,1,0:T(8,128)S(1)}, f32[4,1,1,128,128]{4,3,2,1,0:T(8,128)}, u32[]{:S(2)}) copy-start(f32[4,1,1,128,128]{4,3,2,1,0:T(8,128)} %param.7) | copy-start | bytes 786436
  51.5 43.7 %copy-start.5 = (f32[4,1,1,128,256]{4,3,2,1,0:T(8,128)S(1)}, f32[4,1,1,128,256]{4,3,2,1,0:T(8,128)}, u32[]{:S(2)}) copy-start(f32[4,1,1,128,256]{4,3,2,1,0:T(8,128)} %param.6) | copy-start | bytes 1572868
  132.9 4.2 copy-start.1
  134.4 2.7 collective-permute-start.1
  209.5 4.2 copy-start.2
  211.0 2.7 collective-permute-start.2
  283.1 2.7 collective-permute-start.3
  364.3 2.7 collective-permute-start.4
  444.7 2.7 collective-permute-start.5
  454.9 41.2 %all-to-all-start.11 = ((f32[16,128,256]{2,1,0:T(8,128)}), f32[16,128,256]{2,1,0:T(8,128)S(1)}, u32[]{:S(2)}, u32[]{:S(2)}) async-start(f32[16,128,256]{2,1,0:T(8,128)} %shard_map.82), calls=%async_computation.11 | async-start | bytes 4194304 | tf_op jit(solution)/shard_map/all_to_all | solution.py:97

commit v6 on v5

--- a/solution.py
+++ b/solution.py
@@ -26,7 +26,9 @@
     return high, low
 
 
-def _terms_kernel(transposed, group, picked_ref, placed_ref, filled_ref, tiles_ref, operand_ref, out_ref, split_ref):
+def _terms_kernel(transposed, pairs_per_step, tile_ref, first_ref, second_ref, source_ref, live_ref, *refs):
+    tiles = refs[:2 * pairs_per_step]
+    operand_ref, out_ref, split_ref = refs[2 * pairs_per_step:]
     step = pl.program_id(0)
 
     @pl.when(step == 0)
@@ -36,14 +38,14 @@
             high, low = _split(operand_ref[source])
             split_ref[source] = jnp.concatenate([high, low, high], axis=0)
 
-    filled = filled_ref[0]
-    for g in range(group):
-        b = step * group + g
-
-        @pl.when(b < filled)
+    for g in range(pairs_per_step):
+        p = step * pairs_per_step + g
+
+        @pl.when(live_ref[p] > 0)
         def _():
-            high, low = _split(tiles_ref[g])
-            values = split_ref[picked_ref[b]]
+            tile = jnp.concatenate([tiles[2 * g][0], tiles[2 * g + 1][0]], axis=1 if transposed else 0)
+            high, low = _split(tile)
+            values = split_ref[source_ref[p]]
             if transposed:
                 stacked = jnp.concatenate([high, high, low], axis=0)
                 product = lax.dot_general(stacked, values, (((0,), (0,)), ((), ())),
@@ -51,37 +53,73 @@
             else:
                 stacked = jnp.concatenate([high, high, low], axis=1)
                 product = jnp.dot(stacked, values, preferred_element_type=jnp.float32)
-            out_ref[placed_ref[b]] += product
+            rows = product.shape[0] // 2
+            out_ref[first_ref[p]] += product[:rows]
+
+            @pl.when(live_ref[p] > 1)
+            def _():
+                out_ref[second_ref[p]] += product[rows:]
+
+
+def pair_blocks(picked, placed, filled, n_src):
+    slot_count = picked.shape[0]
+    span = slot_count + n_src
+    span += span % 2
+    index = jnp.arange(slot_count, dtype=jnp.int32)
+    key = jnp.where(index < filled, jnp.clip(picked, 0, n_src - 1), n_src)
+    order = jnp.argsort(key, stable=True).astype(jnp.int32)
+    sorted_key = key[order]
+    counts = jnp.zeros((n_src + 1,), jnp.int32).at[key].add(1)
+    starts = jnp.cumsum(counts) - counts
+    padded = (counts[:n_src] + 1) // 2 * 2
+    padded_starts = jnp.cumsum(padded) - padded
+    rank = index - starts[sorted_key]
+    live = sorted_key < n_src
+    position = jnp.where(live, padded_starts[jnp.minimum(sorted_key, n_src - 1)] + rank, span)
+    slots = jnp.full((span + 1,), -1, jnp.int32).at[position].set(order)[:span].reshape(span // 2, 2)
+    first, second = slots[:, 0], slots[:, 1]
+    has_second = second >= 0
+    second = jnp.where(has_second, second, jnp.maximum(first, 0))
+    first = jnp.maximum(first, 0)
+    live_count = jnp.where(slots[:, 0] >= 0, 1 + has_second.astype(jnp.int32), 0)
+    return first, second, live_count
 
 
 def block_terms_kernel(tile_stack, picked, placed, filled, operand, count, transposed):
     slot_count, s, _ = tile_stack.shape
     n_src, _, width = operand.shape
-    group = math.gcd(slot_count, GROUP)
-    steps = slot_count // group
-
-    def tile_map(j, picked_ref, placed_ref, filled_ref):
-        last = jnp.maximum(filled_ref[0] - 1, 0) // group
-        return (jnp.minimum(j, last), 0, 0)
+    first, second, live = pair_blocks(picked, placed, filled, n_src)
+    pair_count = first.shape[0]
+    pairs_per_step = 4
+    steps = -(-pair_count // pairs_per_step)
+    extra = steps * pairs_per_step - pair_count
+    first = jnp.pad(first, (0, extra))
+    second = jnp.pad(second, (0, extra))
+    live = jnp.pad(live, (0, extra))
+    source = jnp.clip(picked, 0, n_src - 1)[first]
+    target_first = jnp.clip(placed, 0, count - 1)[first]
+    target_second = jnp.clip(placed, 0, count - 1)[second]
+    tile_index = jnp.stack([first, second], axis=1).reshape(-1)
+
+    def tile_map(k):
+        return lambda j, tile_ref, *_: (tile_ref[j * 2 * pairs_per_step + k], 0, 0)
 
     grid_spec = pltpu.PrefetchScalarGridSpec(
-        num_scalar_prefetch=3,
+        num_scalar_prefetch=5,
         grid=(steps,),
-        in_specs=[
-            pl.BlockSpec((group, s, s), tile_map),
-            pl.BlockSpec((n_src, s, width), lambda j, *_: (0, 0, 0)),
-        ],
+        in_specs=[pl.BlockSpec((1, s, s), tile_map(k)) for k in range(2 * pairs_per_step)]
+        + [pl.BlockSpec((n_src, s, width), lambda j, *_: (0, 0, 0))],
         out_specs=pl.BlockSpec((count, s, width), lambda j, *_: (0, 0, 0)),
         scratch_shapes=[pltpu.VMEM((n_src, 3 * s, width), jnp.bfloat16)],
     )
     flops = 2 * slot_count * s * s * width
     return pl.pallas_call(
-        functools.partial(_terms_kernel, transposed, group),
+        functools.partial(_terms_kernel, transposed, pairs_per_step),
         grid_spec=grid_spec,
         out_shape=jax.ShapeDtypeStruct((count, s, width), jnp.float32),
         compiler_params=pltpu.CompilerParams(dimension_semantics=("arbitrary",)),
         cost_estimate=pl.CostEstimate(flops=flops, bytes_accessed=4 * (slot_count * s * s + 2 * n_src * s * width), transcendentals=0),
-    )(jnp.clip(picked, 0, n_src - 1), jnp.clip(placed, 0, count - 1), jnp.reshape(filled, (1,)), tile_stack, operand)
+    )(tile_index, target_first, target_second, source, live, *([tile_stack] * (2 * pairs_per_step)), operand)
 
 
 def block_terms(tile_stack, picked, placed, filled, operand, totals, transposed):

time: 498 us -> 532 us (1.068)
  blocking collectives: 345 us -> 104 us
  waiting for transfers between devices: 62.8 us -> 208 us
  local copies, waits for them, and re-layouts: 17.6 us -> 71.6 us
  starting transfers between devices: 20.8 us -> 59.3 us
  other arithmetic: 7.69 us -> 37.1 us
    all_to_all x5 -> x0, blocking collectives: 159 us -> none  [gather_blocks(): return lax.all_to_all(stacked, axis, 0, 0, tiled=True)]
    all_to_all x1 -> x6, waiting for transfers between devices: 19.6 us -> 120 us  [gather_blocks(): return lax.all_to_all(stacked, axis, 0, 0, tiled=True)]
    all_to_all x5 -> x3, blocking collectives: 186 us -> 104 us  [scatter_sum(): return lax.all_to_all(parts, axis, 0, 0, tiled=True).sum(axis=0)]
    all_to_all x1 -> x3, waiting for transfers between devices: 27.4 us -> 80.8 us  [scatter_sum(): return lax.all_to_all(parts, axis, 0, 0, tiled=True).sum(axis=0)]
    gather x0 -> x36, local copies, waits for them, and re-layouts: none -> 35.8 us  [the longest x6 7.39 us: block_terms_kernel(): target_first = jnp.clip(placed, 0, count - 1)[first]]
    all_to_all x1 -> x6, starting transfers between devices: 7.52 us -> 35.2 us  [gather_blocks(): return lax.all_to_all(stacked, axis, 0, 0, tiled=True)]
    sort x0 -> x6, other arithmetic: none -> 12.2 us  [pair_blocks(): order = jnp.argsort(key, stable=True).astype(jnp.int32)]
    all_to_all x1 -> x3, starting transfers between devices: 12.9 us -> 23.5 us  [scatter_sum(): return lax.all_to_all(parts, axis, 0, 0, tiled=True).sum(axis=0)]
  transfers between devices with their start and end apart: 8 -> 15, of which waited for: 8 -> 12; matrix products, arithmetic and copies ran while one was open for 2% -> 16% of each run, Pallas kernels for 0% -> 0%
where the time goes in v6:
time: 532 us; the launch traced here: 529 us
  waiting for transfers between devices  208 us (39%)
  blocking collectives  104 us (20%)
  local copies, waits for them, and re-layouts  71.6 us (13%)
  starting transfers between devices  59.3 us (11%)
  Pallas kernels  42.9 us (8%)
  other arithmetic  37.1 us (7%)
    all_to_all x6, waiting for transfers between devices, gather_blocks(): return lax.all_to_all(stacked, axis, 0, 0, tiled=True)  120 us
    all_to_all x3, blocking collectives, scatter_sum(): return lax.all_to_all(parts, axis, 0, 0, tiled=True).sum(axis=0)  104 us
    all_to_all x3, waiting for transfers between devices, scatter_sum(): return lax.all_to_all(parts, axis, 0, 0, tiled=True).sum(axis=0)  80.8 us
    pallas_call x6, Pallas kernels, block_terms_kernel(): pl.pallas_call(functools.partial(_terms_kernel, transposed, pairs_per_ste...  42.9 us
    all_to_all x6, starting transfers between devices, gather_blocks(): return lax.all_to_all(stacked, axis, 0, 0, tiled=True)  35.2 us
    all_to_all x3, starting transfers between devices, scatter_sum(): return lax.all_to_all(parts, axis, 0, 0, tiled=True).sum(axis=0)  23.5 us
    sort x6, other arithmetic, pair_blocks(): order = jnp.argsort(key, stable=True).astype(jnp.int32)  12.2 us
  transfers between devices with their start and end apart: 15, of which 12 were waited for; matrix products, arithmetic and copies ran while one was open for 16% of the time, Pallas kernels for 0%

profile of v6, /device:TPU:8, one launch (start us, length us, event | category | flops | bytes accessed | tf_op | source)
XLA Modules:
  0.0 528.7 jit_solution(18296958871224572423)
XLA Ops:
  1.8 1.5 broadcast_in_dim.64
  3.4 7.5 %all-to-all-start = ((f32[16,128,256]{2,1,0:T(8,128)}), f32[16,128,256]{2,1,0:T(8,128)S(1)}, u32[]{:S(2)}, u32[]{:S(2)}) async-start(f32[16,128,256]{2,1,0:T(8,128)} %broadcast_in_dim.64), calls=%async_computation | async-start | bytes 4194304 | tf_op jit(solution)/shard_map/all_to_all | solution.py:131
  11.6 2.0 fusion.82
  13.6 2.0 compare_select_fusion.106
  16.8 2.0 sort.87
  23.7 1.2 gather_fusion.3
  26.1 1.2 gather_fusion.5
  27.3 7.7 %slice_bitcast_fusion.2 = (f32[48,128,128]{2,1,0:T(8,128)}, f32[48,128,128]{2,1,0:T(8,128)}, f32[48,128,128]{2,1,0:T(8,128)}) fusion(f32[3,1,1,48,128,128]{5,4,3,2,1,0:T(8,128)} %param.8), kind=kLoop, calls=%fused_computation.50 | loop fusion | bytes 18874368 | tf_op jit(solution)/shard_map/squeeze | solution.py:177
  35.0 4.9 all-to-all-done.refs_8_
  39.9 1.3 copy-done.3
  41.3 6.2 %shard_map.77 = f32[16,128,256]{2,1,0:T(8,128)} custom-call(s32[64]{0:T(128)} %reshape.1423.tile_ref, s32[32]{0:T(128)} %gather_fusion.3, s32[32]{0:T(128)} %gather_fusion.4, s32[32]{0:T(128)} %gather_fusion.5, s32[32]{0:T(128)} %get-tuple-element.28.live_ref, ...), custom_call_target="tpu_custom_call" | custom-call | flops 402653184 | bytes 7340032 | tf_op jit(solution)/shard_map/pallas_call | solution.py:116
  47.4 1.4 slice.317
  49.0 2.6 collective-permute-done
  52.8 10.1 %all-to-all-start.1 = ((f32[8,128,256]{2,1,0:T(8,128)}), f32[8,128,256]{2,1,0:T(8,128)S(1)}, u32[]{:S(2)}, u32[]{:S(2)}) async-start(f32[8,128,256]{2,1,0:T(8,128)} %slice_add_fusion.2), calls=%async_computation.1 | async-start | bytes 2097152 | tf_op jit(solution)/shard_map/all_to_all | solution.py:135
  64.1 2.0 sort.88
  66.1 25.9 %all-to-all-done.1 = f32[8,128,256]{2,1,0:T(8,128)S(1)} async-done(((f32[8,128,256]{2,1,0:T(8,128)}), f32[8,128,256]{2,1,0:T(8,128)S(1)}, u32[]{:S(2)}, u32[]{:S(2)}) %all-to-all-start.1) | async-done | bytes 1048608 | tf_op jit(solution)/shard_map/all_to_all | solution.py:135
  92.3 1.5 broadcast_in_dim.66
  93.9 8.4 %all-to-all-start.2 = ((f32[16,128,256]{2,1,0:T(8,128)}), f32[16,128,256]{2,1,0:T(8,128)S(1)}, u32[]{:S(2)}, u32[]{:S(2)}) async-start(f32[16,128,256]{2,1,0:T(8,128)} %broadcast_in_dim.66), calls=%async_computation.2 | async-start | bytes 4194304 | tf_op jit(solution)/shard_map/all_to_all | solution.py:131
  107.2 1.2 gather_fusion.9
  109.6 1.2 gather_fusion.11
  110.8 20.9 %all-to-all-done.2.refs_8_ = f32[16,128,256]{2,1,0:T(8,128)S(1)} async-done(((f32[16,128,256]{2,1,0:T(8,128)}), f32[16,128,256]{2,1,0:T(8,128)S(1)}, u32[]{:S(2)}, u32[]{:S(2)}) %all-to-all-start.2) | async-done | bytes 2097184 | tf_op jit(solution)/shard_map/all_to_all | solution.py:131
  131.7 1.3 copy-done.5
  133.0 8.6 %shard_map.78 = f32[16,128,256]{2,1,0:T(8,128)} custom-call(s32[64]{0:T(128)} %reshape.1429.tile_ref, s32[32]{0:T(128)} %gather_fusion.9, s32[32]{0:T(128)} %gather_fusion.10, s32[32]{0:T(128)} %gather_fusion.11, s32[32]{0:T(128)} %get-tuple-element.30.live_ref, ...), custom_call_target="tpu_custom_call" | custom-call | flops 402653184 | bytes 7340032 | tf_op jit(solution)/shard_map/pallas_call | solution.py:116
  141.6 1.4 slice.321
  143.2 2.6 collective-permute-done.1
  147.0 3.6 all-to-all-start.3
  151.4 28.4 %all-to-all-done.3 = f32[8,128,256]{2,1,0:T(8,128)S(1)} async-done(((f32[8,128,256]{2,1,0:T(8,128)}), f32[8,128,256]{2,1,0:T(8,128)S(1)}, u32[]{:S(2)}, u32[]{:S(2)}) %all-to-all-start.3) | async-done | bytes 1048608 | tf_op jit(solution)/shard_map/all_to_all | solution.py:135
  180.2 1.5 broadcast_in_dim.68
  181.7 8.6 %all-to-all-start.4 = ((f32[16,128,256]{2,1,0:T(8,128)}), f32[16,128,256]{2,1,0:T(8,128)S(1)}, u32[]{:S(2)}, u32[]{:S(2)}) async-start(f32[16,128,256]{2,1,0:T(8,128)} %broadcast_in_dim.68), calls=%async_computation.4 | async-start | bytes 4194304 | tf_op jit(solution)/shard_map/all_to_all | solution.py:131
  190.6 2.0 sort.89
  197.5 1.2 gather_fusion.15
  199.9 1.2 gather_fusion.17
  201.1 18.6 %all-to-all-done.4.refs_8_ = f32[16,128,256]{2,1,0:T(8,128)S(1)} async-done(((f32[16,128,256]{2,1,0:T(8,128)}), f32[16,128,256]{2,1,0:T(8,128)S(1)}, u32[]{:S(2)}, u32[]{:S(2)}) %all-to-all-start.4) | async-done | bytes 2097184 | tf_op jit(solution)/shard_map/all_to_all | solution.py:131
  219.7 1.3 copy-done.4
  221.0 6.4 %shard_map.79 = f32[16,128,256]{2,1,0:T(8,128)} custom-call(s32[64]{0:T(128)} %reshape.1435.tile_ref, s32[32]{0:T(128)} %gather_fusion.15, s32[32]{0:T(128)} %gather_fusion.16, s32[32]{0:T(128)} %gather_fusion.17, s32[32]{0:T(128)} %get-tuple-element.32.live_ref, ...), custom_call_target="tpu_custom_call" | custom-call | flops 402653184 | bytes 7340032 | tf_op jit(solution)/shard_map/pallas_call | solution.py:116
  227.4 1.5 slice.325
  229.3 2.4 collective-permute-done.2
  231.8 31.9 %all_to_all.60 = f32[8,128,256]{2,1,0:T(8,128)S(1)} all-to-all(f32[8,128,256]{2,1,0:T(8,128)S(1)} %slice_add_fusion), channel_id=1, replica_groups=mesh['row'=16,'chip'=8,'core'=2] {'chip'}, dimensions={0} | all-to-all | bytes 2097152 | tf_op jit(solution)/shard_map/all_to_all | solution.py:135
  263.7 1.3 fusion
  266.5 3.6 all-to-all-start.6
  270.9 2.0 sort.92
  273.8 25.4 %all-to-all-done.6 = f32[8,128,256]{2,1,0:T(8,128)S(1)} async-done(((f32[8,128,256]{2,1,0:T(8,128)}), f32[8,128,256]{2,1,0:T(8,128)S(1)}, u32[]{:S(2)}, u32[]{:S(2)}) %all-to-all-start.6) | async-done | bytes 1048608 | tf_op jit(solution)/shard_map/all_to_all | solution.py:131
  302.9 1.2 gather_fusion.35
  307.2 1.5 pad_maximum_fusion.refs_8_
  308.7 6.5 %shard_map.80 = f32[16,128,256]{2,1,0:T(8,128)} custom-call(s32[64]{0:T(128)} %reshape.1453.tile_ref, s32[32]{0:T(128)} %gather_fusion.33, s32[32]{0:T(128)} %gather_fusion.34, s32[32]{0:T(128)} %gather_fusion.35, s32[32]{0:T(128)} %get-tuple-element.26.live_ref, ...), custom_call_target="tpu_custom_call" | custom-call | flops 402653184 | bytes 7340032 | tf_op jit(solution)/shard_map/pallas_call | solution.py:116
  315.2 38.3 %all_to_all.61 = f32[16,128,256]{2,1,0:T(8,128)S(1)} all-to-all(f32[16,128,256]{2,1,0:T(8,128)} %shard_map.80), channel_id=1, replica_groups=mesh['row'=16,'chip'=8,'core'=2] {'row'}, dimensions={0} | all-to-all | bytes 4194304 | tf_op jit(solution)/shard_map/all_to_all | solution.py:135
  355.3 3.6 all-to-all-start.8
  359.7 2.0 sort.91
  362.6 24.6 %all-to-all-done.8 = f32[8,128,256]{2,1,0:T(8,128)S(1)} async-done(((f32[8,128,256]{2,1,0:T(8,128)}), f32[8,128,256]{2,1,0:T(8,128)S(1)}, u32[]{:S(2)}, u32[]{:S(2)}) %all-to-all-start.8) | async-done | bytes 1048608 | tf_op jit(solution)/shard_map/all_to_all | solution.py:131
  391.1 1.3 gather_fusion.29
  392.4 1.3 gather_fusion.27
  395.5 1.6 pad_maximum_fusion.1.refs_8_
  397.1 8.8 %shard_map.81 = f32[16,128,256]{2,1,0:T(8,128)} custom-call(s32[64]{0:T(128)} %reshape.1447.tile_ref, s32[32]{0:T(128)} %gather_fusion.27, s32[32]{0:T(128)} %gather_fusion.28, s32[32]{0:T(128)} %gather_fusion.29, s32[32]{0:T(128)} %get-tuple-element.24.live_ref, ...), custom_call_target="tpu_custom_call" | custom-call | flops 402653184 | bytes 7340032 | tf_op jit(solution)/shard_map/pallas_call | solution.py:116
  405.8 33.7 %all_to_all.62 = f32[16,128,256]{2,1,0:T(8,128)S(1)} all-to-all(f32[16,128,256]{2,1,0:T(8,128)} %shard_map.81), channel_id=1, replica_groups=mesh['row'=16,'chip'=8,'core'=2] {'row'}, dimensions={0} | all-to-all | bytes 4194304 | tf_op jit(solution)/shard_map/all_to_all | solution.py:135
  441.2 3.6 all-to-all-start.10
  445.7 2.0 sort.90
  448.5 25.3 %all-to-all-done.10 = f32[8,128,256]{2,1,0:T(8,128)S(1)} async-done(((f32[8,128,256]{2,1,0:T(8,128)}), f32[8,128,256]{2,1,0:T(8,128)S(1)}, u32[]{:S(2)}, u32[]{:S(2)}) %all-to-all-start.10) | async-done | bytes 1048608 | tf_op jit(solution)/shard_map/all_to_all | solution.py:131
  477.5 1.2 gather_fusion.23
  478.7 1.3 gather_fusion.21
  480.7 1.2 gather_fusion.22
  481.9 1.6 pad_maximum_fusion.2.refs_8_
  483.5 6.4 %shard_map.82 = f32[16,128,256]{2,1,0:T(8,128)} custom-call(s32[64]{0:T(128)} %reshape.1441.tile_ref, s32[32]{0:T(128)} %gather_fusion.21, s32[32]{0:T(128)} %gather_fusion.22, s32[32]{0:T(128)} %gather_fusion.23, s32[32]{0:T(128)} %get-tuple-element.22.live_ref, ...), custom_call_target="tpu_custom_call" | custom-call | flops 402653184 | bytes 7340032 | tf_op jit(solution)/shard_map/pallas_call | solution.py:116
  490.0 9.8 %all-to-all-start.11 = ((f32[16,128,256]{2,1,0:T(8,128)}), f32[16,128,256]{2,1,0:T(8,128)S(1)}, u32[]{:S(2)}, u32[]{:S(2)}) async-start(f32[16,128,256]{2,1,0:T(8,128)} %shard_map.82), calls=%async_computation.11 | async-start | bytes 4194304 | tf_op jit(solution)/shard_map/all_to_all | solution.py:135
  500.7 26.5 %all-to-all-done.11 = f32[16,128,256]{2,1,0:T(8,128)S(1)} async-done(((f32[16,128,256]{2,1,0:T(8,128)}), f32[16,128,256]{2,1,0:T(8,128)S(1)}, u32[]{:S(2)}, u32[]{:S(2)}) %all-to-all-start.11) | async-done | bytes 2097184 | tf_op jit(solution)/shard_map/all_to_all | solution.py:135
  (225 shorter events, 56.3 us)
Async XLA Ops:
  3.4 7.5 %copy-start.10 = (s32[3,1,1]{0,2,1:T(1,128)S(1)}, s32[3,1,1]{0,2,1:T(1,128)}, u32[]{:S(2)}) copy-start(s32[3,1,1]{0,2,1:T(1,128)} %param.11) | copy-start | bytes 40
  3.4 8.2 %copy-start.8 = (s32[3,1,1,48]{3,2,1,0:T(1,128)S(1)}, s32[3,1,1,48]{3,2,1,0:T(1,128)}, u32[]{:S(2)}) copy-start(s32[3,1,1,48]{3,2,1,0:T(1,128)} %param.9) | copy-start | bytes 1732
  3.4 8.2 %copy-start.9 = (s32[3,1,1,48]{3,2,1,0:T(1,128)S(1)}, s32[3,1,1,48]{3,2,1,0:T(1,128)}, u32[]{:S(2)}) copy-start(s32[3,1,1,48]{3,2,1,0:T(1,128)} %param.10) | copy-start | bytes 1732
  3.4 36.6 %all-to-all-start = ((f32[16,128,256]{2,1,0:T(8,128)}), f32[16,128,256]{2,1,0:T(8,128)S(1)}, u32[]{:S(2)}, u32[]{:S(2)}) async-start(f32[16,128,256]{2,1,0:T(8,128)} %broadcast_in_dim.64), calls=%async_computation | async-start | bytes 4194304 | tf_op jit(solution)/shard_map/all_to_all | solution.py:131
  39.9 1.3 copy-start.3
  47.4 4.2 copy-start
  48.9 2.7 collective-permute-start
  52.8 39.3 %copy-start.6 = (f32[4,1,1,128,128]{4,3,2,1,0:T(8,128)S(1)}, f32[4,1,1,128,128]{4,3,2,1,0:T(8,128)}, u32[]{:S(2)}) copy-start(f32[4,1,1,128,128]{4,3,2,1,0:T(8,128)} %param.7) | copy-start | bytes 786436
  52.8 39.3 %copy-start.7 = (f32[4,1,1,128,256]{4,3,2,1,0:T(8,128)S(1)}, f32[4,1,1,128,256]{4,3,2,1,0:T(8,128)}, u32[]{:S(2)}) copy-start(f32[4,1,1,128,256]{4,3,2,1,0:T(8,128)} %param.6) | copy-start | bytes 1572868
  52.8 39.2 %all-to-all-start.1 = ((f32[8,128,256]{2,1,0:T(8,128)}), f32[8,128,256]{2,1,0:T(8,128)S(1)}, u32[]{:S(2)}, u32[]{:S(2)}) async-start(f32[8,128,256]{2,1,0:T(8,128)} %slice_add_fusion.2), calls=%async_computation.1 | async-start | bytes 2097152 | tf_op jit(solution)/shard_map/all_to_all | solution.py:135
  93.9 37.8 %all-to-all-start.2 = ((f32[16,128,256]{2,1,0:T(8,128)}), f32[16,128,256]{2,1,0:T(8,128)S(1)}, u32[]{:S(2)}, u32[]{:S(2)}) async-start(f32[16,128,256]{2,1,0:T(8,128)} %broadcast_in_dim.66), calls=%async_computation.2 | async-start | bytes 4194304 | tf_op jit(solution)/shard_map/all_to_all | solution.py:131
  131.7 1.3 copy-start.5
  141.6 4.2 copy-start.1
  143.1 2.7 collective-permute-start.1
  147.0 32.9 %all-to-all-start.3 = ((f32[8,128,256]{2,1,0:T(8,128)}), f32[8,128,256]{2,1,0:T(8,128)S(1)}, u32[]{:S(2)}, u32[]{:S(2)}) async-start(f32[8,128,256]{2,1,0:T(8,128)} %slice_add_fusion.1), calls=%async_computation.3 | async-start | bytes 2097152 | tf_op jit(solution)/shard_map/all_to_all | solution.py:135
  181.7 38.0 %all-to-all-start.4 = ((f32[16,128,256]{2,1,0:T(8,128)}), f32[16,128,256]{2,1,0:T(8,128)S(1)}, u32[]{:S(2)}, u32[]{:S(2)}) async-start(f32[16,128,256]{2,1,0:T(8,128)} %broadcast_in_dim.68), calls=%async_computation.4 | async-start | bytes 4194304 | tf_op jit(solution)/shard_map/all_to_all | solution.py:131
  219.7 1.3 copy-start.4
  227.4 4.2 copy-start.2
  228.9 2.7 collective-permute-start.2
  266.5 32.8 %all-to-all-start.6 = ((f32[8,128,256]{2,1,0:T(8,128)}), f32[8,128,256]{2,1,0:T(8,128)S(1)}, u32[]{:S(2)}, u32[]{:S(2)}) async-start(f32[8,128,256]{2,1,0:T(8,128)} %broadcast_in_dim.73), calls=%async_computation.6 | async-start | bytes 2097152 | tf_op jit(solution)/shard_map/all_to_all | solution.py:131
  299.2 8.0 %collective-permute-start.3 = (f32[8,128,256]{2,1,0:T(8,128)S(1)}, f32[8,128,256]{2,1,0:T(8,128)S(1)}, u32[]{:S(2)}, u32[]{:S(2)}) collective-permute-start(f32[8,128,256]{2,1,0:T(8,128)S(1)} %all-to-all-done.6), channel_id=1, source_target_pairs={{0,1},{1,0},{2,3},{3,2},{4,5},{5,4},{6,7},{7,6},{8,9},{9,8},{10,11... | collective-permute-start | bytes 3145736 | tf_op jit(solution)/shard_map/ppermute | solution.py:148
  355.3 31.9 %all-to-all-start.8 = ((f32[8,128,256]{2,1,0:T(8,128)}), f32[8,128,256]{2,1,0:T(8,128)S(1)}, u32[]{:S(2)}, u32[]{:S(2)}) async-start(f32[8,128,256]{2,1,0:T(8,128)} %broadcast_in_dim.74), calls=%async_computation.8 | async-start | bytes 2097152 | tf_op jit(solution)/shard_map/all_to_all | solution.py:131
  387.2 8.3 %collective-permute-start.4 = (f32[8,128,256]{2,1,0:T(8,128)S(1)}, f32[8,128,256]{2,1,0:T(8,128)S(1)}, u32[]{:S(2)}, u32[]{:S(2)}) collective-permute-start(f32[8,128,256]{2,1,0:T(8,128)S(1)} %all-to-all-done.8), channel_id=1, source_target_pairs={{0,1},{1,0},{2,3},{3,2},{4,5},{5,4},{6,7},{7,6},{8,9},{9,8},{10,11... | collective-permute-start | bytes 3145736 | tf_op jit(solution)/shard_map/ppermute | solution.py:148
  441.2 32.6 %all-to-all-start.10 = ((f32[8,128,256]{2,1,0:T(8,128)}), f32[8,128,256]{2,1,0:T(8,128)S(1)}, u32[]{:S(2)}, u32[]{:S(2)}) async-start(f32[8,128,256]{2,1,0:T(8,128)} %broadcast_in_dim.75), calls=%async_computation.10 | async-start | bytes 2097152 | tf_op jit(solution)/shard_map/all_to_all | solution.py:131
  473.8 8.1 %collective-permute-start.5 = (f32[8,128,256]{2,1,0:T(8,128)S(1)}, f32[8,128,256]{2,1,0:T(8,128)S(1)}, u32[]{:S(2)}, u32[]{:S(2)}) collective-permute-start(f32[8,128,256]{2,1,0:T(8,128)S(1)} %all-to-all-done.10), channel_id=1, source_target_pairs={{0,1},{1,0},{2,3},{3,2},{4,5},{5,4},{6,7},{7,6},{8,9},{9,8},{10,11... | collective-permute-start | bytes 3145736 | tf_op jit(solution)/shard_map/ppermute | solution.py:148
  490.0 37.2 %all-to-all-start.11 = ((f32[16,128,256]{2,1,0:T(8,128)}), f32[16,128,256]{2,1,0:T(8,128)S(1)}, u32[]{:S(2)}, u32[]{:S(2)}) async-start(f32[16,128,256]{2,1,0:T(8,128)} %shard_map.82), calls=%async_computation.11 | async-start | bytes 4194304 | tf_op jit(solution)/shard_map/all_to_all | solution.py:135

commit v7 on v6

--- a/solution.py
+++ b/solution.py
@@ -61,7 +61,7 @@
                 out_ref[second_ref[p]] += product[rows:]
 
 
-def pair_blocks(picked, placed, filled, n_src):
+def pair_blocks(picked, filled, n_src):
     slot_count = picked.shape[0]
     span = slot_count + n_src
     span += span % 2
@@ -85,10 +85,10 @@
     return first, second, live_count
 
 
-def block_terms_kernel(tile_stack, picked, placed, filled, operand, count, transposed):
+def block_terms_kernel(tile_stack, picked, placed, pairing, operand, count, transposed):
     slot_count, s, _ = tile_stack.shape
     n_src, _, width = operand.shape
-    first, second, live = pair_blocks(picked, placed, filled, n_src)
+    first, second, live = pairing
     pair_count = first.shape[0]
     pairs_per_step = 4
     steps = -(-pair_count // pairs_per_step)
@@ -122,8 +122,8 @@
     )(tile_index, target_first, target_second, source, live, *([tile_stack] * (2 * pairs_per_step)), operand)
 
 
-def block_terms(tile_stack, picked, placed, filled, operand, totals, transposed):
-    return block_terms_kernel(tile_stack, picked, placed, filled, operand, totals.shape[0], transposed)
+def block_terms(tile_stack, picked, placed, pairing, operand, totals, transposed):
+    return block_terms_kernel(tile_stack, picked, placed, pairing, operand, totals.shape[0], transposed)
 
 
 def gather_blocks(block, axis, count):
@@ -168,6 +168,9 @@
     row_count = lax.axis_size("row")
     col_count = lax.axis_size("chip") * lax.axis_size("core")
     block_shape = rhs_local.shape[1:]
+    forward_pairs = jax.vmap(functools.partial(pair_blocks, n_src=row_count))(sources_local, filled_local)
+    backward_picked = column_slot(targets_local)
+    backward_pairs = jax.vmap(functools.partial(pair_blocks, n_src=col_count))(backward_picked, filled_local)
     forward = [apply_inverse(inverse_local[0], rhs_local[0])]
     for level_index in range(1, levels):
         forward_gathered = gather_blocks(forward[-1], "row", row_count)
@@ -177,7 +180,7 @@
                 tiles_local[level_index - 1],
                 sources_local[level_index - 1],
                 column_slot(targets_local[level_index - 1]),
-                filled_local[level_index - 1],
+                tuple(t[level_index - 1] for t in forward_pairs),
                 forward_gathered,
                 forward_zero_terms,
                 False,
@@ -193,9 +196,9 @@
         zero_terms = jnp.zeros((row_count,) + block_shape, jnp.float32)
         totals = block_terms(
             tiles_local[level_index],
-            column_slot(targets_local[level_index]),
+            backward_picked[level_index],
             sources_local[level_index],
-            filled_local[level_index],
+            tuple(t[level_index] for t in backward_pairs),
             gathered,
             zero_terms,
             True,

time: 532 us -> 549 us (1.032)
  blocking collectives: 104 us -> 238 us
  waiting for transfers between devices: 208 us -> 114 us
  starting transfers between devices: 59.3 us -> 35.3 us
  other arithmetic: 37.1 us -> 24.8 us
  local copies, waits for them, and re-layouts: 71.6 us -> 83.3 us
    all_to_all x3 -> x5, blocking collectives: 104 us -> 177 us  [scatter_sum(): return lax.all_to_all(parts, axis, 0, 0, tiled=True).sum(axis=0)]
    all_to_all x0 -> x2, blocking collectives: none -> 60.7 us  [gather_blocks(): return lax.all_to_all(stacked, axis, 0, 0, tiled=True)]
    all_to_all x3 -> x1, waiting for transfers between devices: 80.8 us -> 29 us  [scatter_sum(): return lax.all_to_all(parts, axis, 0, 0, tiled=True).sum(axis=0)]
    all_to_all x6 -> x4, waiting for transfers between devices: 120 us -> 77.2 us  [gather_blocks(): return lax.all_to_all(stacked, axis, 0, 0, tiled=True)]
    all_to_all x3 -> x1, starting transfers between devices: 23.5 us -> 8.96 us  [scatter_sum(): return lax.all_to_all(parts, axis, 0, 0, tiled=True).sum(axis=0)]
    sort x6 -> x2, other arithmetic: 12.2 us -> 2.02 us  [pair_blocks(): order = jnp.argsort(key, stable=True).astype(jnp.int32)]
    scatter x6 -> x4, local copies, waits for them, and re-layouts: 4.59 us -> 14.5 us  [pair_blocks(): jnp.full((span + 1,), -1, jnp.int32).at[position].set(order)[:span]]
    all_to_all x6 -> x4, starting transfers between devices: 35.2 us -> 25.8 us  [gather_blocks(): return lax.all_to_all(stacked, axis, 0, 0, tiled=True)]
  transfers between devices with their start and end apart: 15 -> 11, of which waited for: 12 -> 7; matrix products, arithmetic and copies ran while one was open for 16% -> 16% of each run, Pallas kernels for 0% -> 0%
where the time goes in v7:
time: 549 us; the launch traced here: 550 us
  blocking collectives  238 us (43%)
  waiting for transfers between devices  114 us (21%)
  local copies, waits for them, and re-layouts  83.3 us (15%)
  Pallas kernels  46.7 us (9%)
  starting transfers between devices  35.3 us (6%)
  other arithmetic  24.8 us (5%)
  matrix products  6.28 us (1%)
    all_to_all x5, blocking collectives, scatter_sum(): return lax.all_to_all(parts, axis, 0, 0, tiled=True).sum(axis=0)  177 us
    all_to_all x4, waiting for transfers between devices, gather_blocks(): return lax.all_to_all(stacked, axis, 0, 0, tiled=True)  77.2 us
    all_to_all x2, blocking collectives, gather_blocks(): return lax.all_to_all(stacked, axis, 0, 0, tiled=True)  60.7 us
    pallas_call x6, Pallas kernels, block_terms_kernel(): pl.pallas_call(functools.partial(_terms_kernel, transposed, pairs_per_ste...  46.7 us
    all_to_all x1, waiting for transfers between devices, scatter_sum(): return lax.all_to_all(parts, axis, 0, 0, tiled=True).sum(axis=0)  29 us
    all_to_all x4, starting transfers between devices, gather_blocks(): return lax.all_to_all(stacked, axis, 0, 0, tiled=True)  25.8 us
    scatter x4, local copies, waits for them, and re-layouts, pair_blocks(): jnp.full((span + 1,), -1, jnp.int32).at[position].set(order)[:span]  14.5 us
    scatter-add x3, other arithmetic, pair_blocks(): counts = jnp.zeros((n_src + 1,), jnp.int32).at[key].add(1)  14.5 us
  transfers between devices with their start and end apart: 11, of which 7 were waited for; matrix products, arithmetic and copies ran while one was open for 16% of the time, Pallas kernels for 0%

profile of v7, /device:TPU:8, one launch (start us, length us, event | category | flops | bytes accessed | tf_op | source)
XLA Modules:
  0.0 549.5 jit_solution(2155151986671381054)
XLA Ops:
  0.6 1.2 fusion.6
  1.8 1.5 broadcast_in_dim.52
  3.4 7.5 %all-to-all-start = ((f32[16,128,256]{2,1,0:T(8,128)}), f32[16,128,256]{2,1,0:T(8,128)S(1)}, u32[]{:S(2)}, u32[]{:S(2)}) async-start(f32[16,128,256]{2,1,0:T(8,128)} %broadcast_in_dim.52), calls=%async_computation | async-start | bytes 4194304 | tf_op jit(solution)/shard_map/all_to_all | solution.py:131
  13.7 7.2 %scatter_fusion.2 = s32[3,17]{1,0:T(4,128)S(1)} fusion(s32[3,17]{1,0:T(4,128)S(1)} %broadcast.667.clone.1, s32[144]{0:T(256)S(1)} %reshape.1037, s32[144]{0:T(256)S(1)} %broadcast.826), kind=kCustom, calls=%fused_computation.26 | custom fusion | flops 144 | bytes 2880 | tf_op jit(solution)/shard_map/vmap()/scatter-add | solution.py:72
  21.2 2.7 gather_fusion.21
  24.1 2.7 gather_fusion.22
  27.2 2.7 gather_fusion.23
  30.2 7.2 %scatter_fusion.3 = s32[3,65]{1,0:T(4,128)S(1)} fusion(s32[3,65]{1,0:T(4,128)S(1)} %broadcast.665.clone.1, s32[144]{0:T(256)S(1)} %reshape.1043, s32[144]{0:T(256)S(1)} %reshape.1045), kind=kCustom, calls=%fused_computation.27 | custom fusion | bytes 2880 | tf_op jit(solution)/shard_map/vmap()/scatter | solution.py:79
  37.6 7.2 %scatter_fusion = s32[3,17]{1,0:T(4,128)S(1)} fusion(s32[3,17]{1,0:T(4,128)S(1)} %broadcast.667.clone, s32[144]{0:T(256)S(1)} %reshape.1025, s32[144]{0:T(256)S(1)} %broadcast.826), kind=kCustom, calls=%fused_computation.24 | custom fusion | flops 144 | bytes 2880 | tf_op jit(solution)/shard_map/vmap()/scatter-add | solution.py:72
  45.1 2.7 gather_fusion.18
  48.0 2.7 gather_fusion.20
  51.1 2.7 gather_fusion.19
  54.0 7.2 %scatter_fusion.1 = s32[3,65]{1,0:T(4,128)S(1)} fusion(s32[3,65]{1,0:T(4,128)S(1)} %broadcast.665.clone, s32[144]{0:T(256)S(1)} %reshape.1031, s32[144]{0:T(256)S(1)} %reshape.1033), kind=kCustom, calls=%fused_computation.25 | custom fusion | bytes 2880 | tf_op jit(solution)/shard_map/vmap()/scatter | solution.py:79
  62.7 1.2 gather_fusion.1
  64.0 1.2 gather_fusion
  66.9 7.7 %slice_bitcast_fusion.2 = (f32[48,128,128]{2,1,0:T(8,128)}, f32[48,128,128]{2,1,0:T(8,128)}, f32[48,128,128]{2,1,0:T(8,128)}) fusion(f32[3,1,1,48,128,128]{5,4,3,2,1,0:T(8,128)} %param.8), kind=kLoop, calls=%fused_computation.30 | loop fusion | bytes 18874368 | tf_op jit(solution)/shard_map/squeeze | solution.py:180
  74.6 1.3 copy-done.3
  75.9 7.3 %shard_map.77 = f32[16,128,256]{2,1,0:T(8,128)} custom-call(s32[64]{0:T(128)} %reshape.838.tile_ref, s32[32]{0:T(128)} %gather_fusion, s32[32]{0:T(128)} %gather_fusion.1, s32[32]{0:T(128)} %gather_fusion.2, s32[32]{0:T(128)} %get-tuple-element.45.live_ref, f32[48,128,128]{2,1,0:T(8,128)} %get-tuple-element.24.refs_0_.refs_1_.refs_2_.refs_3_.refs_4_.refs_5_.refs_6_.refs_7_, ...), custom_call_target="tpu_custom_call" | custom-call | flops 402653184 | bytes 7340032 | tf_op jit(solution)/shard_map/pallas_call | solution.py:116
  83.2 1.4 slice.303
  84.9 2.6 collective-permute-done
  87.7 40.1 %all_to_all.60 = f32[8,128,256]{2,1,0:T(8,128)S(1)} all-to-all(f32[8,128,256]{2,1,0:T(8,128)S(1)} %slice_add_fusion.2), channel_id=1, replica_groups=mesh['row'=16,'chip'=8,'core'=2] {'chip'}, dimensions={0} | all-to-all | bytes 2097152 | tf_op jit(solution)/shard_map/all_to_all | solution.py:135
  129.1 1.5 broadcast_in_dim.53
  130.6 6.6 %all-to-all-start.2 = ((f32[16,128,256]{2,1,0:T(8,128)}), f32[16,128,256]{2,1,0:T(8,128)S(1)}, u32[]{:S(2)}, u32[]{:S(2)}) async-start(f32[16,128,256]{2,1,0:T(8,128)} %broadcast_in_dim.53), calls=%async_computation.2 | async-start | bytes 4194304 | tf_op jit(solution)/shard_map/all_to_all | solution.py:131
  137.9 1.2 gather_fusion.4
  140.3 1.2 gather_fusion.5
  141.5 23.5 %all-to-all-done.2.refs_8_ = f32[16,128,256]{2,1,0:T(8,128)S(1)} async-done(((f32[16,128,256]{2,1,0:T(8,128)}), f32[16,128,256]{2,1,0:T(8,128)S(1)}, u32[]{:S(2)}, u32[]{:S(2)}) %all-to-all-start.2) | async-done | bytes 2097184 | tf_op jit(solution)/shard_map/all_to_all | solution.py:131
  165.0 1.3 copy-done.5
  166.3 7.3 %shard_map.78 = f32[16,128,256]{2,1,0:T(8,128)} custom-call(s32[64]{0:T(128)} %reshape.839.tile_ref, s32[32]{0:T(128)} %gather_fusion.3, s32[32]{0:T(128)} %gather_fusion.4, s32[32]{0:T(128)} %gather_fusion.5, s32[32]{0:T(128)} %get-tuple-element.47.live_ref, ...), custom_call_target="tpu_custom_call" | custom-call | flops 402653184 | bytes 7340032 | tf_op jit(solution)/shard_map/pallas_call | solution.py:116
  173.6 1.4 slice.306
  175.1 2.6 collective-permute-done.1
  177.9 33.2 %all_to_all.61 = f32[8,128,256]{2,1,0:T(8,128)S(1)} all-to-all(f32[8,128,256]{2,1,0:T(8,128)S(1)} %slice_add_fusion.1), channel_id=1, replica_groups=mesh['row'=16,'chip'=8,'core'=2] {'chip'}, dimensions={0} | all-to-all | bytes 2097152 | tf_op jit(solution)/shard_map/all_to_all | solution.py:135
  212.3 1.5 broadcast_in_dim.54
  213.9 8.2 %all-to-all-start.4 = ((f32[16,128,256]{2,1,0:T(8,128)}), f32[16,128,256]{2,1,0:T(8,128)S(1)}, u32[]{:S(2)}, u32[]{:S(2)}) async-start(f32[16,128,256]{2,1,0:T(8,128)} %broadcast_in_dim.54), calls=%async_computation.4 | async-start | bytes 4194304 | tf_op jit(solution)/shard_map/all_to_all | solution.py:131
  224.0 1.2 gather_fusion.6
  225.2 1.2 gather_fusion.8
  226.4 25.6 %all-to-all-done.4.refs_8_ = f32[16,128,256]{2,1,0:T(8,128)S(1)} async-done(((f32[16,128,256]{2,1,0:T(8,128)}), f32[16,128,256]{2,1,0:T(8,128)S(1)}, u32[]{:S(2)}, u32[]{:S(2)}) %all-to-all-start.4) | async-done | bytes 2097184 | tf_op jit(solution)/shard_map/all_to_all | solution.py:131
  252.0 1.3 copy-done.4
  253.3 8.2 %shard_map.79 = f32[16,128,256]{2,1,0:T(8,128)} custom-call(s32[64]{0:T(128)} %reshape.840.tile_ref, s32[32]{0:T(128)} %gather_fusion.6, s32[32]{0:T(128)} %gather_fusion.7, s32[32]{0:T(128)} %gather_fusion.8, s32[32]{0:T(128)} %get-tuple-element.46.live_ref, ...), custom_call_target="tpu_custom_call" | custom-call | flops 402653184 | bytes 7340032 | tf_op jit(solution)/shard_map/pallas_call | solution.py:116
  261.5 1.4 slice.309
  263.1 2.6 collective-permute-done.2
  265.9 31.7 %all_to_all.62 = f32[8,128,256]{2,1,0:T(8,128)S(1)} all-to-all(f32[8,128,256]{2,1,0:T(8,128)S(1)} %slice_add_fusion), channel_id=1, replica_groups=mesh['row'=16,'chip'=8,'core'=2] {'chip'}, dimensions={0} | all-to-all | bytes 2097152 | tf_op jit(solution)/shard_map/all_to_all | solution.py:135
  297.7 1.3 fusion
  300.4 3.6 all-to-all-start.6
  305.0 28.1 %all-to-all-done.6 = f32[8,128,256]{2,1,0:T(8,128)S(1)} async-done(((f32[8,128,256]{2,1,0:T(8,128)}), f32[8,128,256]{2,1,0:T(8,128)S(1)}, u32[]{:S(2)}, u32[]{:S(2)}) %all-to-all-start.6) | async-done | bytes 1048608 | tf_op jit(solution)/shard_map/all_to_all | solution.py:131
  333.1 1.2 gather_fusion.16
  334.4 1.2 gather_fusion.15
  335.6 1.2 gather_fusion.17
  337.3 1.5 pad_maximum_fusion.refs_8_
  338.8 8.7 %shard_map.80 = f32[16,128,256]{2,1,0:T(8,128)} custom-call(s32[64]{0:T(128)} %reshape.844.tile_ref, s32[32]{0:T(128)} %gather_fusion.15, s32[32]{0:T(128)} %gather_fusion.16, s32[32]{0:T(128)} %gather_fusion.17, s32[32]{0:T(128)} %get-tuple-element.30.live_ref, ...), custom_call_target="tpu_custom_call" | custom-call | flops 402653184 | bytes 7340032 | tf_op jit(solution)/shard_map/pallas_call | solution.py:116
  347.5 36.0 %all_to_all.63 = f32[16,128,256]{2,1,0:T(8,128)S(1)} all-to-all(f32[16,128,256]{2,1,0:T(8,128)} %shard_map.80), channel_id=1, replica_groups=mesh['row'=16,'chip'=8,'core'=2] {'row'}, dimensions={0} | all-to-all | bytes 4194304 | tf_op jit(solution)/shard_map/all_to_all | solution.py:135
  384.2 30.1 %all_to_all.64 = f32[8,128,256]{2,1,0:T(8,128)S(1)} all-to-all(f32[8,128,256]{2,1,0:T(8,128)S(1)} %broadcast_in_dim.59), channel_id=1, replica_groups=mesh['row'=16,'chip'=8,'core'=2] {'chip'}, dimensions={0} | all-to-all | bytes 2097152 | tf_op jit(solution)/shard_map/all_to_all | solution.py:131
  415.1 1.3 gather_fusion.13
  416.4 1.2 gather_fusion.12
  418.8 1.5 pad_maximum_fusion.1.refs_8_
  420.3 7.7 %shard_map.81 = f32[16,128,256]{2,1,0:T(8,128)} custom-call(s32[64]{0:T(128)} %reshape.843.tile_ref, s32[32]{0:T(128)} %gather_fusion.12, s32[32]{0:T(128)} %gather_fusion.13, s32[32]{0:T(128)} %gather_fusion.14, s32[32]{0:T(128)} %get-tuple-element.31.live_ref, ...), custom_call_target="tpu_custom_call" | custom-call | flops 402653184 | bytes 7340032 | tf_op jit(solution)/shard_map/pallas_call | solution.py:116
  428.0 36.3 %all_to_all.65 = f32[16,128,256]{2,1,0:T(8,128)S(1)} all-to-all(f32[16,128,256]{2,1,0:T(8,128)} %shard_map.81), channel_id=1, replica_groups=mesh['row'=16,'chip'=8,'core'=2] {'row'}, dimensions={0} | all-to-all | bytes 4194304 | tf_op jit(solution)/shard_map/all_to_all | solution.py:135
  465.1 30.6 %all_to_all.66 = f32[8,128,256]{2,1,0:T(8,128)S(1)} all-to-all(f32[8,128,256]{2,1,0:T(8,128)S(1)} %broadcast_in_dim.60), channel_id=1, replica_groups=mesh['row'=16,'chip'=8,'core'=2] {'chip'}, dimensions={0} | all-to-all | bytes 2097152 | tf_op jit(solution)/shard_map/all_to_all | solution.py:131
  496.4 1.3 gather_fusion.10
  497.7 1.2 gather_fusion.9
  498.9 1.2 gather_fusion.11
  500.1 1.5 pad_maximum_fusion.2.refs_8_
  501.6 7.4 %shard_map.82 = f32[16,128,256]{2,1,0:T(8,128)} custom-call(s32[64]{0:T(128)} %reshape.842.tile_ref, s32[32]{0:T(128)} %gather_fusion.9, s32[32]{0:T(128)} %gather_fusion.10, s32[32]{0:T(128)} %gather_fusion.11, s32[32]{0:T(128)} %get-tuple-element.29.live_ref, ...), custom_call_target="tpu_custom_call" | custom-call | flops 402653184 | bytes 7340032 | tf_op jit(solution)/shard_map/pallas_call | solution.py:116
  509.1 9.0 %all-to-all-start.11 = ((f32[16,128,256]{2,1,0:T(8,128)}), f32[16,128,256]{2,1,0:T(8,128)S(1)}, u32[]{:S(2)}, u32[]{:S(2)}) async-start(f32[16,128,256]{2,1,0:T(8,128)} %shard_map.82), calls=%async_computation.11 | async-start | bytes 4194304 | tf_op jit(solution)/shard_map/all_to_all | solution.py:135
  519.0 29.0 %all-to-all-done.11 = f32[16,128,256]{2,1,0:T(8,128)S(1)} async-done(((f32[16,128,256]{2,1,0:T(8,128)}), f32[16,128,256]{2,1,0:T(8,128)S(1)}, u32[]{:S(2)}, u32[]{:S(2)}) %all-to-all-start.11) | async-done | bytes 2097184 | tf_op jit(solution)/shard_map/all_to_all | solution.py:135
  (159 shorter events, 25.1 us)
Async XLA Ops:
  3.4 7.5 %copy-start.7 = (s32[3,1,1,48]{3,2,1,0:T(1,128)S(1)}, s32[3,1,1,48]{3,2,1,0:T(1,128)}, u32[]{:S(2)}) copy-start(s32[3,1,1,48]{3,2,1,0:T(1,128)} %param.10) | copy-start | bytes 1732
  3.4 7.5 %copy-start.8 = (s32[3,1,1,48]{3,2,1,0:T(1,128)S(1)}, s32[3,1,1,48]{3,2,1,0:T(1,128)}, u32[]{:S(2)}) copy-start(s32[3,1,1,48]{3,2,1,0:T(1,128)} %param.9) | copy-start | bytes 1732
  3.4 7.5 %copy-start.9 = (s32[3,1,1]{0,2,1:T(1,128)S(1)}, s32[3,1,1]{0,2,1:T(1,128)}, u32[]{:S(2)}) copy-start(s32[3,1,1]{0,2,1:T(1,128)} %param.11) | copy-start | bytes 40
  3.4 71.2 %all-to-all-start = ((f32[16,128,256]{2,1,0:T(8,128)}), f32[16,128,256]{2,1,0:T(8,128)S(1)}, u32[]{:S(2)}, u32[]{:S(2)}) async-start(f32[16,128,256]{2,1,0:T(8,128)} %broadcast_in_dim.52), calls=%async_computation | async-start | bytes 4194304 | tf_op jit(solution)/shard_map/all_to_all | solution.py:131
  74.6 1.3 copy-start.3
  83.2 4.4 copy-start
  84.6 2.9 collective-permute-start
  87.7 40.2 %copy-start.6 = (f32[4,1,1,128,128]{4,3,2,1,0:T(8,128)S(1)}, f32[4,1,1,128,128]{4,3,2,1,0:T(8,128)}, u32[]{:S(2)}) copy-start(f32[4,1,1,128,128]{4,3,2,1,0:T(8,128)} %param.7) | copy-start | bytes 786436
  130.6 34.4 %all-to-all-start.2 = ((f32[16,128,256]{2,1,0:T(8,128)}), f32[16,128,256]{2,1,0:T(8,128)S(1)}, u32[]{:S(2)}, u32[]{:S(2)}) async-start(f32[16,128,256]{2,1,0:T(8,128)} %broadcast_in_dim.53), calls=%async_computation.2 | async-start | bytes 4194304 | tf_op jit(solution)/shard_map/all_to_all | solution.py:131
  165.0 1.3 copy-start.5
  173.6 4.2 copy-start.1
  175.0 2.7 collective-permute-start.1
  213.9 38.1 %all-to-all-start.4 = ((f32[16,128,256]{2,1,0:T(8,128)}), f32[16,128,256]{2,1,0:T(8,128)S(1)}, u32[]{:S(2)}, u32[]{:S(2)}) async-start(f32[16,128,256]{2,1,0:T(8,128)} %broadcast_in_dim.54), calls=%async_computation.4 | async-start | bytes 4194304 | tf_op jit(solution)/shard_map/all_to_all | solution.py:131
  252.0 1.3 copy-start.4
  261.5 4.2 copy-start.2
  263.0 2.7 collective-permute-start.2
  300.4 32.7 %all-to-all-start.6 = ((f32[8,128,256]{2,1,0:T(8,128)}), f32[8,128,256]{2,1,0:T(8,128)S(1)}, u32[]{:S(2)}, u32[]{:S(2)}) async-start(f32[8,128,256]{2,1,0:T(8,128)} %broadcast_in_dim.58), calls=%async_computation.6 | async-start | bytes 2097152 | tf_op jit(solution)/shard_map/all_to_all | solution.py:131
  333.1 4.2 collective-permute-start.3
  414.4 4.4 collective-permute-start.4
  495.7 4.5 collective-permute-start.5
  509.1 38.9 %all-to-all-start.11 = ((f32[16,128,256]{2,1,0:T(8,128)}), f32[16,128,256]{2,1,0:T(8,128)S(1)}, u32[]{:S(2)}, u32[]{:S(2)}) async-start(f32[16,128,256]{2,1,0:T(8,128)} %shard_map.82), calls=%async_computation.11 | async-start | bytes 4194304 | tf_op jit(solution)/shard_map/all_to_all | solution.py:135

commit v8 on v7

--- a/solution.py
+++ b/solution.py
@@ -61,45 +61,53 @@
                 out_ref[second_ref[p]] += product[rows:]
 
 
-def pair_blocks(picked, filled, n_src):
+def pair_blocks(picked, placed, filled, n_src, count):
     slot_count = picked.shape[0]
     span = slot_count + n_src
     span += span % 2
     index = jnp.arange(slot_count, dtype=jnp.int32)
-    key = jnp.where(index < filled, jnp.clip(picked, 0, n_src - 1), n_src)
-    order = jnp.argsort(key, stable=True).astype(jnp.int32)
-    sorted_key = key[order]
-    counts = jnp.zeros((n_src + 1,), jnp.int32).at[key].add(1)
-    starts = jnp.cumsum(counts) - counts
-    padded = (counts[:n_src] + 1) // 2 * 2
+    picked = jnp.clip(picked, 0, n_src - 1)
+    placed = jnp.clip(placed, 0, count - 1)
+    key = jnp.where(index < filled, picked, n_src)
+    same = key[:, None] == key[None, :]
+    rank = jnp.sum(same & (index[None, :] < index[:, None]), axis=1, dtype=jnp.int32)
+    groups = jnp.arange(n_src, dtype=jnp.int32)
+    member = key[:, None] == groups[None, :]
+    counts = jnp.sum(member, axis=0, dtype=jnp.int32)
+    padded = (counts + 1) // 2 * 2
     padded_starts = jnp.cumsum(padded) - padded
-    rank = index - starts[sorted_key]
-    live = sorted_key < n_src
-    position = jnp.where(live, padded_starts[jnp.minimum(sorted_key, n_src - 1)] + rank, span)
-    slots = jnp.full((span + 1,), -1, jnp.int32).at[position].set(order)[:span].reshape(span // 2, 2)
-    first, second = slots[:, 0], slots[:, 1]
-    has_second = second >= 0
-    second = jnp.where(has_second, second, jnp.maximum(first, 0))
-    first = jnp.maximum(first, 0)
-    live_count = jnp.where(slots[:, 0] >= 0, 1 + has_second.astype(jnp.int32), 0)
-    return first, second, live_count
-
-
-def block_terms_kernel(tile_stack, picked, placed, pairing, operand, count, transposed):
+    start = jnp.sum(jnp.where(member, padded_starts[None, :], 0), axis=1, dtype=jnp.int32)
+    position = jnp.where(key < n_src, start + rank, span)
+    hit = position[None, :] == jnp.arange(span, dtype=jnp.int32)[:, None]
+    used = jnp.any(hit, axis=1).reshape(span // 2, 2)
+
+    def pick(values):
+        return jnp.sum(jnp.where(hit, values[None, :], 0), axis=1, dtype=jnp.int32).reshape(span // 2, 2)
+
+    tiles = pick(index)
+    sources = pick(picked)
+    targets = pick(placed)
+    has_second = used[:, 1]
+    second_tile = jnp.where(has_second, tiles[:, 1], tiles[:, 0])
+    second_target = jnp.where(has_second, targets[:, 1], targets[:, 0])
+    live = jnp.where(used[:, 0], 1 + has_second.astype(jnp.int32), 0)
+    tile_index = jnp.stack([tiles[:, 0], second_tile], axis=1).reshape(-1)
+    return tile_index, targets[:, 0], second_target, sources[:, 0], live
+
+
+def block_terms_kernel(tile_stack, pairing, operand, count, transposed):
     slot_count, s, _ = tile_stack.shape
     n_src, _, width = operand.shape
-    first, second, live = pairing
-    pair_count = first.shape[0]
+    tile_index, target_first, target_second, source, live = pairing
+    pair_count = live.shape[0]
     pairs_per_step = 4
     steps = -(-pair_count // pairs_per_step)
     extra = steps * pairs_per_step - pair_count
-    first = jnp.pad(first, (0, extra))
-    second = jnp.pad(second, (0, extra))
+    tile_index = jnp.pad(tile_index, (0, 2 * extra))
+    target_first = jnp.pad(target_first, (0, extra))
+    target_second = jnp.pad(target_second, (0, extra))
+    source = jnp.pad(source, (0, extra))
     live = jnp.pad(live, (0, extra))
-    source = jnp.clip(picked, 0, n_src - 1)[first]
-    target_first = jnp.clip(placed, 0, count - 1)[first]
-    target_second = jnp.clip(placed, 0, count - 1)[second]
-    tile_index = jnp.stack([first, second], axis=1).reshape(-1)
 
     def tile_map(k):
         return lambda j, tile_ref, *_: (tile_ref[j * 2 * pairs_per_step + k], 0, 0)
@@ -123,7 +131,7 @@
 
 
 def block_terms(tile_stack, picked, placed, pairing, operand, totals, transposed):
-    return block_terms_kernel(tile_stack, picked, placed, pairing, operand, totals.shape[0], transposed)
+    return block_terms_kernel(tile_stack, pairing, operand, totals.shape[0], transposed)
 
 
 def gather_blocks(block, axis, count):
@@ -168,9 +176,11 @@
     row_count = lax.axis_size("row")
     col_count = lax.axis_size("chip") * lax.axis_size("core")
     block_shape = rhs_local.shape[1:]
-    forward_pairs = jax.vmap(functools.partial(pair_blocks, n_src=row_count))(sources_local, filled_local)
+    forward_pairs = jax.vmap(functools.partial(pair_blocks, n_src=row_count, count=col_count))(
+        sources_local, column_slot(targets_local), filled_local)
     backward_picked = column_slot(targets_local)
-    backward_pairs = jax.vmap(functools.partial(pair_blocks, n_src=col_count))(backward_picked, filled_local)
+    backward_pairs = jax.vmap(functools.partial(pair_blocks, n_src=col_count, count=row_count))(
+        backward_picked, sources_local, filled_local)
     forward = [apply_inverse(inverse_local[0], rhs_local[0])]
     for level_index in range(1, levels):
         forward_gathered = gather_blocks(forward[-1], "row", row_count)

time: 549 us -> 501 us (0.913)
  local copies, waits for them, and re-layouts: 83.3 us -> 33.1 us
  blocking collectives: 238 us -> 265 us
  other arithmetic: 24.8 us -> 8.37 us
  waiting for transfers between devices: 114 us -> 108 us
    gather x36 -> x0, local copies, waits for them, and re-layouts: 39.2 us -> none  [the longest x6 7.38 us: block_terms_kernel(): target_second = jnp.clip(placed, 0, count - 1)[second]]
    all_to_all x2 -> x3, blocking collectives: 60.7 us -> 96.3 us  [gather_blocks(): return lax.all_to_all(stacked, axis, 0, 0, tiled=True)]
    scatter x4 -> x0, local copies, waits for them, and re-layouts: 14.5 us -> none  [pair_blocks(): jnp.full((span + 1,), -1, jnp.int32).at[position].set(order)[:span]]
    scatter-add x3 -> x0, other arithmetic: 14.5 us -> none  [pair_blocks(): counts = jnp.zeros((n_src + 1,), jnp.int32).at[key].add(1)]
    all_to_all x5, blocking collectives: 177 us -> 168 us  [scatter_sum(): return lax.all_to_all(parts, axis, 0, 0, tiled=True).sum(axis=0)]
    all_to_all x4 -> x3, waiting for transfers between devices: 77.2 us -> 69.1 us  [gather_blocks(): return lax.all_to_all(stacked, axis, 0, 0, tiled=True)]
    all_to_all x4 -> x3, starting transfers between devices: 25.8 us -> 22.5 us  [gather_blocks(): return lax.all_to_all(stacked, axis, 0, 0, tiled=True)]
  transfers between devices with their start and end apart: 11 -> 10, of which waited for: 7 -> 9; matrix products, arithmetic and copies ran while one was open for 16% -> 4% of each run, Pallas kernels for 0% -> 0%
where the time goes in v8:
time: 501 us; the launch traced here: 500 us
  blocking collectives  265 us (53%)
  waiting for transfers between devices  108 us (22%)
  Pallas kernels  50.2 us (10%)
  local copies, waits for them, and re-layouts  33.1 us (7%)
  starting transfers between devices  30.1 us (6%)
  other arithmetic  8.37 us (2%)
    all_to_all x5, blocking collectives, scatter_sum(): return lax.all_to_all(parts, axis, 0, 0, tiled=True).sum(axis=0)  168 us
    all_to_all x3, blocking collectives, gather_blocks(): return lax.all_to_all(stacked, axis, 0, 0, tiled=True)  96.3 us
    all_to_all x3, waiting for transfers between devices, gather_blocks(): return lax.all_to_all(stacked, axis, 0, 0, tiled=True)  69.1 us
    pallas_call x6, Pallas kernels, block_terms_kernel(): pl.pallas_call(functools.partial(_terms_kernel, transposed, pairs_per_ste...  50.2 us
    all_to_all x1, waiting for transfers between devices, scatter_sum(): return lax.all_to_all(parts, axis, 0, 0, tiled=True).sum(axis=0)  26.8 us
    all_to_all x3, starting transfers between devices, gather_blocks(): return lax.all_to_all(stacked, axis, 0, 0, tiled=True)  22.5 us
  transfers between devices with their start and end apart: 10, of which 9 were waited for; matrix products, arithmetic and copies ran while one was open for 4% of the time, Pallas kernels for 0%

profile of v8, /device:TPU:8, one launch (start us, length us, event | category | flops | bytes accessed | tf_op | source)
XLA Modules:
  0.0 499.6 jit_solution(574179725093778393)
XLA Ops:
  0.6 1.2 fusion.6
  1.8 1.5 broadcast_in_dim.159
  3.4 7.5 %all-to-all-start = ((f32[16,128,256]{2,1,0:T(8,128)}), f32[16,128,256]{2,1,0:T(8,128)S(1)}, u32[]{:S(2)}, u32[]{:S(2)}) async-start(f32[16,128,256]{2,1,0:T(8,128)} %broadcast_in_dim.159), calls=%async_computation | async-start | bytes 4194304 | tf_op jit(solution)/shard_map/all_to_all | solution.py:139
  11.8 0.3 convert_reduce_fusion
  13.3 0.6 squeeze.149.tile_ref
  14.0 0.7 slice_reduce_fusion.23
  14.6 0.6 slice_reduce_fusion.20
  15.3 0.7 slice_reduce_fusion.22
  16.0 0.7 slice_reduce_fusion.21
  16.7 7.7 %slice_bitcast_fusion.2 = (f32[48,128,128]{2,1,0:T(8,128)}, f32[48,128,128]{2,1,0:T(8,128)}, f32[48,128,128]{2,1,0:T(8,128)}) fusion(f32[3,1,1,48,128,128]{5,4,3,2,1,0:T(8,128)} %param.8), kind=kLoop, calls=%fused_computation.2 | loop fusion | bytes 18874368 | tf_op jit(solution)/shard_map/squeeze | solution.py:190
  24.4 15.5 %all-to-all-done.refs_8_ = f32[16,128,256]{2,1,0:T(8,128)S(1)} async-done(((f32[16,128,256]{2,1,0:T(8,128)}), f32[16,128,256]{2,1,0:T(8,128)S(1)}, u32[]{:S(2)}, u32[]{:S(2)}) %all-to-all-start) | async-done | bytes 2097184 | tf_op jit(solution)/shard_map/all_to_all | solution.py:139
  39.9 1.3 copy-done.3
  41.3 8.6 %shard_map.77 = f32[16,128,256]{2,1,0:T(8,128)} custom-call(s32[64]{0:T(128)} %squeeze.149.tile_ref, s32[32]{0:T(128)} %get-tuple-element.33.first_ref, s32[32]{0:T(128)} %get-tuple-element.30.second_ref, s32[32]{0:T(128)} %get-tuple-element.27.source_ref, s32[32]{0:T(128)} %get-tuple-element.24.live_ref, ...), custom_call_target="tpu_custom_call" | custom-call | flops 402653184 | bytes 7340032 | tf_op jit(solution)/shard_map/pallas_call | solution.py:124
  49.9 1.4 slice.315
  51.4 2.6 collective-permute-done
  54.2 38.1 %all_to_all.60 = f32[8,128,256]{2,1,0:T(8,128)S(1)} all-to-all(f32[8,128,256]{2,1,0:T(8,128)S(1)} %slice_add_fusion.2), channel_id=1, replica_groups=mesh['row'=16,'chip'=8,'core'=2] {'chip'}, dimensions={0} | all-to-all | bytes 2097152 | tf_op jit(solution)/shard_map/all_to_all | solution.py:143
  92.4 0.3 fusion.4
  92.7 1.5 broadcast_in_dim.160
  94.2 7.5 %all-to-all-start.2 = ((f32[16,128,256]{2,1,0:T(8,128)}), f32[16,128,256]{2,1,0:T(8,128)S(1)}, u32[]{:S(2)}, u32[]{:S(2)}) async-start(f32[16,128,256]{2,1,0:T(8,128)} %broadcast_in_dim.160), calls=%async_computation.2 | async-start | bytes 4194304 | tf_op jit(solution)/shard_map/all_to_all | solution.py:139
  101.7 0.6 squeeze.157.tile_ref
  102.4 27.0 %all-to-all-done.2.refs_8_ = f32[16,128,256]{2,1,0:T(8,128)S(1)} async-done(((f32[16,128,256]{2,1,0:T(8,128)}), f32[16,128,256]{2,1,0:T(8,128)S(1)}, u32[]{:S(2)}, u32[]{:S(2)}) %all-to-all-start.2) | async-done | bytes 2097184 | tf_op jit(solution)/shard_map/all_to_all | solution.py:139
  129.4 1.3 copy-done.5
  130.7 6.8 %shard_map.78 = f32[16,128,256]{2,1,0:T(8,128)} custom-call(s32[64]{0:T(128)} %squeeze.157.tile_ref, s32[32]{0:T(128)} %get-tuple-element.34.first_ref, s32[32]{0:T(128)} %get-tuple-element.32.second_ref, s32[32]{0:T(128)} %get-tuple-element.29.source_ref, s32[32]{0:T(128)} %get-tuple-element.26.live_ref, ...), custom_call_target="tpu_custom_call" | custom-call | flops 402653184 | bytes 7340032 | tf_op jit(solution)/shard_map/pallas_call | solution.py:124
  137.5 1.4 slice.323
  139.1 2.6 collective-permute-done.1
  141.8 32.2 %all_to_all.61 = f32[8,128,256]{2,1,0:T(8,128)S(1)} all-to-all(f32[8,128,256]{2,1,0:T(8,128)S(1)} %slice_add_fusion.1), channel_id=1, replica_groups=mesh['row'=16,'chip'=8,'core'=2] {'chip'}, dimensions={0} | all-to-all | bytes 2097152 | tf_op jit(solution)/shard_map/all_to_all | solution.py:143
  174.2 0.3 fusion.2
  174.4 1.5 broadcast_in_dim.161
  176.0 7.5 %all-to-all-start.4 = ((f32[16,128,256]{2,1,0:T(8,128)}), f32[16,128,256]{2,1,0:T(8,128)S(1)}, u32[]{:S(2)}, u32[]{:S(2)}) async-start(f32[16,128,256]{2,1,0:T(8,128)} %broadcast_in_dim.161), calls=%async_computation.4 | async-start | bytes 4194304 | tf_op jit(solution)/shard_map/all_to_all | solution.py:139
  183.6 0.6 squeeze.164.tile_ref
  184.2 26.6 %all-to-all-done.4.refs_8_ = f32[16,128,256]{2,1,0:T(8,128)S(1)} async-done(((f32[16,128,256]{2,1,0:T(8,128)}), f32[16,128,256]{2,1,0:T(8,128)S(1)}, u32[]{:S(2)}, u32[]{:S(2)}) %all-to-all-start.4) | async-done | bytes 2097184 | tf_op jit(solution)/shard_map/all_to_all | solution.py:139
  210.8 1.3 copy-done.4
  212.1 9.1 %shard_map.79 = f32[16,128,256]{2,1,0:T(8,128)} custom-call(s32[64]{0:T(128)} %squeeze.164.tile_ref, s32[32]{0:T(128)} %get-tuple-element.35.first_ref, s32[32]{0:T(128)} %get-tuple-element.31.second_ref, s32[32]{0:T(128)} %get-tuple-element.28.source_ref, s32[32]{0:T(128)} %get-tuple-element.25.live_ref, ...), custom_call_target="tpu_custom_call" | custom-call | flops 402653184 | bytes 7340032 | tf_op jit(solution)/shard_map/pallas_call | solution.py:124
  221.2 1.4 slice.329
  222.7 2.6 collective-permute-done.2
  225.5 31.7 %all_to_all.62 = f32[8,128,256]{2,1,0:T(8,128)S(1)} all-to-all(f32[8,128,256]{2,1,0:T(8,128)S(1)} %slice_add_fusion), channel_id=1, replica_groups=mesh['row'=16,'chip'=8,'core'=2] {'chip'}, dimensions={0} | all-to-all | bytes 2097152 | tf_op jit(solution)/shard_map/all_to_all | solution.py:143
  257.3 1.3 fusion
  259.1 31.6 %all_to_all.63 = f32[8,128,256]{2,1,0:T(8,128)S(1)} all-to-all(f32[8,128,256]{2,1,0:T(8,128)S(1)} %broadcast_in_dim.165), channel_id=1, replica_groups=mesh['row'=16,'chip'=8,'core'=2] {'chip'}, dimensions={0} | all-to-all | bytes 2097152 | tf_op jit(solution)/shard_map/all_to_all | solution.py:139
  291.5 0.6 squeeze.181.tile_ref
  292.3 0.7 slice_reduce_fusion.11
  292.9 0.7 slice_reduce_fusion.8
  293.6 0.7 slice_reduce_fusion.10
  294.3 0.7 slice_reduce_fusion.9
  295.0 1.5 pad_maximum_fusion.refs_8_
  296.5 9.5 %shard_map.80 = f32[16,128,256]{2,1,0:T(8,128)} custom-call(s32[64]{0:T(128)} %squeeze.181.tile_ref, s32[32]{0:T(128)} %get-tuple-element.23.first_ref, s32[32]{0:T(128)} %get-tuple-element.19.second_ref, s32[32]{0:T(128)} %get-tuple-element.16.source_ref, s32[32]{0:T(128)} %get-tuple-element.13.live_ref, ...), custom_call_target="tpu_custom_call" | custom-call | flops 402653184 | bytes 7340032 | tf_op jit(solution)/shard_map/pallas_call | solution.py:124
  306.0 33.4 %all_to_all.64 = f32[16,128,256]{2,1,0:T(8,128)S(1)} all-to-all(f32[16,128,256]{2,1,0:T(8,128)} %shard_map.80), channel_id=1, replica_groups=mesh['row'=16,'chip'=8,'core'=2] {'row'}, dimensions={0} | all-to-all | bytes 4194304 | tf_op jit(solution)/shard_map/all_to_all | solution.py:143
  339.6 0.4 fusion.11
  340.2 31.2 %all_to_all.65 = f32[8,128,256]{2,1,0:T(8,128)S(1)} all-to-all(f32[8,128,256]{2,1,0:T(8,128)S(1)} %broadcast_in_dim.166), channel_id=1, replica_groups=mesh['row'=16,'chip'=8,'core'=2] {'chip'}, dimensions={0} | all-to-all | bytes 2097152 | tf_op jit(solution)/shard_map/all_to_all | solution.py:139
  371.4 0.6 squeeze.176.tile_ref
  372.0 1.9 collective-permute-done.4
  374.0 1.5 pad_maximum_fusion.1.refs_8_
  375.5 7.0 %shard_map.81 = f32[16,128,256]{2,1,0:T(8,128)} custom-call(s32[64]{0:T(128)} %squeeze.176.tile_ref, s32[32]{0:T(128)} %get-tuple-element.22.first_ref, s32[32]{0:T(128)} %get-tuple-element.20.second_ref, s32[32]{0:T(128)} %get-tuple-element.17.source_ref, s32[32]{0:T(128)} %get-tuple-element.14.live_ref, ...), custom_call_target="tpu_custom_call" | custom-call | flops 402653184 | bytes 7340032 | tf_op jit(solution)/shard_map/pallas_call | solution.py:124
  382.5 32.9 %all_to_all.66 = f32[16,128,256]{2,1,0:T(8,128)S(1)} all-to-all(f32[16,128,256]{2,1,0:T(8,128)} %shard_map.81), channel_id=1, replica_groups=mesh['row'=16,'chip'=8,'core'=2] {'row'}, dimensions={0} | all-to-all | bytes 4194304 | tf_op jit(solution)/shard_map/all_to_all | solution.py:143
  415.5 0.4 fusion.9
  416.1 33.6 %all_to_all.67 = f32[8,128,256]{2,1,0:T(8,128)S(1)} all-to-all(f32[8,128,256]{2,1,0:T(8,128)S(1)} %broadcast_in_dim.167), channel_id=1, replica_groups=mesh['row'=16,'chip'=8,'core'=2] {'chip'}, dimensions={0} | all-to-all | bytes 2097152 | tf_op jit(solution)/shard_map/all_to_all | solution.py:139
  449.9 0.6 squeeze.171.tile_ref
  450.5 1.8 collective-permute-done.5
  452.3 1.6 pad_maximum_fusion.2.refs_8_
  453.9 9.2 %shard_map.82 = f32[16,128,256]{2,1,0:T(8,128)} custom-call(s32[64]{0:T(128)} %squeeze.171.tile_ref, s32[32]{0:T(128)} %get-tuple-element.21.first_ref, s32[32]{0:T(128)} %get-tuple-element.18.second_ref, s32[32]{0:T(128)} %get-tuple-element.15.source_ref, s32[32]{0:T(128)} %get-tuple-element.12.live_ref, ...), custom_call_target="tpu_custom_call" | custom-call | flops 402653184 | bytes 7340032 | tf_op jit(solution)/shard_map/pallas_call | solution.py:124
  463.1 7.2 %all-to-all-start.11 = ((f32[16,128,256]{2,1,0:T(8,128)}), f32[16,128,256]{2,1,0:T(8,128)S(1)}, u32[]{:S(2)}, u32[]{:S(2)}) async-start(f32[16,128,256]{2,1,0:T(8,128)} %shard_map.82), calls=%async_computation.11 | async-start | bytes 4194304 | tf_op jit(solution)/shard_map/all_to_all | solution.py:143
  470.4 0.8 maximum_bitcast_fusion
  471.2 26.8 %all-to-all-done.11 = f32[16,128,256]{2,1,0:T(8,128)S(1)} async-done(((f32[16,128,256]{2,1,0:T(8,128)}), f32[16,128,256]{2,1,0:T(8,128)S(1)}, u32[]{:S(2)}, u32[]{:S(2)}) %all-to-all-start.11) | async-done | bytes 2097184 | tf_op jit(solution)/shard_map/all_to_all | solution.py:143
  498.2 0.4 convolution_bitcast_fusion
  498.6 1.0 copy.78
  (83 shorter events, 5.7 us)
Async XLA Ops:
  3.4 7.5 %copy-start.8 = (s32[3,1,1,48]{3,2,1,0:T(1,128)S(1)}, s32[3,1,1,48]{3,2,1,0:T(1,128)}, u32[]{:S(2)}) copy-start(s32[3,1,1,48]{3,2,1,0:T(1,128)} %param.9) | copy-start | bytes 1732
  3.4 7.5 %copy-start.9 = (s32[3,1,1]{0,2,1:T(1,128)S(1)}, s32[3,1,1]{0,2,1:T(1,128)}, u32[]{:S(2)}) copy-start(s32[3,1,1]{0,2,1:T(1,128)} %param.11) | copy-start | bytes 40
  3.4 7.6 %copy-start.10 = (s32[3,1,1,48]{3,2,1,0:T(1,128)S(1)}, s32[3,1,1,48]{3,2,1,0:T(1,128)}, u32[]{:S(2)}) copy-start(s32[3,1,1,48]{3,2,1,0:T(1,128)} %param.10) | copy-start | bytes 1732
  3.4 36.6 %all-to-all-start = ((f32[16,128,256]{2,1,0:T(8,128)}), f32[16,128,256]{2,1,0:T(8,128)S(1)}, u32[]{:S(2)}, u32[]{:S(2)}) async-start(f32[16,128,256]{2,1,0:T(8,128)} %broadcast_in_dim.159), calls=%async_computation | async-start | bytes 4194304 | tf_op jit(solution)/shard_map/all_to_all | solution.py:139
  39.9 1.3 copy-start.3
  49.9 4.2 copy-start
  51.3 2.7 collective-permute-start
  54.2 38.1 %copy-start.6 = (f32[4,1,1,128,128]{4,3,2,1,0:T(8,128)S(1)}, f32[4,1,1,128,128]{4,3,2,1,0:T(8,128)}, u32[]{:S(2)}) copy-start(f32[4,1,1,128,128]{4,3,2,1,0:T(8,128)} %param.7) | copy-start | bytes 786436
  54.2 38.1 %copy-start.7 = (f32[4,1,1,128,256]{4,3,2,1,0:T(8,128)S(1)}, f32[4,1,1,128,256]{4,3,2,1,0:T(8,128)}, u32[]{:S(2)}) copy-start(f32[4,1,1,128,256]{4,3,2,1,0:T(8,128)} %param.6) | copy-start | bytes 1572868
  94.2 35.2 %all-to-all-start.2 = ((f32[16,128,256]{2,1,0:T(8,128)}), f32[16,128,256]{2,1,0:T(8,128)S(1)}, u32[]{:S(2)}, u32[]{:S(2)}) async-start(f32[16,128,256]{2,1,0:T(8,128)} %broadcast_in_dim.160), calls=%async_computation.2 | async-start | bytes 4194304 | tf_op jit(solution)/shard_map/all_to_all | solution.py:139
  129.4 1.3 copy-start.5
  137.5 4.2 copy-start.1
  139.0 2.7 collective-permute-start.1
  176.0 34.8 %all-to-all-start.4 = ((f32[16,128,256]{2,1,0:T(8,128)}), f32[16,128,256]{2,1,0:T(8,128)S(1)}, u32[]{:S(2)}, u32[]{:S(2)}) async-start(f32[16,128,256]{2,1,0:T(8,128)} %broadcast_in_dim.161), calls=%async_computation.4 | async-start | bytes 4194304 | tf_op jit(solution)/shard_map/all_to_all | solution.py:139
  210.8 1.3 copy-start.4
  221.2 4.2 copy-start.2
  222.6 2.7 collective-permute-start.2
  290.7 4.3 collective-permute-start.3
  371.3 2.7 collective-permute-start.4
  449.6 2.7 collective-permute-start.5
  463.1 35.0 %all-to-all-start.11 = ((f32[16,128,256]{2,1,0:T(8,128)}), f32[16,128,256]{2,1,0:T(8,128)S(1)}, u32[]{:S(2)}, u32[]{:S(2)}) async-start(f32[16,128,256]{2,1,0:T(8,128)} %shard_map.82), calls=%async_computation.11 | async-start | bytes 4194304 | tf_op jit(solution)/shard_map/all_to_all | solution.py:143

commit v9 on v5

--- a/solution.py
+++ b/solution.py
@@ -13,11 +13,11 @@
 
 
 def apply_inverse(inverse, values):
-    return jnp.einsum("...st,...tn->...sn", inverse, values, precision=lax.Precision.HIGHEST)
+    return jnp.einsum("...st,...tn->...sn", inverse, values, precision=lax.Precision.HIGH)
 
 
 def apply_transposed(inverse, values):
-    return jnp.einsum("...ts,...tn->...sn", inverse, values, precision=lax.Precision.HIGHEST)
+    return jnp.einsum("...ts,...tn->...sn", inverse, values, precision=lax.Precision.HIGH)
 
 
 def _split(values):

time: 498 us -> 498 us (level)
  blocking collectives: 345 us -> 333 us
  Pallas kernels: 39.7 us -> 48.1 us
    all_to_all x5, blocking collectives: 186 us -> 177 us  [scatter_sum(): return lax.all_to_all(parts, axis, 0, 0, tiled=True).sum(axis=0)]
    pallas_call x6, Pallas kernels: 39.7 us -> 48.1 us  [block_terms_kernel(): pl.pallas_call(functools.partial(_terms_kernel, transposed, group), grid_...]
where the time goes in v9:
time: 498 us; the launch traced here: 494 us
  blocking collectives  333 us (67%)
  waiting for transfers between devices  64.2 us (13%)
  Pallas kernels  48.1 us (10%)
  starting transfers between devices  19.7 us (4%)
  local copies, waits for them, and re-layouts  17.6 us (4%)
  other arithmetic  7.69 us (2%)
    all_to_all x5, blocking collectives, scatter_sum(): return lax.all_to_all(parts, axis, 0, 0, tiled=True).sum(axis=0)  177 us
    all_to_all x5, blocking collectives, gather_blocks(): return lax.all_to_all(stacked, axis, 0, 0, tiled=True)  156 us
    pallas_call x6, Pallas kernels, block_terms_kernel(): pl.pallas_call(functools.partial(_terms_kernel, transposed, group), grid_...  48.1 us
    all_to_all x1, waiting for transfers between devices, scatter_sum(): return lax.all_to_all(parts, axis, 0, 0, tiled=True).sum(axis=0)  28.7 us
    all_to_all x1, waiting for transfers between devices, gather_blocks(): return lax.all_to_all(stacked, axis, 0, 0, tiled=True)  19.6 us
    all_to_all x1, starting transfers between devices, scatter_sum(): return lax.all_to_all(parts, axis, 0, 0, tiled=True).sum(axis=0)  11.9 us
  transfers between devices with their start and end apart: 8, of which 8 were waited for; matrix products, arithmetic and copies ran while one was open for 2% of the time, Pallas kernels for 0%

profile of v9, /device:TPU:8, one launch (start us, length us, event | category | flops | bytes accessed | tf_op | source)
XLA Modules:
  0.0 493.7 jit_solution(13033511661123532021)
XLA Ops:
  0.6 1.1 fusion.6
  1.8 1.5 broadcast_in_dim.22
  3.3 7.5 %all-to-all-start = ((f32[16,128,256]{2,1,0:T(8,128)}), f32[16,128,256]{2,1,0:T(8,128)S(1)}, u32[]{:S(2)}, u32[]{:S(2)}) async-start(f32[16,128,256]{2,1,0:T(8,128)} %broadcast_in_dim.22), calls=%async_computation | async-start | bytes 4194304 | tf_op jit(solution)/shard_map/all_to_all | solution.py:93
  10.8 0.6 fusion.51
  11.4 0.5 clamp_bitcast_fusion.2
  12.0 0.6 fusion.48
  12.6 7.7 %slice_bitcast_fusion.2 = (f32[48,128,128]{2,1,0:T(8,128)}, f32[48,128,128]{2,1,0:T(8,128)}, f32[48,128,128]{2,1,0:T(8,128)}) fusion(f32[3,1,1,48,128,128]{5,4,3,2,1,0:T(8,128)} %param.8), kind=kLoop, calls=%fused_computation.2 | loop fusion | bytes 18874368 | tf_op jit(solution)/shard_map/squeeze | solution.py:139
  20.3 19.6 %all-to-all-done.operand_ref = f32[16,128,256]{2,1,0:T(8,128)S(1)} async-done(((f32[16,128,256]{2,1,0:T(8,128)}), f32[16,128,256]{2,1,0:T(8,128)S(1)}, u32[]{:S(2)}, u32[]{:S(2)}) %all-to-all-start) | async-done | bytes 2097184 | tf_op jit(solution)/shard_map/all_to_all | solution.py:93
  39.9 1.3 copy-done.3
  41.2 5.9 %shard_map.77 = f32[16,128,256]{2,1,0:T(8,128)} custom-call(s32[48]{0:T(128)} %get-tuple-element.10.picked_ref.placed_ref, s32[48]{0:T(128)} %get-tuple-element.7.placed_ref.picked_ref, s32[1]{0:T(128)} %bitcast.5.filled_ref, f32[48,128,128]{2,1,0:T(8,128)} %get-tuple-element.4.tiles_ref, f32[16,128,256]{2,1,0:T(8,128)} %copy-done.3), custom_call_target="tpu_custom_call" | custom-call | flops 402653184 | bytes 7340032 | tf_op jit(solution)/shard_map/pallas_call | solution.py:78
  47.1 1.5 slice.150
  48.5 0.1 collective-permute-start
  48.6 2.6 collective-permute-done
  51.3 0.1 slice_add_fusion.2
  51.5 44.0 %all_to_all.60 = f32[8,128,256]{2,1,0:T(8,128)S(1)} all-to-all(f32[8,128,256]{2,1,0:T(8,128)S(1)} %slice_add_fusion.2), channel_id=1, replica_groups=mesh['row'=16,'chip'=8,'core'=2] {'chip'}, dimensions={0} | all-to-all | bytes 2097152 | tf_op jit(solution)/shard_map/all_to_all | solution.py:97
  95.6 0.2 fusion.4
  95.8 0.2 broadcast_in_dim.23
  96.0 29.1 %all_to_all.61.operand_ref = f32[16,128,256]{2,1,0:T(8,128)} all-to-all(f32[16,128,256]{2,1,0:T(8,128)S(1)} %broadcast_in_dim.23), channel_id=1, replica_groups=mesh['row'=16,'chip'=8,'core'=2] {'row'}, dimensions={0} | all-to-all | bytes 4194304 | tf_op jit(solution)/shard_map/all_to_all | solution.py:93
  125.1 7.8 %shard_map.78 = f32[16,128,256]{2,1,0:T(8,128)} custom-call(s32[48]{0:T(128)} %get-tuple-element.12.picked_ref.placed_ref, s32[48]{0:T(128)} %get-tuple-element.9.placed_ref.picked_ref, s32[1]{0:T(128)} %bitcast.14.filled_ref, f32[48,128,128]{2,1,0:T(8,128)} %get-tuple-element.6.tiles_ref, f32[16,128,256]{2,1,0:T(8,128)} %all_to_all.61.operand_ref), custom_call_target="tpu_custom_call" | custom-call | flops 402653184 | bytes 7340032 | tf_op jit(solution)/shard_map/pallas_call | solution.py:78
  132.9 1.5 slice.152
  134.4 0.1 collective-permute-start.1
  134.5 2.6 collective-permute-done.1
  137.1 0.1 slice_add_fusion.1
  137.3 31.7 %all_to_all.62 = f32[8,128,256]{2,1,0:T(8,128)S(1)} all-to-all(f32[8,128,256]{2,1,0:T(8,128)S(1)} %slice_add_fusion.1), channel_id=1, replica_groups=mesh['row'=16,'chip'=8,'core'=2] {'chip'}, dimensions={0} | all-to-all | bytes 2097152 | tf_op jit(solution)/shard_map/all_to_all | solution.py:97
  169.0 0.2 fusion.2
  169.3 0.2 broadcast_in_dim.24
  169.5 35.6 %all_to_all.63.operand_ref = f32[16,128,256]{2,1,0:T(8,128)} all-to-all(f32[16,128,256]{2,1,0:T(8,128)S(1)} %broadcast_in_dim.24), channel_id=1, replica_groups=mesh['row'=16,'chip'=8,'core'=2] {'row'}, dimensions={0} | all-to-all | bytes 4194304 | tf_op jit(solution)/shard_map/all_to_all | solution.py:93
  205.1 10.0 %shard_map.79 = f32[16,128,256]{2,1,0:T(8,128)} custom-call(s32[48]{0:T(128)} %get-tuple-element.11.picked_ref.placed_ref, s32[48]{0:T(128)} %get-tuple-element.8.placed_ref.picked_ref, s32[1]{0:T(128)} %bitcast.23.filled_ref, f32[48,128,128]{2,1,0:T(8,128)} %get-tuple-element.5.tiles_ref, f32[16,128,256]{2,1,0:T(8,128)} %all_to_all.63.operand_ref), custom_call_target="tpu_custom_call" | custom-call | flops 402653184 | bytes 7340032 | tf_op jit(solution)/shard_map/pallas_call | solution.py:78
  215.0 1.5 slice.154
  216.5 0.1 collective-permute-start.2
  216.6 2.6 collective-permute-done.2
  219.3 0.1 slice_add_fusion
  219.4 34.5 %all_to_all.64 = f32[8,128,256]{2,1,0:T(8,128)S(1)} all-to-all(f32[8,128,256]{2,1,0:T(8,128)S(1)} %slice_add_fusion), channel_id=1, replica_groups=mesh['row'=16,'chip'=8,'core'=2] {'chip'}, dimensions={0} | all-to-all | bytes 2097152 | tf_op jit(solution)/shard_map/all_to_all | solution.py:97
  254.0 0.3 fusion
  254.3 0.2 fusion.17
  254.5 0.1 copy.11
  254.6 0.1 broadcast_in_dim.52
  254.7 30.4 %all_to_all.65 = f32[8,128,256]{2,1,0:T(8,128)S(1)} all-to-all(f32[8,128,256]{2,1,0:T(8,128)S(1)} %broadcast_in_dim.52), channel_id=1, replica_groups=mesh['row'=16,'chip'=8,'core'=2] {'chip'}, dimensions={0} | all-to-all | bytes 2097152 | tf_op jit(solution)/shard_map/all_to_all | solution.py:93
  285.1 2.7 collective-permute-done.3
  287.7 1.5 pad_maximum_fusion.operand_ref
  289.3 10.6 %shard_map.80 = f32[16,128,256]{2,1,0:T(8,128)} custom-call(s32[48]{0:T(128)} %get-tuple-element.8.placed_ref.picked_ref, s32[48]{0:T(128)} %get-tuple-element.11.picked_ref.placed_ref, s32[1]{0:T(128)} %bitcast.23.filled_ref, f32[48,128,128]{2,1,0:T(8,128)} %get-tuple-element.5.tiles_ref, f32[16,128,256]{2,1,0:T(8,128)} %pad_maximum_fusion.operand_ref), custom_call_target="tpu_custom_call" | custom-call | flops 402653184 | bytes 7340032 | tf_op jit(solution)/shard_map/pallas_call | solution.py:78
  299.8 32.4 %all_to_all.66 = f32[16,128,256]{2,1,0:T(8,128)S(1)} all-to-all(f32[16,128,256]{2,1,0:T(8,128)} %shard_map.80), channel_id=1, replica_groups=mesh['row'=16,'chip'=8,'core'=2] {'row'}, dimensions={0} | all-to-all | bytes 4194304 | tf_op jit(solution)/shard_map/all_to_all | solution.py:97
  332.2 0.1 reduce_sum.66
  332.3 0.3 fusion.11
  332.6 0.1 copy.12
  332.8 29.5 %all_to_all.67 = f32[8,128,256]{2,1,0:T(8,128)S(1)} all-to-all(f32[8,128,256]{2,1,0:T(8,128)S(1)} %broadcast_in_dim.53), channel_id=1, replica_groups=mesh['row'=16,'chip'=8,'core'=2] {'chip'}, dimensions={0} | all-to-all | bytes 2097152 | tf_op jit(solution)/shard_map/all_to_all | solution.py:93
  362.3 2.7 collective-permute-done.4
  365.0 1.6 pad_maximum_fusion.1.operand_ref
  366.6 8.0 %shard_map.81 = f32[16,128,256]{2,1,0:T(8,128)} custom-call(s32[48]{0:T(128)} %get-tuple-element.9.placed_ref.picked_ref, s32[48]{0:T(128)} %get-tuple-element.12.picked_ref.placed_ref, s32[1]{0:T(128)} %bitcast.14.filled_ref, f32[48,128,128]{2,1,0:T(8,128)} %get-tuple-element.6.tiles_ref, f32[16,128,256]{2,1,0:T(8,128)} %pad_maximum_fusion.1.operand_ref), custom_call_target="tpu_custom_call" | custom-call | flops 402653184 | bytes 7340032 | tf_op jit(solution)/shard_map/pallas_call | solution.py:78
  374.6 34.1 %all_to_all.68 = f32[16,128,256]{2,1,0:T(8,128)S(1)} all-to-all(f32[16,128,256]{2,1,0:T(8,128)} %shard_map.81), channel_id=1, replica_groups=mesh['row'=16,'chip'=8,'core'=2] {'row'}, dimensions={0} | all-to-all | bytes 4194304 | tf_op jit(solution)/shard_map/all_to_all | solution.py:97
  408.7 0.1 reduce_sum.67
  408.8 0.3 fusion.9
  409.1 0.1 copy.13
  409.3 31.3 %all_to_all.69 = f32[8,128,256]{2,1,0:T(8,128)S(1)} all-to-all(f32[8,128,256]{2,1,0:T(8,128)S(1)} %broadcast_in_dim.54), channel_id=1, replica_groups=mesh['row'=16,'chip'=8,'core'=2] {'chip'}, dimensions={0} | all-to-all | bytes 2097152 | tf_op jit(solution)/shard_map/all_to_all | solution.py:93
  440.6 2.7 collective-permute-done.5
  443.2 1.6 pad_maximum_fusion.2.operand_ref
  444.8 5.9 %shard_map.82 = f32[16,128,256]{2,1,0:T(8,128)} custom-call(s32[48]{0:T(128)} %get-tuple-element.7.placed_ref.picked_ref, s32[48]{0:T(128)} %get-tuple-element.10.picked_ref.placed_ref, s32[1]{0:T(128)} %bitcast.5.filled_ref, f32[48,128,128]{2,1,0:T(8,128)} %get-tuple-element.4.tiles_ref, f32[16,128,256]{2,1,0:T(8,128)} %pad_maximum_fusion.2.operand_ref), custom_call_target="tpu_custom_call" | custom-call | flops 402653184 | bytes 7340032 | tf_op jit(solution)/shard_map/pallas_call | solution.py:78
  450.7 11.9 %all-to-all-start.11 = ((f32[16,128,256]{2,1,0:T(8,128)}), f32[16,128,256]{2,1,0:T(8,128)S(1)}, u32[]{:S(2)}, u32[]{:S(2)}) async-start(f32[16,128,256]{2,1,0:T(8,128)} %shard_map.82), calls=%async_computation.11 | async-start | bytes 4194304 | tf_op jit(solution)/shard_map/all_to_all | solution.py:97
  462.6 0.1 copy.10
  462.7 0.8 maximum_bitcast_fusion
  463.5 28.7 %all-to-all-done.11 = f32[16,128,256]{2,1,0:T(8,128)S(1)} async-done(((f32[16,128,256]{2,1,0:T(8,128)}), f32[16,128,256]{2,1,0:T(8,128)S(1)}, u32[]{:S(2)}, u32[]{:S(2)}) %all-to-all-start.11) | async-done | bytes 2097184 | tf_op jit(solution)/shard_map/all_to_all | solution.py:97
  492.2 0.1 reduce_sum.68
  492.3 0.3 convolution_bitcast_fusion
  492.7 1.0 copy.15
  (26 shorter events, 0.4 us)
Async XLA Ops:
  3.3 7.5 %copy-start.6 = (s32[3,1,1]{0,2,1:T(1,128)S(1)}, s32[3,1,1]{0,2,1:T(1,128)}, u32[]{:S(2)}) copy-start(s32[3,1,1]{0,2,1:T(1,128)} %param.11) | copy-start | bytes 40
  3.3 8.2 %copy-start.8 = (s32[3,1,1,48]{3,2,1,0:T(1,128)S(1)}, s32[3,1,1,48]{3,2,1,0:T(1,128)}, u32[]{:S(2)}) copy-start(s32[3,1,1,48]{3,2,1,0:T(1,128)} %param.9) | copy-start | bytes 1732
  3.3 8.7 %copy-start.7 = (s32[3,1,1,48]{3,2,1,0:T(1,128)S(1)}, s32[3,1,1,48]{3,2,1,0:T(1,128)}, u32[]{:S(2)}) copy-start(s32[3,1,1,48]{3,2,1,0:T(1,128)} %param.10) | copy-start | bytes 1732
  3.3 36.6 %all-to-all-start = ((f32[16,128,256]{2,1,0:T(8,128)}), f32[16,128,256]{2,1,0:T(8,128)S(1)}, u32[]{:S(2)}, u32[]{:S(2)}) async-start(f32[16,128,256]{2,1,0:T(8,128)} %broadcast_in_dim.22), calls=%async_computation | async-start | bytes 4194304 | tf_op jit(solution)/shard_map/all_to_all | solution.py:93
  39.9 1.3 copy-start.3
  47.1 4.2 copy-start
  48.5 2.7 collective-permute-start
  51.4 44.1 %copy-start.4 = (f32[4,1,1,128,128]{4,3,2,1,0:T(8,128)S(1)}, f32[4,1,1,128,128]{4,3,2,1,0:T(8,128)}, u32[]{:S(2)}) copy-start(f32[4,1,1,128,128]{4,3,2,1,0:T(8,128)} %param.7) | copy-start | bytes 786436
  51.4 44.1 %copy-start.5 = (f32[4,1,1,128,256]{4,3,2,1,0:T(8,128)S(1)}, f32[4,1,1,128,256]{4,3,2,1,0:T(8,128)}, u32[]{:S(2)}) copy-start(f32[4,1,1,128,256]{4,3,2,1,0:T(8,128)} %param.6) | copy-start | bytes 1572868
  132.9 4.2 copy-start.1
  134.4 2.7 collective-permute-start.1
  215.0 4.2 copy-start.2
  216.5 2.7 collective-permute-start.2
  285.1 2.7 collective-permute-start.3
  362.3 2.7 collective-permute-start.4
  440.6 2.7 collective-permute-start.5
  450.7 41.5 %all-to-all-start.11 = ((f32[16,128,256]{2,1,0:T(8,128)}), f32[16,128,256]{2,1,0:T(8,128)S(1)}, u32[]{:S(2)}, u32[]{:S(2)}) async-start(f32[16,128,256]{2,1,0:T(8,128)} %shard_map.82), calls=%async_computation.11 | async-start | bytes 4194304 | tf_op jit(solution)/shard_map/all_to_all | solution.py:97
